TPU v7x, 256 devices: a whole 4x4x8 slice. The times are simulated.
256 devices in a mesh: chan: 64 (over y, z, core), ctr: 4 (over x).
Axes of the slice: x: 4, y: 4, z: 8, core: 2. Of those that a mesh axis runs over, the one named last changes fastest.
Arguments:
- amplitudes: float32 [4608, 64, 256], P('ctr', 'chan'), may hold values from -6 to 6
- pair_interaction: bfloat16 [64, 4608, 4608], P('chan', None, 'ctr'), may hold values from -0.09375 to 0.09375
- ph_interaction: float32 [128, 128, 128], P('chan'), may hold values from -0.5 to 0.5
- pp_size: int32 [64], P('chan'), may hold values from 1 to 72, as said below
- ph_owner: int32 [72, 64, 2], P('ctr', 'chan'), may hold values from 0 to 127, as said below
Outputs:
- residual: float32 [4608, 64, 256], P('ctr', 'chan')
Inputs may be any that keep to these rules, and one draw needn't show every extreme that they name: Channel c has its first 64 * pp_size[c] particle pairs live; every draw has a channel with 72 live tiles. `ph_owner`: the ph channel g is owned by index g // 2 of chan. Of the 36 tiles that one device holds, at most 2 have ph channels owned by one index of chan; in every draw some index of chan receives exactly 2 tiles from every device.
All inputs are finite; a program needn't handle non-finite values.
Results may differ from a plain program's by a relative error of at most 0.002.
Values may be sent and summed in bfloat16 or wider, within the bound.
No kernel may reach another device: no remote copies, remote signals or barrier semaphores. Data moves between devices by JAX's collectives and lax.ppermute only.
A program may use at most 128 MiB of HBM per device.

v0:
```python
import jax
import jax.numpy as jnp
from jax import lax
from jax.sharding import PartitionSpec as P


def local(amplitudes, pair_interaction, ph_interaction, pp_size, ph_owner):
    row_count, chan_count, hole_width = amplitudes.shape
    row_tiles, _, col_tiles = ph_owner.shape
    tile_rows = row_count // row_tiles
    tile_cols = hole_width // col_tiles
    offset = lax.axis_index("ctr") * row_count
    positions = offset + jnp.arange(row_count, dtype=jnp.int32)
    live_mask = positions[:, None] < (pp_size * tile_rows)[None, :]
    masked = jnp.where(live_mask[:, :, None], amplitudes, jnp.zeros_like(amplitudes))
    lowered = masked.astype(jnp.bfloat16)
    ladder = lax.psum_scatter(
        jnp.einsum("crk,kch->rch", pair_interaction, lowered, preferred_element_type=jnp.float32),
        "ctr",
        scatter_dimension=0,
        tiled=True,
    )
    tile_count = row_tiles * chan_count * col_tiles
    tile_data = masked.reshape(row_tiles, tile_rows, chan_count, col_tiles, tile_cols)
    tile_data = jnp.transpose(tile_data, (0, 2, 3, 1, 4)).reshape(tile_count, tile_rows, tile_cols)
    owners = ph_owner.reshape(tile_count)
    chan_size = lax.axis_size("chan")
    capacity = max(2, 2 * tile_count // chan_size)
    per_owner = ph_interaction.shape[0]
    target = owners // per_owner
    onehot = (target[:, None] == jnp.arange(chan_size, dtype=jnp.int32)[None, :]).astype(jnp.int32)
    slot_rank = jnp.sum((jnp.cumsum(onehot, axis=0) - onehot) * onehot, axis=1)
    slot = target * capacity + slot_rank
    outgoing = (
        jnp.zeros((chan_size * capacity, tile_rows, tile_cols), jnp.float32).at[slot].set(tile_data)
    )
    outgoing = outgoing.reshape(chan_size, capacity, tile_rows, tile_cols)
    channel_ids = (
        jnp.zeros((chan_size * capacity,), jnp.int32)
        .at[slot]
        .set(owners)
        .reshape(chan_size, capacity)
    )
    block = lax.all_to_all(outgoing, "chan", split_axis=0, concat_axis=0, tiled=True)
    labels = lax.all_to_all(channel_ids, "chan", split_axis=0, concat_axis=0, tiled=True)
    local_ids = labels % per_owner
    result = jnp.zeros_like(block)
    for which in range(per_owner):
        product = jnp.einsum(
            "abst,tu->absu", block, ph_interaction[which], precision=lax.Precision.HIGHEST
        )
        result = jnp.where((local_ids == which)[:, :, None, None], product, result)
    returned = lax.all_to_all(result, "chan", split_axis=0, concat_axis=0, tiled=True)
    returned = returned.reshape(chan_size * capacity, tile_rows, tile_cols)
    cycle_tiles = returned[slot]
    cycle = cycle_tiles.reshape(row_tiles, chan_count, col_tiles, tile_rows, tile_cols)
    cycle = jnp.transpose(cycle, (0, 3, 1, 2, 4)).reshape(row_count, chan_count, hole_width)
    return jnp.where(live_mask[:, :, None], ladder, jnp.zeros_like(ladder)) + cycle


def solution(mesh):
    in_specs = (
        P("ctr", "chan", None),
        P("chan", None, "ctr"),
        P("chan", None, None),
        P("chan"),
        P("ctr", "chan", None),
    )
    out_specs = P("ctr", "chan", None)
    return jax.shard_map(local, mesh=mesh, in_specs=in_specs, out_specs=out_specs, check_vma=False)
```

profile of v0, /device:TPU:1, one launch (start us, length us, event | category | flops | bytes accessed | tf_op | source)
XLA Modules:
  0.0 274.9 jit_solution(18108409532837801456)
XLA Ops:
  6.5 0.8 copy.25
  7.3 0.1 reshape.196
  7.4 0.1 reshape.176
  7.5 0.1 fusion.12
  7.6 0.1 reduce_window_sum.11
  7.6 0.2 select_reduce_fusion
  7.8 0.7 scatter_custom_fusion
  8.5 0.8 all_to_all.14
  9.3 13.3 %all-to-all-start = ((s32[64,1,2]{2,1,0:T(1,128)}), s32[64,1,2]{2,1,0:T(1,128)}, u32[]{:S(2)}, u32[]{:S(2)}) async-start(s32[64,1,2]{2,1,0:T(1,128)} %bitcast.7), calls=%async_computation.1 | async-start | bytes 65536 | tf_op jit(solution)/shard_map/all_to_all | solution.py:45
  23.3 2.6 copy.24
  25.9 0.1 broadcast_select_fusion
  26.0 2.0 copy.30
  28.0 0.1 copy.31
  28.1 2.5 broadcast_in_dim.47
  30.7 6.7 %scatter_fusion = f32[128,64,128]{2,1,0:T(8,128)} fusion(f32[128,64,128]{2,1,0:T(8,128)} %broadcast_in_dim.47, s32[36]{0:T(128)S(1)} %fusion.14, f32[36,64,128]{2,1,0:T(8,128)S(1)} %bitcast.57), kind=kCustom, calls=%fused_computation.2 | custom fusion | bytes 3539088 | tf_op jit(solution)/shard_map/scatter | solution.py:35
  37.3 10.5 %all-to-all-start.1 = ((f32[64,2,64,128]{3,2,1,0:T(8,128)}), f32[64,2,64,128]{3,2,1,0:T(8,128)}, u32[]{:S(2)}, u32[]{:S(2)}) async-start(f32[64,2,64,128]{3,2,1,0:T(8,128)} %bitcast.53), calls=%async_computation.2 | async-start | bytes 8388608 | tf_op jit(solution)/shard_map/all_to_all | solution.py:44
  47.8 0.0 reduce-scatter.2.cloned.1.call-start
  47.9 12.4 %fusion.2 = f32[4608,1,256]{0,2,1:T(8,128)} fusion(bf16[1,4608,1152]{2,1,0:T(8,128)(2,1)} %param.6, f32[1152,1,256]{0,2,1:T(8,128)S(1)} %broadcast_select_fusion), kind=kOutput, calls=%fused_computation.5 | convolution fusion | flops 2718203904 | bytes 16515072 | tf_op jit(solution)/shard_map/crk,kch->rch/dot_general | solution.py:18
  60.3 0.9 copy.28
  61.2 0.1 copy.32
  61.3 0.1 copy.29
  61.4 82.3 %all-to-all-done.1 = f32[64,2,64,128]{3,2,1,0:T(8,128)} async-done(((f32[64,2,64,128]{3,2,1,0:T(8,128)}), f32[64,2,64,128]{3,2,1,0:T(8,128)}, u32[]{:S(2)}, u32[]{:S(2)}) %all-to-all-start.1) | async-done | bytes 4194336 | tf_op jit(solution)/shard_map/all_to_all | solution.py:44
  143.7 6.4 %fusion.8 = f32[64,2,64,128]{3,2,1,0:T(8,128)S(1)} fusion(f32[64,2,64,128]{3,2,1,0:T(8,128)} %all-to-all-done.1, f32[2,128,128]{2,1,0:T(8,128)S(1)} %copy-done), kind=kOutput, calls=%fused_computation.12 | convolution fusion | flops 1610612736 | bytes 8454144 | tf_op jit(solution)/shard_map/abst,tu->absu/dot_general | solution.py:49
  150.2 6.7 %select_select_fusion = f32[64,2,64,128]{3,2,1,0:T(8,128)} fusion(f32[64,2,64,128]{3,2,1,0:T(8,128)S(1)} %fusion.8, f32[64,2,64,128]{3,2,1,0:T(8,128)} %all-to-all-done.1, pred[64,2]{1,0:T(8,128)(4,1)S(1)} %copy.32, pred[64,2]{1,0:T(8,128)(4,1)S(1)} %copy.29, f32[2,128,128]{2,1,0:T(8,128)S(1)} %copy-done), kind=kOutput, calls=%fused_computation.6 | convolution fusion | flops 1612709888 | bytes 12664832 | tf_op jit(solution)/shard_map/abst,tu->absu/dot_general | solution.py:49
  156.9 5.9 %all-to-all-start.2 = ((f32[64,2,64,128]{3,2,1,0:T(8,128)}), f32[64,2,64,128]{3,2,1,0:T(8,128)}, u32[]{:S(2)}, u32[]{:S(2)}) async-start(f32[64,2,64,128]{3,2,1,0:T(8,128)} %select_select_fusion), calls=%async_computation.3 | async-start | bytes 8388608 | tf_op jit(solution)/shard_map/all_to_all | solution.py:53
  162.9 95.9 %all-to-all-done.2 = f32[64,2,64,128]{3,2,1,0:T(8,128)} async-done(((f32[64,2,64,128]{3,2,1,0:T(8,128)}), f32[64,2,64,128]{3,2,1,0:T(8,128)}, u32[]{:S(2)}, u32[]{:S(2)}) %all-to-all-start.2) | async-done | bytes 4194336 | tf_op jit(solution)/shard_map/all_to_all | solution.py:53
  258.7 2.8 %gather_fusion = f32[36,64,128]{2,1,0:T(8,128)S(1)} fusion(f32[128,64,128]{2,1,0:T(8,128)} %bitcast.19, s32[1024]{0:T(1024)S(1)} %pad_clamp_fusion), kind=kCustom, calls=%fused_computation | custom fusion | bytes 2359440 | tf_op jit(solution)/shard_map/gather | solution.py:55
  261.5 0.9 copy.33
  262.5 1.9 copy.34
  264.4 0.0 reduce-scatter.2.cloned.1.call-done
  264.5 1.5 select_add_fusion
  265.9 2.1 copy.35
  (10 shorter events, 0.1 us)
Async XLA Ops:
  9.3 28.0 %all-to-all-start = ((s32[64,1,2]{2,1,0:T(1,128)}), s32[64,1,2]{2,1,0:T(1,128)}, u32[]{:S(2)}, u32[]{:S(2)}) async-start(s32[64,1,2]{2,1,0:T(1,128)} %bitcast.7), calls=%async_computation.1 | async-start | bytes 65536 | tf_op jit(solution)/shard_map/all_to_all | solution.py:45
  37.3 106.4 %all-to-all-start.1 = ((f32[64,2,64,128]{3,2,1,0:T(8,128)}), f32[64,2,64,128]{3,2,1,0:T(8,128)}, u32[]{:S(2)}, u32[]{:S(2)}) async-start(f32[64,2,64,128]{3,2,1,0:T(8,128)} %bitcast.53), calls=%async_computation.2 | async-start | bytes 8388608 | tf_op jit(solution)/shard_map/all_to_all | solution.py:44
  47.8 216.6 %reduce-scatter.2.cloned.1.call-start = ((), (), s32[]{:S(2)}) async-start(), calls=%async_computation.4 | async-start | bytes 5898240 | tf_op jit(solution)/shard_map/reduce_scatter | solution.py:17
  60.2 83.5 %copy-start = (f32[2,128,128]{2,1,0:T(8,128)S(1)}, f32[2,128,128]{2,1,0:T(8,128)}, u32[]{:S(2)}) copy-start(f32[2,128,128]{2,1,0:T(8,128)} %param.7) | copy-start | bytes 393220
  156.9 101.8 %all-to-all-start.2 = ((f32[64,2,64,128]{3,2,1,0:T(8,128)}), f32[64,2,64,128]{3,2,1,0:T(8,128)}, u32[]{:S(2)}, u32[]{:S(2)}) async-start(f32[64,2,64,128]{3,2,1,0:T(8,128)} %select_select_fusion), calls=%async_computation.3 | async-start | bytes 8388608 | tf_op jit(solution)/shard_map/all_to_all | solution.py:53
Sparse Core Ops, SparseCore 0:
  60.4 54.6 reduce-scatter.1
where the time goes:
time: 276 us; the launch traced here: 275 us
  waiting for transfers between devices  178 us (64%)
  starting transfers between devices  29.8 us (11%)
  matrix products  25.5 us (9%)
  local copies, waits for them, and re-layouts  25.1 us (9%)
  between operations  14.2 us (5%)
    all_to_all x1, waiting for transfers between devices, local(): lax.all_to_all(result, 'chan', split_axis=0, concat_axis=0, tiled=True)  95.9 us
    all_to_all x1, waiting for transfers between devices, local(): lax.all_to_all(outgoing, 'chan', split_axis=0, concat_axis=0, tiled=True)  82.3 us
    all_to_all x1, starting transfers between devices, local(): lax.all_to_all(channel_ids, 'chan', split_axis=0, concat_axis=0, tiled=True)  13.3 us
    dot_general x2, matrix products, local(): jnp.einsum('abst,tu->absu', block, ph_interaction[which], precision=lax.P...  13.2 us
    dot_general x1, matrix products, local(): jnp.einsum('crk,kch->rch', pair_interaction, lowered, preferred_element_t...  12.4 us
    all_to_all x1, starting transfers between devices, local(): lax.all_to_all(outgoing, 'chan', split_axis=0, concat_axis=0, tiled=True)  10.5 us
    scatter x1, local copies, waits for them, and re-layouts, local(): jnp.zeros((chan_size * capacity, tile_rows, tile_cols), jnp.float32)  6.65 us
    all_to_all x1, starting transfers between devices, local(): lax.all_to_all(result, 'chan', split_axis=0, concat_axis=0, tiled=True)  5.94 us
  transfers between devices with their start and end apart: 4, of which 2 were waited for; matrix products, arithmetic and copies ran while one was open for 17% of the time, Pallas kernels for 0%

commit v1 on v0

v1 whole, which is shorter than its diff:
```python
import jax
import jax.numpy as jnp
from jax import lax
from jax.sharding import PartitionSpec as P


def local(amplitudes, pair_interaction, ph_interaction, pp_size, ph_owner):
    row_count, chan_count, hole_width = amplitudes.shape
    row_tiles, _, col_tiles = ph_owner.shape
    tile_rows = row_count // row_tiles
    tile_cols = hole_width // col_tiles
    ph_all = lax.all_gather(ph_interaction, "chan", axis=0, tiled=True)
    offset = lax.axis_index("ctr") * row_count
    positions = offset + jnp.arange(row_count, dtype=jnp.int32)
    live_mask = positions[:, None] < (pp_size * tile_rows)[None, :]
    masked = jnp.where(live_mask[:, :, None], amplitudes, jnp.zeros_like(amplitudes))
    lowered = masked.astype(jnp.bfloat16)
    ladder = lax.psum_scatter(
        jnp.einsum("crk,kch->rch", pair_interaction, lowered, preferred_element_type=jnp.float32),
        "ctr",
        scatter_dimension=0,
        tiled=True,
    )
    blocks = masked.reshape(row_tiles, tile_rows, chan_count, col_tiles, tile_cols)
    chosen = ph_all[ph_owner]
    cycle = jnp.einsum(
        "rschk,rchkl->rschl", blocks, chosen, precision=lax.Precision.HIGHEST
    ).reshape(row_count, chan_count, hole_width)
    return jnp.where(live_mask[:, :, None], ladder, jnp.zeros_like(ladder)) + cycle


def solution(mesh):
    in_specs = (
        P("ctr", "chan", None),
        P("chan", None, "ctr"),
        P("chan", None, None),
        P("chan"),
        P("ctr", "chan", None),
    )
    out_specs = P("ctr", "chan", None)
    return jax.shard_map(local, mesh=mesh, in_specs=in_specs, out_specs=out_specs, check_vma=False)
```

time: 276 us -> 119 us (0.43)
  waiting for transfers between devices: 178 us -> 73.6 us
  starting transfers between devices: 29.8 us -> 0.05 us
  local copies, waits for them, and re-layouts: 25.1 us -> 13.1 us
  matrix products: 25.5 us -> 14.6 us
    all_to_all x3 -> x0, waiting for transfers between devices: 178 us -> none  [the longest x1 95.9 us: local(): lax.all_to_all(result, 'chan', split_axis=0, concat_axis=0, tiled=True)]
    all_gather x0 -> x1, waiting for transfers between devices: none -> 72.8 us  [local(): ph_all = lax.all_gather(ph_interaction, 'chan', axis=0, tiled=True)]
    all_to_all x3 -> x0, starting transfers between devices: 29.8 us -> none  [the longest x1 13.3 us: local(): lax.all_to_all(channel_ids, 'chan', split_axis=0, concat_axis=0, tiled=True)]
    dot_general x2 -> x1, matrix products: 13.2 us -> 2.18 us  [local(): jnp.einsum('rschk,rchkl->rschl', blocks, chosen, precision=lax.Precision....]
    scatter x2 -> x0, local copies, waits for them, and re-layouts: 7.34 us -> none  [the longest x1 6.65 us: local(): jnp.zeros((chan_size * capacity, tile_rows, tile_cols), jnp.float32)]
  transfers between devices with their start and end apart: 4 -> 2, of which waited for: 2 -> 1; matrix products, arithmetic and copies ran while one was open for 17% -> 21% of each run, Pallas kernels for 0% -> 0%
where the time goes in v1:
time: 119 us; the launch traced here: 118 us
  waiting for transfers between devices  73.6 us (62%)
  between operations  15.6 us (13%)
  matrix products  14.6 us (12%)
  local copies, waits for them, and re-layouts  13.1 us (11%)
  other arithmetic  1.5 us (1%)
    all_gather x1, waiting for transfers between devices, local(): ph_all = lax.all_gather(ph_interaction, 'chan', axis=0, tiled=True)  72.8 us
    dot_general x1, matrix products, local(): jnp.einsum('crk,kch->rch', pair_interaction, lowered, preferred_element_t...  12.4 us
    gather x1, local copies, waits for them, and re-layouts, local(): chosen = ph_all[ph_owner]  4.08 us
    unnamed x3, local copies, waits for them, and re-layouts  2.91 us
  transfers between devices with their start and end apart: 2, of which 1 were waited for; matrix products, arithmetic and copies ran while one was open for 21% of the time, Pallas kernels for 0%

profile of v1, /device:TPU:1, one launch (start us, length us, event | category | flops | bytes accessed | tf_op | source)
XLA Modules:
  0.0 118.4 jit_solution(1773826140644148565)
XLA Ops:
  7.4 0.0 all-gather.2.cloned.1.call-start
  7.4 0.7 all-gather.2.cloned.1.call-update
  8.1 0.0 reduce-scatter.2.cloned.1.call-start
  8.1 2.6 %copy.18 = f32[1152,1,256]{0,2,1:T(8,128)S(1)} copy(f32[1152,1,256]{2,1,0:T(1,128)} %param.5) | data formatting | bytes 2359296 | tf_op args[0]
  11.4 0.1 broadcast_select_fusion
  11.5 12.4 %fusion.2 = f32[4608,1,256]{0,2,1:T(8,128)} fusion(bf16[1,4608,1152]{2,1,0:T(8,128)(2,1)} %param.6, f32[1152,1,256]{0,2,1:T(8,128)S(1)} %broadcast_select_fusion), kind=kOutput, calls=%fused_computation.3 | convolution fusion | flops 2718203904 | bytes 16515072 | tf_op jit(solution)/shard_map/crk,kch->rch/dot_general | solution.py:19
  23.9 0.0 reduce-scatter.2.cloned.1.call-update
  23.9 0.0 copy-start
  23.9 0.4 copy.20
  24.3 0.3 copy-done
  24.6 0.1 copy.19
  24.7 0.1 reshape.38
  24.8 0.6 reshape.34
  25.4 72.8 %all-gather.2.cloned.1.call-done = f32[128,128,128]{2,1,0:T(8,128)} async-done(((f32[2,128,128]{2,1,0:T(8,128)}), f32[128,128,128]{2,1,0:T(8,128)}) %all-gather.2.cloned.1.call-update) | async-done | bytes 8388624 | tf_op jit(solution)/shard_map/all_gather | solution.py:12
  98.3 4.1 %gather_fusion = f32[36,128,128]{2,1,0:T(8,128)S(1)} fusion(f32[128,128,128]{2,1,0:T(8,128)} %all-gather.2.cloned.1.call-done, s32[1024]{0:T(1024)S(1)} %pad_clamp_fusion), kind=kCustom, calls=%fused_computation | custom fusion | bytes 4718736 | tf_op jit(solution)/shard_map/gather | solution.py:25
  102.4 2.2 %convolution_bitcast_fusion = f32[18,64,1,2,128]{4,1,3,0,2:T(8,128)S(1)} fusion(f32[18,2,128,128]{3,2,1,0:T(8,128)S(1)} %bitcast.24, f32[18,64,2,128]{3,2,1,0:T(2,128)S(1)} %reshape.34), kind=kOutput, calls=%fused_computation.4 | convolution fusion | flops 452984832 | bytes 4718592 | tf_op jit(solution)/shard_map/rschk,rchkl->rschl/dot_general | solution.py:26
  104.5 0.9 copy.22
  105.5 1.9 %copy.23 = f32[1152,1,256]{0,2,1:T(8,128)S(1)} copy(f32[1152,1,256]{2,1,0:T(1,128)S(1)} %bitcast.25) | data formatting | bytes 2359296 | tf_op jit(solution)/shard_map/reshape | solution.py:28
  107.4 0.0 reduce-scatter.2.cloned.1.call-done
  107.5 1.4 %select_add_fusion = f32[1152,1,256]{0,2,1:T(8,128)S(1)} fusion(f32[1152,1,256]{0,2,1:T(8,128)S(1)} %copy.23, f32[1152,1,256]{0,2,1:T(8,128)} %reduce-scatter.2.cloned.1.call-done, pred[1152]{0:T(1024)(128)(4,1)S(1)} %add_compare_fusion), kind=kLoop, calls=%fused_computation.6 | loop fusion | flops 589824 | bytes 3540096 | tf_op jit(solution)/shard_map/add | solution.py:29
  108.9 2.1 %copy.24 = f32[1152,1,256]{2,1,0:T(1,128)} copy(f32[1152,1,256]{0,2,1:T(8,128)S(1)} %select_add_fusion) | data formatting | bytes 2359296 | tf_op jit(solution)/shard_map/add | solution.py:29
  (3 shorter events, 0.0 us)
Async XLA Ops:
  7.4 90.9 %all-gather.2.cloned.1.call-start = ((), (), s32[]{:S(2)}) async-start(), calls=%async_computation.2 | async-start | bytes 8519680 | tf_op jit(solution)/shard_map/all_gather | solution.py:12
  8.1 99.4 %reduce-scatter.2.cloned.1.call-start = ((), (), s32[]{:S(2)}) async-start(), calls=%async_computation.1 | async-start | bytes 5898240 | tf_op jit(solution)/shard_map/reduce_scatter | solution.py:18
  23.9 0.7 copy-start
Sparse Core Ops, SparseCore 0:
  11.0 87.2 all-gather.1
Sparse Core Ops, SparseCore 1:
  24.0 57.3 reduce-scatter.1

commit v2 on v1

--- a/solution.py
+++ b/solution.py
@@ -1,7 +1,10 @@
 import jax
 import jax.numpy as jnp
 from jax import lax
+from jax.sharding import Mesh
 from jax.sharding import PartitionSpec as P
+
+CHAN = ("cy", "cz", "core")
 
 
 def local(amplitudes, pair_interaction, ph_interaction, pp_size, ph_owner):
@@ -9,7 +12,11 @@
     row_tiles, _, col_tiles = ph_owner.shape
     tile_rows = row_count // row_tiles
     tile_cols = hole_width // col_tiles
-    ph_all = lax.all_gather(ph_interaction, "chan", axis=0, tiled=True)
+    per_dev = ph_interaction.shape[0]
+    cores = lax.axis_size("core")
+    half = lax.all_gather(ph_interaction, ("cy", "cz"), axis=0, tiled=False)
+    ph_all = lax.all_gather(half, "core", axis=1, tiled=False)
+    ph_all = ph_all.reshape((-1,) + ph_interaction.shape[1:])
     offset = lax.axis_index("ctr") * row_count
     positions = offset + jnp.arange(row_count, dtype=jnp.int32)
     live_mask = positions[:, None] < (pp_size * tile_rows)[None, :]
@@ -30,12 +37,19 @@
 
 
 def solution(mesh):
+    chan_size, ctr_size = mesh.devices.shape
+    cores = 2
+    cz = 8
+    fine = Mesh(
+        mesh.devices.reshape(chan_size // (cz * cores), cz, cores, ctr_size),
+        CHAN + ("ctr",),
+    )
     in_specs = (
-        P("ctr", "chan", None),
-        P("chan", None, "ctr"),
-        P("chan", None, None),
-        P("chan"),
-        P("ctr", "chan", None),
+        P("ctr", CHAN, None),
+        P(CHAN, None, "ctr"),
+        P(CHAN, None, None),
+        P(CHAN),
+        P("ctr", CHAN, None),
     )
-    out_specs = P("ctr", "chan", None)
-    return jax.shard_map(local, mesh=mesh, in_specs=in_specs, out_specs=out_specs, check_vma=False)
+    out_specs = P("ctr", CHAN, None)
+    return jax.shard_map(local, mesh=fine, in_specs=in_specs, out_specs=out_specs, check_vma=False)

time: 119 us -> 175 us (1.47)
  waiting for transfers between devices: 73.6 us -> 129 us
    reduce_scatter x1, waiting for transfers between devices: 0.03 us -> 32.6 us  [local(): lax.psum_scatter(jnp.einsum('crk,kch->rch', pair_interaction, lowered, pr...]
    all_gather x1 -> x2, waiting for transfers between devices: 72.8 us -> 95.4 us  [the longest x1 85.6 us: local(): half = lax.all_gather(ph_interaction, ('cy', 'cz'), axis=0, tiled=False)]
  transfers between devices with their start and end apart: 2 -> 3, of which waited for: 1 -> 3; matrix products, arithmetic and copies ran while one was open for 21% -> 14% of each run, Pallas kernels for 0% -> 0%
where the time goes in v2:
time: 175 us
  waiting for transfers between devices  129 us (74%)
  between operations  15.6 us (9%)
  matrix products  14.6 us (8%)
  local copies, waits for them, and re-layouts  14.2 us (8%)
    all_gather x1, waiting for transfers between devices, local(): half = lax.all_gather(ph_interaction, ('cy', 'cz'), axis=0, tiled=False)  85.6 us
    reduce_scatter x1, waiting for transfers between devices, local(): lax.psum_scatter(jnp.einsum('crk,kch->rch', pair_interaction, lowered, pr...  32.6 us
    dot_general x1, matrix products, local(): jnp.einsum('crk,kch->rch', pair_interaction, lowered, preferred_element_t...  12.4 us
    all_gather x1, waiting for transfers between devices, local(): ph_all = lax.all_gather(half, 'core', axis=1, tiled=False)  9.72 us
    gather x1, local copies, waits for them, and re-layouts, local(): chosen = ph_all[ph_owner]  4.6 us
  transfers between devices with their start and end apart: 3, of which 3 were waited for; matrix products, arithmetic and copies ran while one was open for 14% of the time, Pallas kernels for 0%

profile of v2, /device:TPU:1, one launch (start us, length us, event | category | flops | bytes accessed | tf_op | source)
XLA Modules:
  0.0 174.6 jit_solution(18372495136050464014)
XLA Ops:
  7.4 0.0 all-gather.5.cloned.1.call-start
  7.4 0.7 all-gather.5.cloned.1.call-update
  8.1 0.0 all-gather.7.cloned.1.call-start
  8.1 85.6 %all-gather.5.cloned.1.call-done = f32[64,128,128]{2,1,0:T(8,128)} async-done(((f32[2,128,128]{2,1,0:T(8,128)}), f32[64,128,128]{2,1,0:T(8,128)}) %all-gather.5.cloned.1.call-update) | async-done | bytes 4194320 | tf_op jit(solution)/shard_map/all_gather | solution.py:17
  93.8 0.0 copy-start
  93.8 0.0 all-gather.7.cloned.1.call-update
  93.8 0.0 reduce-scatter.2.cloned.1.call-start
  93.9 1.2 copy-done
  95.0 1.9 %copy.18 = f32[1152,1,256]{0,2,1:T(8,128)S(1)} copy(f32[1152,1,256]{2,1,0:T(1,128)S(1)} %copy-done) | data formatting | bytes 2359296 | tf_op args[0]
  97.6 0.1 broadcast_select_fusion
  97.7 12.4 %fusion.2 = f32[4608,1,256]{0,2,1:T(8,128)} fusion(bf16[1,4608,1152]{2,1,0:T(8,128)(2,1)} %param.6, f32[1152,1,256]{0,2,1:T(8,128)S(1)} %broadcast_select_fusion), kind=kOutput, calls=%fused_computation.3 | convolution fusion | flops 2718203904 | bytes 16515072 | tf_op jit(solution)/shard_map/crk,kch->rch/dot_general | solution.py:26
  110.1 0.0 reduce-scatter.2.cloned.1.call-update
  110.2 0.0 copy-start.1
  110.2 0.4 copy.20
  110.6 0.3 copy-done.1
  110.9 0.1 copy.19
  111.0 0.1 reshape.42
  111.1 0.6 reshape.38
  111.7 9.7 %all-gather.7.cloned.1.call-done = f32[32,4,128,128]{3,2,1,0:T(8,128)} async-done(((f32[32,2,128,128]{3,2,1,0:T(8,128)}), f32[32,4,128,128]{3,2,1,0:T(8,128)}) %all-gather.7.cloned.1.call-update) | async-done | bytes 8388624 | tf_op jit(solution)/shard_map/all_gather | solution.py:18
  121.4 4.6 %gather_fusion = f32[36,128,128]{2,1,0:T(8,128)S(1)} fusion(f32[128,128,128]{2,1,0:T(8,128)} %bitcast.29, s32[1024]{0:T(1024)S(1)} %pad_clamp_fusion), kind=kCustom, calls=%fused_computation | custom fusion | bytes 4718736 | tf_op jit(solution)/shard_map/gather | solution.py:32
  126.0 2.2 %convolution_bitcast_fusion = f32[18,64,1,2,128]{4,1,3,0,2:T(8,128)S(1)} fusion(f32[18,2,128,128]{3,2,1,0:T(8,128)S(1)} %bitcast.26, f32[18,64,2,128]{3,2,1,0:T(2,128)S(1)} %reshape.38), kind=kOutput, calls=%fused_computation.4 | convolution fusion | flops 452984832 | bytes 4718592 | tf_op jit(solution)/shard_map/rschk,rchkl->rschl/dot_general | solution.py:33
  128.2 0.9 copy.22
  129.1 1.9 %copy.23 = f32[1152,1,256]{0,2,1:T(8,128)S(1)} copy(f32[1152,1,256]{2,1,0:T(1,128)S(1)} %bitcast.27) | data formatting | bytes 2359296 | tf_op jit(solution)/shard_map/reshape | solution.py:35
  131.1 32.6 %reduce-scatter.2.cloned.1.call-done = f32[1152,1,256]{0,2,1:T(8,128)} async-done(((f32[4608,1,256]{0,2,1:T(8,128)}), f32[1152,1,256]{0,2,1:T(8,128)}) %reduce-scatter.2.cloned.1.call-update) | async-done | bytes 1179664 | tf_op jit(solution)/shard_map/reduce_scatter | solution.py:25
  163.7 1.4 select_add_fusion
  165.1 2.1 %copy.24 = f32[1152,1,256]{2,1,0:T(1,128)} copy(f32[1152,1,256]{0,2,1:T(8,128)S(1)} %select_add_fusion) | data formatting | bytes 2359296 | tf_op jit(solution)/shard_map/add | solution.py:36
  (3 shorter events, 0.0 us)
Async XLA Ops:
  7.4 86.4 %all-gather.5.cloned.1.call-start = ((), (), s32[]{:S(2)}) async-start(), calls=%async_computation.2 | async-start | bytes 4325376 | tf_op jit(solution)/shard_map/all_gather | solution.py:17
  8.1 113.3 %all-gather.7.cloned.1.call-start = ((), (), s32[]{:S(2)}) async-start(), calls=%async_computation.3 | async-start | bytes 12582912 | tf_op jit(solution)/shard_map/all_gather | solution.py:18
  93.8 1.3 copy-start
  93.8 69.9 %reduce-scatter.2.cloned.1.call-start = ((), (), s32[]{:S(2)}) async-start(), calls=%async_computation.1 | async-start | bytes 5898240 | tf_op jit(solution)/shard_map/reduce_scatter | solution.py:25
  110.2 0.7 copy-start.1
Sparse Core Ops, SparseCore 0:
  10.8 82.9 all-gather.4
  95.6 25.7 all-gather.6
Sparse Core Ops, SparseCore 1:
  110.2 53.4 reduce-scatter.1

commit v3 on v2

--- a/solution.py
+++ b/solution.py
@@ -7,16 +7,40 @@
 CHAN = ("cy", "cz", "core")
 
 
+def shift(x, axis, step):
+    n = lax.axis_size(axis)
+    return lax.ppermute(x, axis, [(k, (k + step) % n) for k in range(n)])
+
+
+def ring_gather(x, axis):
+    n = lax.axis_size(axis)
+    up = [x]
+    down = [x]
+    for _ in range((n - 1) // 2):
+        up.append(shift(up[-1], axis, -1))
+        down.append(shift(down[-1], axis, 1))
+    pieces = up
+    if n % 2 == 0:
+        cut = x.shape[0] // 2
+        far = jnp.concatenate(
+            [shift(up[-1][:cut], axis, -1), shift(down[-1][cut:], axis, 1)], axis=0
+        )
+        pieces = pieces + [far]
+    pieces = pieces + down[1:][::-1]
+    return jnp.stack(pieces, axis=0)
+
+
 def local(amplitudes, pair_interaction, ph_interaction, pp_size, ph_owner):
     row_count, chan_count, hole_width = amplitudes.shape
     row_tiles, _, col_tiles = ph_owner.shape
     tile_rows = row_count // row_tiles
     tile_cols = hole_width // col_tiles
     per_dev = ph_interaction.shape[0]
-    cores = lax.axis_size("core")
-    half = lax.all_gather(ph_interaction, ("cy", "cz"), axis=0, tiled=False)
-    ph_all = lax.all_gather(half, "core", axis=1, tiled=False)
-    ph_all = ph_all.reshape((-1,) + ph_interaction.shape[1:])
+    ny, nz, nc = lax.axis_size("cy"), lax.axis_size("cz"), lax.axis_size("core")
+    gathered = ring_gather(ph_interaction, "cz")
+    gathered = ring_gather(gathered, "cy")
+    gathered = jnp.stack([gathered, shift(gathered, "core", 1)], axis=0)
+    ph_all = gathered.reshape((-1,) + ph_interaction.shape[1:])
     offset = lax.axis_index("ctr") * row_count
     positions = offset + jnp.arange(row_count, dtype=jnp.int32)
     live_mask = positions[:, None] < (pp_size * tile_rows)[None, :]
@@ -28,8 +52,13 @@
         scatter_dimension=0,
         tiled=True,
     )
+    owner_dev = ph_owner // per_dev
+    o_y = (owner_dev // (nz * nc) - lax.axis_index("cy")) % ny
+    o_z = (owner_dev // nc % nz - lax.axis_index("cz")) % nz
+    o_c = (owner_dev % nc - lax.axis_index("core")) % nc
+    slot = ((o_c * ny + o_y) * nz + o_z) * per_dev + ph_owner % per_dev
     blocks = masked.reshape(row_tiles, tile_rows, chan_count, col_tiles, tile_cols)
-    chosen = ph_all[ph_owner]
+    chosen = ph_all[slot]
     cycle = jnp.einsum(
         "rschk,rchkl->rschl", blocks, chosen, precision=lax.Precision.HIGHEST
     ).reshape(row_count, chan_count, hole_width)

time: 175 us -> 128 us (0.73)
  waiting for transfers between devices: 129 us -> 42.8 us
  starting transfers between devices: 0.08 us -> 29 us
  other arithmetic: 1.49 us -> 13.7 us
    all_gather x2 -> x0, waiting for transfers between devices: 95.4 us -> none  [the longest x1 85.6 us: local(): half = lax.all_gather(ph_interaction, ('cy', 'cz'), axis=0, tiled=False)]
    ppermute x0 -> x13, waiting for transfers between devices: none -> 42.8 us  [shift(): return lax.ppermute(x, axis, [(k, (k + step) % n) for k in range(n)])]
    reduce_scatter x1, waiting for transfers between devices: 32.6 us -> 0.02 us  [local(): lax.psum_scatter(jnp.einsum('crk,kch->rch', pair_interaction, lowered, pr...]
    ppermute x0 -> x13, starting transfers between devices: none -> 29 us  [shift(): return lax.ppermute(x, axis, [(k, (k + step) % n) for k in range(n)])]
    another operation x0 -> x3, other arithmetic: none -> 12.2 us  [the longest x2 12.1 us: local(): gathered = jnp.stack([gathered, shift(gathered, 'core', 1)], axis=0)]
    unnamed x5 -> x11, local copies, waits for them, and re-layouts: 3.44 us -> 3.55 us
  transfers between devices with their start and end apart: 3 -> 14, of which waited for: 3 -> 9; matrix products, arithmetic and copies ran while one was open for 14% -> 18% of each run, Pallas kernels for 0% -> 0%
where the time goes in v3:
time: 128 us
  waiting for transfers between devices  42.8 us (33%)
  starting transfers between devices  29 us (23%)
  matrix products  14.6 us (11%)
  between operations  14.3 us (11%)
  local copies, waits for them, and re-layouts  13.9 us (11%)
  other arithmetic  13.7 us (11%)
    ppermute x13, waiting for transfers between devices, shift(): return lax.ppermute(x, axis, [(k, (k + step) % n) for k in range(n)])  42.8 us
    ppermute x13, starting transfers between devices, shift(): return lax.ppermute(x, axis, [(k, (k + step) % n) for k in range(n)])  29 us
    dot_general x1, matrix products, local(): jnp.einsum('crk,kch->rch', pair_interaction, lowered, preferred_element_t...  12.4 us
    another operation x2, other arithmetic, local(): gathered = jnp.stack([gathered, shift(gathered, 'core', 1)], axis=0)  12.1 us
    gather x1, local copies, waits for them, and re-layouts, local(): chosen = ph_all[slot]  4.08 us
    unnamed x11, local copies, waits for them, and re-layouts  3.55 us
  transfers between devices with their start and end apart: 14, of which 9 were waited for; matrix products, arithmetic and copies ran while one was open for 18% of the time, Pallas kernels for 0%

profile of v3, /device:TPU:1, one launch (start us, length us, event | category | flops | bytes accessed | tf_op | source)
XLA Modules:
  0.0 128.2 jit_solution(14219557129925550499)
XLA Ops:
  7.2 2.6 %copy.11 = f32[1152,1,256]{0,2,1:T(8,128)S(1)} copy(f32[1152,1,256]{2,1,0:T(1,128)} %param.5) | data formatting | bytes 2359296 | tf_op args[0]
  9.9 12.4 %fusion.2 = f32[4608,1,256]{0,2,1:T(8,128)} fusion(bf16[1,4608,1152]{2,1,0:T(8,128)(2,1)} %param.6, f32[1152,1,256]{0,2,1:T(8,128)S(1)} %broadcast_select_fusion), kind=kOutput, calls=%fused_computation.4 | convolution fusion | flops 2718203904 | bytes 16515072 | tf_op jit(solution)/shard_map/crk,kch->rch/dot_general | solution.py:50
  22.4 0.9 copy-done
  23.2 6.4 %collective-permute-start = (f32[2,128,128]{2,1,0:T(8,128)S(1)}, f32[2,128,128]{2,1,0:T(8,128)S(1)}, u32[]{:S(2)}, u32[]{:S(2)}) collective-permute-start(f32[2,128,128]{2,1,0:T(8,128)S(1)} %copy-done), channel_id=1, source_target_pairs={{0,56},{8,0},{16,8},{24,16},{32,24},{40,32},{48,40},{56,48},{1,57}... | collective-permute-start | bytes 393224 | tf_op jit(solution)/shard_map/ppermute | solution.py:12
  29.7 2.1 %collective-permute-done = f32[2,128,128]{2,1,0:T(8,128)S(1)} collective-permute-done((f32[2,128,128]{2,1,0:T(8,128)S(1)}, f32[2,128,128]{2,1,0:T(8,128)S(1)}, u32[]{:S(2)}, u32[]{:S(2)}) %collective-permute-start) | collective-permute-done | bytes 131104 | tf_op jit(solution)/shard_map/ppermute | solution.py:12
  31.8 3.4 %collective-permute-start.1 = (f32[2,128,128]{2,1,0:T(8,128)S(1)}, f32[2,128,128]{2,1,0:T(8,128)S(1)}, u32[]{:S(2)}, u32[]{:S(2)}) collective-permute-start(f32[2,128,128]{2,1,0:T(8,128)S(1)} %collective-permute-done), channel_id=1, source_target_pairs={{0,56},{8,0},{16,8},{24,16},{32,24},{40,32},{48,40},{56,48},{1,57}... | collective-permute-start | bytes 393224 | tf_op jit(solution)/shard_map/ppermute | solution.py:12
  35.3 1.9 %collective-permute-done.1 = f32[2,128,128]{2,1,0:T(8,128)S(1)} collective-permute-done((f32[2,128,128]{2,1,0:T(8,128)S(1)}, f32[2,128,128]{2,1,0:T(8,128)S(1)}, u32[]{:S(2)}, u32[]{:S(2)}) %collective-permute-start.1) | collective-permute-done | bytes 131104 | tf_op jit(solution)/shard_map/ppermute | solution.py:12
  37.2 3.1 %collective-permute-start.2 = (f32[2,128,128]{2,1,0:T(8,128)S(1)}, f32[2,128,128]{2,1,0:T(8,128)S(1)}, u32[]{:S(2)}, u32[]{:S(2)}) collective-permute-start(f32[2,128,128]{2,1,0:T(8,128)S(1)} %collective-permute-done.1), channel_id=1, source_target_pairs={{0,56},{8,0},{16,8},{24,16},{32,24},{40,32},{48,40},{56,48},{1,57}... | collective-permute-start | bytes 393224 | tf_op jit(solution)/shard_map/ppermute | solution.py:12
  40.3 1.9 %collective-permute-done.2 = f32[2,128,128]{2,1,0:T(8,128)S(1)} collective-permute-done((f32[2,128,128]{2,1,0:T(8,128)S(1)}, f32[2,128,128]{2,1,0:T(8,128)S(1)}, u32[]{:S(2)}, u32[]{:S(2)}) %collective-permute-start.2) | collective-permute-done | bytes 131104 | tf_op jit(solution)/shard_map/ppermute | solution.py:12
  42.2 3.5 %collective-permute-start.3 = (f32[1,128,128]{2,1,0:T(8,128)S(1)}, f32[1,128,128]{2,1,0:T(8,128)S(1)}, u32[]{:S(2)}, u32[]{:S(2)}) collective-permute-start(f32[1,128,128]{2,1,0:T(8,128)S(1)} %slice.18), channel_id=1, source_target_pairs={{0,56},{8,0},{16,8},{24,16},{32,24},{40,32},{48,40},{56,48},{1,57}... | collective-permute-start | bytes 196616 | tf_op jit(solution)/shard_map/ppermute | solution.py:12
  45.8 1.2 collective-permute-done.3
  47.0 3.5 %collective-permute-done.7 = f32[1,128,128]{2,1,0:T(8,128)S(1)} collective-permute-done((f32[1,128,128]{2,1,0:T(8,128)S(1)}, f32[1,128,128]{2,1,0:T(8,128)S(1)}, u32[]{:S(2)}, u32[]{:S(2)}) %collective-permute-start.7) | collective-permute-done | bytes 65568 | tf_op jit(solution)/shard_map/ppermute | solution.py:12
  50.6 1.4 %collective-permute-start.10 = (f32[8,2,128,128]{3,2,1,0:T(8,128)S(1)}, f32[8,2,128,128]{3,2,1,0:T(8,128)S(1)}, u32[]{:S(2)}, u32[]{:S(2)}) collective-permute-start(f32[8,2,128,128]{3,2,1,0:T(8,128)S(1)} %bitcast_dynamic-update-slice_fusion), channel_id=1, source_target_pairs={{0,64},{64,128},{128,192},{192,0},{1,65},{65,129},{129,193},{193,1... | collective-permute-start | bytes 3145736 | tf_op jit(solution)/shard_map/ppermute | solution.py:12
  52.0 1.5 %collective-permute-start.8 = (f32[8,2,128,128]{3,2,1,0:T(8,128)S(1)}, f32[8,2,128,128]{3,2,1,0:T(8,128)S(1)}, u32[]{:S(2)}, u32[]{:S(2)}) collective-permute-start(f32[8,2,128,128]{3,2,1,0:T(8,128)S(1)} %bitcast_dynamic-update-slice_fusion), channel_id=1, source_target_pairs={{0,192},{64,0},{128,64},{192,128},{1,193},{65,1},{129,65},{193,129... | collective-permute-start | bytes 3145736 | tf_op jit(solution)/shard_map/ppermute | solution.py:12
  53.5 18.8 %collective-permute-done.10 = f32[8,2,128,128]{3,2,1,0:T(8,128)S(1)} collective-permute-done((f32[8,2,128,128]{3,2,1,0:T(8,128)S(1)}, f32[8,2,128,128]{3,2,1,0:T(8,128)S(1)}, u32[]{:S(2)}, u32[]{:S(2)}) %collective-permute-start.10) | collective-permute-done | bytes 1048608 | tf_op jit(solution)/shard_map/ppermute | solution.py:12
  72.5 2.9 %collective-permute-start.9 = (f32[4,2,128,128]{3,2,1,0:T(8,128)S(1)}, f32[4,2,128,128]{3,2,1,0:T(8,128)S(1)}, u32[]{:S(2)}, u32[]{:S(2)}) collective-permute-start(f32[4,2,128,128]{3,2,1,0:T(8,128)S(1)} %slice.20), channel_id=1, source_target_pairs={{0,192},{64,0},{128,64},{192,128},{1,193},{65,1},{129,65},{193,129... | collective-permute-start | bytes 1572872 | tf_op jit(solution)/shard_map/ppermute | solution.py:12
  75.4 7.1 %collective-permute-done.11 = f32[4,2,128,128]{3,2,1,0:T(8,128)S(1)} collective-permute-done((f32[4,2,128,128]{3,2,1,0:T(8,128)S(1)}, f32[4,2,128,128]{3,2,1,0:T(8,128)S(1)}, u32[]{:S(2)}, u32[]{:S(2)}) %collective-permute-start.11) | collective-permute-done | bytes 524320 | tf_op jit(solution)/shard_map/ppermute | solution.py:12
  82.4 0.3 collective-permute-done.9
  82.8 4.3 %fusion.19 = (f32[1,4,8,2,128,128]{5,4,3,2,1,0:T(8,128)}, f32[4,8,2,128,128]{4,3,2,1,0:T(8,128)}) fusion(f32[1,8,2,128,128]{4,3,2,1,0:T(8,128)S(1)} %bitcast.54, f32[1,8,2,128,128]{4,3,2,1,0:T(8,128)S(1)} %maximum_bitcast_fusion, f32[1,8,2,128,128]{4,3,2,1,0:T(8,128)S(1)} %bitcast.55, f32[1,8,2,128,128]{4,3,2,1,0:T(8,128)S(1)} %bitcast.56), kind=kLoop, calls=%fused_computation.60 | loop fusion | flops 3145728 | bytes 12582912 | tf_op jit(solution)/shard_map/stack | solution.py:42
  87.1 6.6 %collective-permute-start.12 = (f32[4,8,2,128,128]{4,3,2,1,0:T(8,128)}, f32[4,8,2,128,128]{4,3,2,1,0:T(8,128)}, u32[]{:S(2)}, u32[]{:S(2)}) collective-permute-start(f32[4,8,2,128,128]{4,3,2,1,0:T(8,128)} %get-tuple-element.6), channel_id=1, source_target_pairs={{0,4},{4,0},{1,5},{5,1},{2,6},{6,2},{3,7},{7,3},{8,12},{12,8},{9,1... | collective-permute-start | bytes 12582920 | tf_op jit(solution)/shard_map/ppermute | solution.py:12
  93.8 0.4 copy.13
  94.2 0.1 copy.12
  94.3 0.1 reshape.42
  94.4 0.6 reshape.38
  95.0 5.9 %collective-permute-done.12 = f32[4,8,2,128,128]{4,3,2,1,0:T(8,128)} collective-permute-done((f32[4,8,2,128,128]{4,3,2,1,0:T(8,128)}, f32[4,8,2,128,128]{4,3,2,1,0:T(8,128)}, u32[]{:S(2)}, u32[]{:S(2)}) %collective-permute-start.12) | collective-permute-done | bytes 4194336 | tf_op jit(solution)/shard_map/ppermute | solution.py:12
  100.9 7.8 %pad_maximum_fusion = f32[2,4,8,2,128,128]{5,4,3,2,1,0:T(8,128)} fusion(f32[1,4,8,2,128,128]{5,4,3,2,1,0:T(8,128)} %bitcast.18, f32[1,4,8,2,128,128]{5,4,3,2,1,0:T(8,128)} %get-tuple-element.5), kind=kLoop, calls=%fused_computation.3 | loop fusion | flops 2097152 | bytes 16777216 | tf_op jit(solution)/shard_map/stack | solution.py:42
  108.7 4.1 %gather_fusion = f32[36,128,128]{2,1,0:T(8,128)S(1)} fusion(f32[128,128,128]{2,1,0:T(8,128)} %bitcast.51, s32[1024]{0:T(1024)S(1)} %pad_clamp_fusion), kind=kCustom, calls=%fused_computation | custom fusion | bytes 4718736 | tf_op jit(solution)/shard_map/gather | solution.py:61
  112.8 2.2 %convolution_bitcast_fusion = f32[18,64,1,2,128]{4,1,3,0,2:T(8,128)S(1)} fusion(f32[18,2,128,128]{3,2,1,0:T(8,128)S(1)} %bitcast.52, f32[18,64,2,128]{3,2,1,0:T(2,128)S(1)} %reshape.38), kind=kOutput, calls=%fused_computation.6 | convolution fusion | flops 452984832 | bytes 4718592 | tf_op jit(solution)/shard_map/rschk,rchkl->rschl/dot_general | solution.py:62
  115.0 0.9 copy.15
  115.9 1.9 %copy.16 = f32[1152,1,256]{0,2,1:T(8,128)S(1)} copy(f32[1152,1,256]{2,1,0:T(1,128)S(1)} %bitcast.53) | data formatting | bytes 2359296 | tf_op jit(solution)/shard_map/reshape | solution.py:64
  117.9 1.4 %select_add_fusion = f32[1152,1,256]{0,2,1:T(8,128)S(1)} fusion(f32[1152,1,256]{0,2,1:T(8,128)S(1)} %copy.16, f32[1152,1,256]{0,2,1:T(8,128)} %reduce-scatter.2.cloned.1.call-done, pred[1152]{0:T(1024)(128)(4,1)S(1)} %add_compare_fusion), kind=kLoop, calls=%fused_computation.8 | loop fusion | flops 589824 | bytes 3540096 | tf_op jit(solution)/shard_map/add | solution.py:65
  119.3 2.1 %copy.17 = f32[1152,1,256]{2,1,0:T(1,128)} copy(f32[1152,1,256]{0,2,1:T(8,128)S(1)} %select_add_fusion) | data formatting | bytes 2359296 | tf_op jit(solution)/shard_map/add | solution.py:65
  (32 shorter events, 0.6 us)
Async XLA Ops:
  6.5 111.3 %reduce-scatter.2.cloned.1.call-start = ((), (), s32[]{:S(2)}) async-start(), calls=%async_computation.1 | async-start | bytes 5898240 | tf_op jit(solution)/shard_map/reduce_scatter | solution.py:49
  22.3 0.9 copy-start
  23.2 8.6 %collective-permute-start = (f32[2,128,128]{2,1,0:T(8,128)S(1)}, f32[2,128,128]{2,1,0:T(8,128)S(1)}, u32[]{:S(2)}, u32[]{:S(2)}) collective-permute-start(f32[2,128,128]{2,1,0:T(8,128)S(1)} %copy-done), channel_id=1, source_target_pairs={{0,56},{8,0},{16,8},{24,16},{32,24},{40,32},{48,40},{56,48},{1,57}... | collective-permute-start | bytes 393224 | tf_op jit(solution)/shard_map/ppermute | solution.py:12
  29.7 5.6 %collective-permute-start.4 = (f32[2,128,128]{2,1,0:T(8,128)S(1)}, f32[2,128,128]{2,1,0:T(8,128)S(1)}, u32[]{:S(2)}, u32[]{:S(2)}) collective-permute-start(f32[2,128,128]{2,1,0:T(8,128)S(1)} %copy-done), channel_id=1, source_target_pairs={{0,8},{8,16},{16,24},{24,32},{32,40},{40,48},{48,56},{56,0},{1,9},... | collective-permute-start | bytes 393224 | tf_op jit(solution)/shard_map/ppermute | solution.py:12
  31.8 5.4 %collective-permute-start.1 = (f32[2,128,128]{2,1,0:T(8,128)S(1)}, f32[2,128,128]{2,1,0:T(8,128)S(1)}, u32[]{:S(2)}, u32[]{:S(2)}) collective-permute-start(f32[2,128,128]{2,1,0:T(8,128)S(1)} %collective-permute-done), channel_id=1, source_target_pairs={{0,56},{8,0},{16,8},{24,16},{32,24},{40,32},{48,40},{56,48},{1,57}... | collective-permute-start | bytes 393224 | tf_op jit(solution)/shard_map/ppermute | solution.py:12
  35.2 5.0 %collective-permute-start.5 = (f32[2,128,128]{2,1,0:T(8,128)S(1)}, f32[2,128,128]{2,1,0:T(8,128)S(1)}, u32[]{:S(2)}, u32[]{:S(2)}) collective-permute-start(f32[2,128,128]{2,1,0:T(8,128)S(1)} %collective-permute-done.4), channel_id=1, source_target_pairs={{0,8},{8,16},{16,24},{24,32},{32,40},{40,48},{48,56},{56,0},{1,9},... | collective-permute-start | bytes 393224 | tf_op jit(solution)/shard_map/ppermute | solution.py:12
  37.2 5.0 %collective-permute-start.2 = (f32[2,128,128]{2,1,0:T(8,128)S(1)}, f32[2,128,128]{2,1,0:T(8,128)S(1)}, u32[]{:S(2)}, u32[]{:S(2)}) collective-permute-start(f32[2,128,128]{2,1,0:T(8,128)S(1)} %collective-permute-done.1), channel_id=1, source_target_pairs={{0,56},{8,0},{16,8},{24,16},{32,24},{40,32},{48,40},{56,48},{1,57}... | collective-permute-start | bytes 393224 | tf_op jit(solution)/shard_map/ppermute | solution.py:12
  40.3 5.4 %collective-permute-start.6 = (f32[2,128,128]{2,1,0:T(8,128)S(1)}, f32[2,128,128]{2,1,0:T(8,128)S(1)}, u32[]{:S(2)}, u32[]{:S(2)}) collective-permute-start(f32[2,128,128]{2,1,0:T(8,128)S(1)} %collective-permute-done.5), channel_id=1, source_target_pairs={{0,8},{8,16},{16,24},{24,32},{32,40},{40,48},{48,56},{56,0},{1,9},... | collective-permute-start | bytes 393224 | tf_op jit(solution)/shard_map/ppermute | solution.py:12
  42.2 4.8 %collective-permute-start.3 = (f32[1,128,128]{2,1,0:T(8,128)S(1)}, f32[1,128,128]{2,1,0:T(8,128)S(1)}, u32[]{:S(2)}, u32[]{:S(2)}) collective-permute-start(f32[1,128,128]{2,1,0:T(8,128)S(1)} %slice.18), channel_id=1, source_target_pairs={{0,56},{8,0},{16,8},{24,16},{32,24},{40,32},{48,40},{56,48},{1,57}... | collective-permute-start | bytes 196616 | tf_op jit(solution)/shard_map/ppermute | solution.py:12
  45.7 4.8 %collective-permute-start.7 = (f32[1,128,128]{2,1,0:T(8,128)S(1)}, f32[1,128,128]{2,1,0:T(8,128)S(1)}, u32[]{:S(2)}, u32[]{:S(2)}) collective-permute-start(f32[1,128,128]{2,1,0:T(8,128)S(1)} %slice.19), channel_id=1, source_target_pairs={{0,8},{8,16},{16,24},{24,32},{32,40},{40,48},{48,56},{56,0},{1,9},... | collective-permute-start | bytes 196616 | tf_op jit(solution)/shard_map/ppermute | solution.py:12
  50.6 21.7 %collective-permute-start.10 = (f32[8,2,128,128]{3,2,1,0:T(8,128)S(1)}, f32[8,2,128,128]{3,2,1,0:T(8,128)S(1)}, u32[]{:S(2)}, u32[]{:S(2)}) collective-permute-start(f32[8,2,128,128]{3,2,1,0:T(8,128)S(1)} %bitcast_dynamic-update-slice_fusion), channel_id=1, source_target_pairs={{0,64},{64,128},{128,192},{192,0},{1,65},{65,129},{129,193},{193,1... | collective-permute-start | bytes 3145736 | tf_op jit(solution)/shard_map/ppermute | solution.py:12
  52.0 20.5 %collective-permute-start.8 = (f32[8,2,128,128]{3,2,1,0:T(8,128)S(1)}, f32[8,2,128,128]{3,2,1,0:T(8,128)S(1)}, u32[]{:S(2)}, u32[]{:S(2)}) collective-permute-start(f32[8,2,128,128]{3,2,1,0:T(8,128)S(1)} %bitcast_dynamic-update-slice_fusion), channel_id=1, source_target_pairs={{0,192},{64,0},{128,64},{192,128},{1,193},{65,1},{129,65},{193,129... | collective-permute-start | bytes 3145736 | tf_op jit(solution)/shard_map/ppermute | solution.py:12
  72.3 10.1 %collective-permute-start.11 = (f32[4,2,128,128]{3,2,1,0:T(8,128)S(1)}, f32[4,2,128,128]{3,2,1,0:T(8,128)S(1)}, u32[]{:S(2)}, u32[]{:S(2)}) collective-permute-start(f32[4,2,128,128]{3,2,1,0:T(8,128)S(1)} %slice.21), channel_id=1, source_target_pairs={{0,64},{64,128},{128,192},{192,0},{1,65},{65,129},{129,193},{193,1... | collective-permute-start | bytes 1572872 | tf_op jit(solution)/shard_map/ppermute | solution.py:12
  72.5 10.3 %collective-permute-start.9 = (f32[4,2,128,128]{3,2,1,0:T(8,128)S(1)}, f32[4,2,128,128]{3,2,1,0:T(8,128)S(1)}, u32[]{:S(2)}, u32[]{:S(2)}) collective-permute-start(f32[4,2,128,128]{3,2,1,0:T(8,128)S(1)} %slice.20), channel_id=1, source_target_pairs={{0,192},{64,0},{128,64},{192,128},{1,193},{65,1},{129,65},{193,129... | collective-permute-start | bytes 1572872 | tf_op jit(solution)/shard_map/ppermute | solution.py:12
  87.1 7.0 %copy-start.1 = (s32[18,1,2]{0,2,1:T(2,128)S(1)}, s32[18,1,2]{0,2,1:T(2,128)}, u32[]{:S(2)}) copy-start(s32[18,1,2]{0,2,1:T(2,128)} %param.9) | copy-start | bytes 436
  87.1 13.7 %collective-permute-start.12 = (f32[4,8,2,128,128]{4,3,2,1,0:T(8,128)}, f32[4,8,2,128,128]{4,3,2,1,0:T(8,128)}, u32[]{:S(2)}, u32[]{:S(2)}) collective-permute-start(f32[4,8,2,128,128]{4,3,2,1,0:T(8,128)} %get-tuple-element.6), channel_id=1, source_target_pairs={{0,4},{4,0},{1,5},{5,1},{2,6},{6,2},{3,7},{7,3},{8,12},{12,8},{9,1... | collective-permute-start | bytes 12582920 | tf_op jit(solution)/shard_map/ppermute | solution.py:12
Sparse Core Ops, SparseCore 0:
  22.5 57.4 reduce-scatter.1

commit v4 on v3

--- a/solution.py
+++ b/solution.py
@@ -37,10 +37,10 @@
     tile_cols = hole_width // col_tiles
     per_dev = ph_interaction.shape[0]
     ny, nz, nc = lax.axis_size("cy"), lax.axis_size("cz"), lax.axis_size("core")
-    gathered = ring_gather(ph_interaction, "cz")
-    gathered = ring_gather(gathered, "cy")
-    gathered = jnp.stack([gathered, shift(gathered, "core", 1)], axis=0)
-    ph_all = gathered.reshape((-1,) + ph_interaction.shape[1:])
+    by_z = ring_gather(ph_interaction, "cz")
+    own = lax.all_gather(by_z, "cy", axis=0, tiled=False)
+    own = own.reshape((-1,) + ph_interaction.shape[1:])
+    sibling = shift(own, "core", 1)
     offset = lax.axis_index("ctr") * row_count
     positions = offset + jnp.arange(row_count, dtype=jnp.int32)
     live_mask = positions[:, None] < (pp_size * tile_rows)[None, :]
@@ -53,12 +53,12 @@
         tiled=True,
     )
     owner_dev = ph_owner // per_dev
-    o_y = (owner_dev // (nz * nc) - lax.axis_index("cy")) % ny
+    o_y = owner_dev // (nz * nc)
     o_z = (owner_dev // nc % nz - lax.axis_index("cz")) % nz
     o_c = (owner_dev % nc - lax.axis_index("core")) % nc
-    slot = ((o_c * ny + o_y) * nz + o_z) * per_dev + ph_owner % per_dev
+    slot = (o_y * nz + o_z) * per_dev + ph_owner % per_dev
     blocks = masked.reshape(row_tiles, tile_rows, chan_count, col_tiles, tile_cols)
-    chosen = ph_all[slot]
+    chosen = jnp.where((o_c == 0)[..., None, None], own[slot], sibling[slot])
     cycle = jnp.einsum(
         "rschk,rchkl->rschl", blocks, chosen, precision=lax.Precision.HIGHEST
     ).reshape(row_count, chan_count, hole_width)

time: 128 us -> 118 us (0.922)
  starting transfers between devices: 29 us -> 16.7 us
  other arithmetic: 13.7 us -> 1.56 us
  waiting for transfers between devices: 42.8 us -> 50.1 us
  local copies, waits for them, and re-layouts: 13.9 us -> 17.8 us
  matrix products: 14.6 us -> 16.3 us
  between operations: 14.3 us -> 15.7 us
    all_gather x0 -> x1, waiting for transfers between devices: none -> 37.8 us  [local(): own = lax.all_gather(by_z, 'cy', axis=0, tiled=False)]
    ppermute x13 -> x9, waiting for transfers between devices: 42.8 us -> 12.2 us  [shift(): return lax.ppermute(x, axis, [(k, (k + step) % n) for k in range(n)])]
    ppermute x13 -> x9, starting transfers between devices: 29 us -> 16.6 us  [shift(): return lax.ppermute(x, axis, [(k, (k + step) % n) for k in range(n)])]
    another operation x3 -> x0, other arithmetic: 12.2 us -> none  [the longest x2 12.1 us: local(): gathered = jnp.stack([gathered, shift(gathered, 'core', 1)], axis=0)]
    gather x1 -> x2, local copies, waits for them, and re-layouts: 4.08 us -> 7.25 us  [local(): chosen = jnp.where((o_c == 0)[..., None, None], own[slot], sibling[slot])]
    dot_general x1, matrix products: 2.18 us -> 3.99 us  [local(): jnp.einsum('rschk,rchkl->rschl', blocks, chosen, precision=lax.Precision....]
    unnamed x11 -> x13, local copies, waits for them, and re-layouts: 3.55 us -> 4.26 us
  transfers between devices with their start and end apart: 14 -> 11, of which waited for: 9 -> 7; matrix products, arithmetic and copies ran while one was open for 18% -> 26% of each run, Pallas kernels for 0% -> 0%
where the time goes in v4:
time: 118 us
  waiting for transfers between devices  50.1 us (42%)
  local copies, waits for them, and re-layouts  17.8 us (15%)
  starting transfers between devices  16.7 us (14%)
  matrix products  16.3 us (14%)
  between operations  15.7 us (13%)
  other arithmetic  1.56 us (1%)
    all_gather x1, waiting for transfers between devices, local(): own = lax.all_gather(by_z, 'cy', axis=0, tiled=False)  37.8 us
    ppermute x9, starting transfers between devices, shift(): return lax.ppermute(x, axis, [(k, (k + step) % n) for k in range(n)])  16.6 us
    dot_general x1, matrix products, local(): jnp.einsum('crk,kch->rch', pair_interaction, lowered, preferred_element_t...  12.4 us
    ppermute x9, waiting for transfers between devices, shift(): return lax.ppermute(x, axis, [(k, (k + step) % n) for k in range(n)])  12.2 us
    gather x2, local copies, waits for them, and re-layouts, local(): chosen = jnp.where((o_c == 0)[..., None, None], own[slot], sibling[slot])  7.25 us
    unnamed x13, local copies, waits for them, and re-layouts  4.26 us
    dot_general x1, matrix products, local(): jnp.einsum('rschk,rchkl->rschl', blocks, chosen, precision=lax.Precision....  3.99 us
  transfers between devices with their start and end apart: 11, of which 7 were waited for; matrix products, arithmetic and copies ran while one was open for 26% of the time, Pallas kernels for 0%

profile of v4, /device:TPU:1, one launch (start us, length us, event | category | flops | bytes accessed | tf_op | source)
XLA Modules:
  0.0 118.2 jit_solution(13641559694713578997)
XLA Ops:
  7.4 6.4 %collective-permute-start = (f32[2,128,128]{2,1,0:T(8,128)}, f32[2,128,128]{2,1,0:T(8,128)S(1)}, u32[]{:S(2)}, u32[]{:S(2)}) collective-permute-start(f32[2,128,128]{2,1,0:T(8,128)} %param.7), channel_id=1, source_target_pairs={{0,56},{8,0},{16,8},{24,16},{32,24},{40,32},{48,40},{56,48},{1,57}... | collective-permute-start | bytes 393224 | tf_op jit(solution)/shard_map/ppermute | solution.py:12
  13.8 1.0 bitcast_dynamic-update-slice_fusion.6
  14.8 1.5 %collective-permute-done = f32[2,128,128]{2,1,0:T(8,128)S(1)} collective-permute-done((f32[2,128,128]{2,1,0:T(8,128)}, f32[2,128,128]{2,1,0:T(8,128)S(1)}, u32[]{:S(2)}, u32[]{:S(2)}) %collective-permute-start) | collective-permute-done | bytes 131104 | tf_op jit(solution)/shard_map/ppermute | solution.py:12
  16.3 3.3 %collective-permute-start.1 = (f32[2,128,128]{2,1,0:T(8,128)S(1)}, f32[2,128,128]{2,1,0:T(8,128)S(1)}, u32[]{:S(2)}, u32[]{:S(2)}) collective-permute-start(f32[2,128,128]{2,1,0:T(8,128)S(1)} %collective-permute-done), channel_id=1, source_target_pairs={{0,56},{8,0},{16,8},{24,16},{32,24},{40,32},{48,40},{56,48},{1,57}... | collective-permute-start | bytes 393224 | tf_op jit(solution)/shard_map/ppermute | solution.py:12
  19.6 1.9 %collective-permute-done.1 = f32[2,128,128]{2,1,0:T(8,128)S(1)} collective-permute-done((f32[2,128,128]{2,1,0:T(8,128)S(1)}, f32[2,128,128]{2,1,0:T(8,128)S(1)}, u32[]{:S(2)}, u32[]{:S(2)}) %collective-permute-start.1) | collective-permute-done | bytes 131104 | tf_op jit(solution)/shard_map/ppermute | solution.py:12
  21.5 3.1 %collective-permute-start.2 = (f32[2,128,128]{2,1,0:T(8,128)S(1)}, f32[2,128,128]{2,1,0:T(8,128)S(1)}, u32[]{:S(2)}, u32[]{:S(2)}) collective-permute-start(f32[2,128,128]{2,1,0:T(8,128)S(1)} %collective-permute-done.1), channel_id=1, source_target_pairs={{0,56},{8,0},{16,8},{24,16},{32,24},{40,32},{48,40},{56,48},{1,57}... | collective-permute-start | bytes 393224 | tf_op jit(solution)/shard_map/ppermute | solution.py:12
  24.6 1.9 %collective-permute-done.2 = f32[2,128,128]{2,1,0:T(8,128)S(1)} collective-permute-done((f32[2,128,128]{2,1,0:T(8,128)S(1)}, f32[2,128,128]{2,1,0:T(8,128)S(1)}, u32[]{:S(2)}, u32[]{:S(2)}) %collective-permute-start.2) | collective-permute-done | bytes 131104 | tf_op jit(solution)/shard_map/ppermute | solution.py:12
  26.5 3.1 %collective-permute-start.3 = (f32[1,128,128]{2,1,0:T(8,128)S(1)}, f32[1,128,128]{2,1,0:T(8,128)S(1)}, u32[]{:S(2)}, u32[]{:S(2)}) collective-permute-start(f32[1,128,128]{2,1,0:T(8,128)S(1)} %slice.12), channel_id=1, source_target_pairs={{0,56},{8,0},{16,8},{24,16},{32,24},{40,32},{48,40},{56,48},{1,57}... | collective-permute-start | bytes 196616 | tf_op jit(solution)/shard_map/ppermute | solution.py:12
  29.7 0.1 collective-permute-start.7
  29.8 1.2 %collective-permute-done.3 = f32[1,128,128]{2,1,0:T(8,128)S(1)} collective-permute-done((f32[1,128,128]{2,1,0:T(8,128)S(1)}, f32[1,128,128]{2,1,0:T(8,128)S(1)}, u32[]{:S(2)}, u32[]{:S(2)}) %collective-permute-start.3) | collective-permute-done | bytes 65568 | tf_op jit(solution)/shard_map/ppermute | solution.py:12
  31.0 3.1 %collective-permute-done.7 = f32[1,128,128]{2,1,0:T(8,128)S(1)} collective-permute-done((f32[1,128,128]{2,1,0:T(8,128)S(1)}, f32[1,128,128]{2,1,0:T(8,128)S(1)}, u32[]{:S(2)}, u32[]{:S(2)}) %collective-permute-start.7) | collective-permute-done | bytes 65568 | tf_op jit(solution)/shard_map/ppermute | solution.py:12
  34.1 1.0 copy-done
  35.1 0.0 reduce-scatter.2.cloned.1.call-start
  35.8 1.9 %copy.20 = f32[1152,1,256]{0,2,1:T(8,128)S(1)} copy(f32[1152,1,256]{2,1,0:T(1,128)S(1)} %copy-done.1) | data formatting | bytes 2359296 | tf_op args[0]
  37.8 0.1 broadcast_select_fusion
  37.9 12.4 %fusion.2 = f32[4608,1,256]{0,2,1:T(8,128)} fusion(bf16[1,4608,1152]{2,1,0:T(8,128)(2,1)} %param.6, f32[1152,1,256]{0,2,1:T(8,128)S(1)} %broadcast_select_fusion), kind=kOutput, calls=%fused_computation.4 | convolution fusion | flops 2718203904 | bytes 16515072 | tf_op jit(solution)/shard_map/crk,kch->rch/dot_general | solution.py:50
  50.3 37.8 %all-gather.3.cloned.1.call-done = f32[32,2,128,128]{3,2,1,0:T(8,128)} async-done(((f32[8,2,128,128]{3,2,1,0:T(8,128)}), f32[32,2,128,128]{3,2,1,0:T(8,128)}) %all-gather.3.cloned.1.call-update) | async-done | bytes 4194320 | tf_op jit(solution)/shard_map/all_gather | solution.py:41
  88.1 0.7 collective-permute-start.8
  88.8 0.4 copy.23
  89.2 0.3 copy-done.2
  89.5 0.1 copy.22
  89.6 0.1 reshape.47
  89.7 0.6 reshape.43
  90.4 0.1 copy.21
  90.5 2.9 %gather_fusion = f32[36,128,128]{2,1,0:T(8,128)S(1)} fusion(f32[64,128,128]{2,1,0:T(8,128)} %bitcast.49, s32[1024]{0:T(1024)S(1)} %pad_clamp_fusion), kind=kCustom, calls=%fused_computation | custom fusion | bytes 4718736 | tf_op jit(solution)/shard_map/gather | solution.py:61
  93.4 2.6 %collective-permute-done.8 = f32[64,128,128]{2,1,0:T(8,128)} collective-permute-done((f32[64,128,128]{2,1,0:T(8,128)}, f32[64,128,128]{2,1,0:T(8,128)}, u32[]{:S(2)}, u32[]{:S(2)}) %collective-permute-start.8) | collective-permute-done | bytes 4194336 | tf_op jit(solution)/shard_map/ppermute | solution.py:12
  95.9 4.4 %gather_fusion.1 = f32[36,128,128]{2,1,0:T(8,128)} fusion(f32[64,128,128]{2,1,0:T(8,128)} %collective-permute-done.8, s32[1024]{0:T(1024)S(1)} %pad_clamp_fusion), kind=kCustom, calls=%fused_computation.1 | custom fusion | bytes 4718736 | tf_op jit(solution)/shard_map/gather | solution.py:61
  100.3 4.0 %fusion.7 = f32[18,64,1,2,128]{4,1,3,0,2:T(8,128)S(1)} fusion(f32[18,2,128,128]{3,2,1,0:T(8,128)S(1)} %bitcast.45, f32[18,2,128,128]{3,2,1,0:T(8,128)} %bitcast.46, f32[18,64,2,128]{3,2,1,0:T(2,128)S(1)} %reshape.43, pred[18,2]{1,0:T(8,128)(4,1)S(1)} %copy.21), kind=kOutput, calls=%fused_computation.7 | convolution fusion | flops 453574656 | bytes 7077924 | tf_op jit(solution)/shard_map/rschk,rchkl->rschl/dot_general | solution.py:62
  104.3 0.9 copy.25
  105.2 1.9 %copy.26 = f32[1152,1,256]{0,2,1:T(8,128)S(1)} copy(f32[1152,1,256]{2,1,0:T(1,128)S(1)} %bitcast.47) | data formatting | bytes 2359296 | tf_op jit(solution)/shard_map/reshape | solution.py:64
  107.2 1.4 %select_add_fusion = f32[1152,1,256]{0,2,1:T(8,128)S(1)} fusion(f32[1152,1,256]{0,2,1:T(8,128)S(1)} %copy.26, f32[1152,1,256]{0,2,1:T(8,128)} %reduce-scatter.2.cloned.1.call-done, pred[1152]{0:T(1024)(128)(4,1)S(1)} %add_compare_fusion), kind=kLoop, calls=%fused_computation.9 | loop fusion | flops 589824 | bytes 3540096 | tf_op jit(solution)/shard_map/add | solution.py:65
  108.6 2.1 %copy.27 = f32[1152,1,256]{2,1,0:T(1,128)} copy(f32[1152,1,256]{0,2,1:T(8,128)S(1)} %select_add_fusion) | data formatting | bytes 2359296 | tf_op jit(solution)/shard_map/add | solution.py:65
  (27 shorter events, 0.2 us)
Async XLA Ops:
  7.4 80.8 %all-gather.3.cloned.1.call-start = ((), (), s32[]{:S(2)}) async-start(), calls=%async_computation.2 | async-start | bytes 5242880 | tf_op jit(solution)/shard_map/all_gather | solution.py:41
  7.4 8.9 %collective-permute-start = (f32[2,128,128]{2,1,0:T(8,128)}, f32[2,128,128]{2,1,0:T(8,128)S(1)}, u32[]{:S(2)}, u32[]{:S(2)}) collective-permute-start(f32[2,128,128]{2,1,0:T(8,128)} %param.7), channel_id=1, source_target_pairs={{0,56},{8,0},{16,8},{24,16},{32,24},{40,32},{48,40},{56,48},{1,57}... | collective-permute-start | bytes 393224 | tf_op jit(solution)/shard_map/ppermute | solution.py:12
  13.8 5.8 %collective-permute-start.4 = (f32[2,128,128]{2,1,0:T(8,128)}, f32[2,128,128]{2,1,0:T(8,128)S(1)}, u32[]{:S(2)}, u32[]{:S(2)}) collective-permute-start(f32[2,128,128]{2,1,0:T(8,128)} %param.7), channel_id=1, source_target_pairs={{0,8},{8,16},{16,24},{24,32},{32,40},{40,48},{48,56},{56,0},{1,9},... | collective-permute-start | bytes 393224 | tf_op jit(solution)/shard_map/ppermute | solution.py:12
  16.3 5.3 %collective-permute-start.1 = (f32[2,128,128]{2,1,0:T(8,128)S(1)}, f32[2,128,128]{2,1,0:T(8,128)S(1)}, u32[]{:S(2)}, u32[]{:S(2)}) collective-permute-start(f32[2,128,128]{2,1,0:T(8,128)S(1)} %collective-permute-done), channel_id=1, source_target_pairs={{0,56},{8,0},{16,8},{24,16},{32,24},{40,32},{48,40},{56,48},{1,57}... | collective-permute-start | bytes 393224 | tf_op jit(solution)/shard_map/ppermute | solution.py:12
  19.6 5.0 %collective-permute-start.5 = (f32[2,128,128]{2,1,0:T(8,128)S(1)}, f32[2,128,128]{2,1,0:T(8,128)S(1)}, u32[]{:S(2)}, u32[]{:S(2)}) collective-permute-start(f32[2,128,128]{2,1,0:T(8,128)S(1)} %collective-permute-done.4), channel_id=1, source_target_pairs={{0,8},{8,16},{16,24},{24,32},{32,40},{40,48},{48,56},{56,0},{1,9},... | collective-permute-start | bytes 393224 | tf_op jit(solution)/shard_map/ppermute | solution.py:12
  21.5 5.0 %collective-permute-start.2 = (f32[2,128,128]{2,1,0:T(8,128)S(1)}, f32[2,128,128]{2,1,0:T(8,128)S(1)}, u32[]{:S(2)}, u32[]{:S(2)}) collective-permute-start(f32[2,128,128]{2,1,0:T(8,128)S(1)} %collective-permute-done.1), channel_id=1, source_target_pairs={{0,56},{8,0},{16,8},{24,16},{32,24},{40,32},{48,40},{56,48},{1,57}... | collective-permute-start | bytes 393224 | tf_op jit(solution)/shard_map/ppermute | solution.py:12
  24.6 5.0 %collective-permute-start.6 = (f32[2,128,128]{2,1,0:T(8,128)S(1)}, f32[2,128,128]{2,1,0:T(8,128)S(1)}, u32[]{:S(2)}, u32[]{:S(2)}) collective-permute-start(f32[2,128,128]{2,1,0:T(8,128)S(1)} %collective-permute-done.5), channel_id=1, source_target_pairs={{0,8},{8,16},{16,24},{24,32},{32,40},{40,48},{48,56},{56,0},{1,9},... | collective-permute-start | bytes 393224 | tf_op jit(solution)/shard_map/ppermute | solution.py:12
  26.5 4.4 %collective-permute-start.3 = (f32[1,128,128]{2,1,0:T(8,128)S(1)}, f32[1,128,128]{2,1,0:T(8,128)S(1)}, u32[]{:S(2)}, u32[]{:S(2)}) collective-permute-start(f32[1,128,128]{2,1,0:T(8,128)S(1)} %slice.12), channel_id=1, source_target_pairs={{0,56},{8,0},{16,8},{24,16},{32,24},{40,32},{48,40},{56,48},{1,57}... | collective-permute-start | bytes 196616 | tf_op jit(solution)/shard_map/ppermute | solution.py:12
  29.6 6.2 %copy-start.1 = (f32[1152,1,256]{2,1,0:T(1,128)S(1)}, f32[1152,1,256]{2,1,0:T(1,128)}, u32[]{:S(2)}) copy-start(f32[1152,1,256]{2,1,0:T(1,128)} %param.5) | copy-start | bytes 3538948
  29.7 4.4 %collective-permute-start.7 = (f32[1,128,128]{2,1,0:T(8,128)S(1)}, f32[1,128,128]{2,1,0:T(8,128)S(1)}, u32[]{:S(2)}, u32[]{:S(2)}) collective-permute-start(f32[1,128,128]{2,1,0:T(8,128)S(1)} %slice.13), channel_id=1, source_target_pairs={{0,8},{8,16},{16,24},{24,32},{32,40},{40,48},{48,56},{56,0},{1,9},... | collective-permute-start | bytes 196616 | tf_op jit(solution)/shard_map/ppermute | solution.py:12
  34.1 1.0 copy-start
  35.1 72.1 %reduce-scatter.2.cloned.1.call-start = ((), (), s32[]{:S(2)}) async-start(), calls=%async_computation.1 | async-start | bytes 5898240 | tf_op jit(solution)/shard_map/reduce_scatter | solution.py:49
  88.1 7.8 %collective-permute-start.8 = (f32[64,128,128]{2,1,0:T(8,128)}, f32[64,128,128]{2,1,0:T(8,128)}, u32[]{:S(2)}, u32[]{:S(2)}) collective-permute-start(f32[64,128,128]{2,1,0:T(8,128)} %bitcast.48), channel_id=1, source_target_pairs={{0,4},{4,0},{1,5},{5,1},{2,6},{6,2},{3,7},{7,3},{8,12},{12,8},{9,1... | collective-permute-start | bytes 12582920 | tf_op jit(solution)/shard_map/ppermute | solution.py:12
  88.8 0.7 copy-start.2
Sparse Core Ops, SparseCore 0:
  35.2 52.8 all-gather.2
Sparse Core Ops, SparseCore 1:
  50.4 55.5 reduce-scatter.1

commit v5 on v4

--- a/solution.py
+++ b/solution.py
@@ -30,6 +30,11 @@
     return jnp.stack(pieces, axis=0)
 
 
+def direct_gather(x, axis):
+    n = lax.axis_size(axis)
+    return jnp.stack([x] + [shift(x, axis, -o) for o in range(1, n)], axis=0)
+
+
 def local(amplitudes, pair_interaction, ph_interaction, pp_size, ph_owner):
     row_count, chan_count, hole_width = amplitudes.shape
     row_tiles, _, col_tiles = ph_owner.shape
@@ -37,7 +42,7 @@
     tile_cols = hole_width // col_tiles
     per_dev = ph_interaction.shape[0]
     ny, nz, nc = lax.axis_size("cy"), lax.axis_size("cz"), lax.axis_size("core")
-    by_z = ring_gather(ph_interaction, "cz")
+    by_z = direct_gather(ph_interaction, "cz")
     own = lax.all_gather(by_z, "cy", axis=0, tiled=False)
     own = own.reshape((-1,) + ph_interaction.shape[1:])
     sibling = shift(own, "core", 1)

time: 118 us -> 124 us (1.051)
  waiting for transfers between devices: 50.1 us -> 56.7 us
    ppermute x9 -> x8, waiting for transfers between devices: 12.2 us -> 23 us  [shift(): return lax.ppermute(x, axis, [(k, (k + step) % n) for k in range(n)])]
    all_gather x1, waiting for transfers between devices: 37.8 us -> 33.7 us  [local(): own = lax.all_gather(by_z, 'cy', axis=0, tiled=False)]
    ppermute x9 -> x8, starting transfers between devices: 16.6 us -> 16.1 us  [shift(): return lax.ppermute(x, axis, [(k, (k + step) % n) for k in range(n)])]
    unnamed x13 -> x14, local copies, waits for them, and re-layouts: 4.26 us -> 4.26 us
  transfers between devices with their start and end apart: 11 -> 10, of which waited for: 7 -> 8; matrix products, arithmetic and copies ran while one was open for 26% -> 25% of each run, Pallas kernels for 0% -> 0%
where the time goes in v5:
time: 124 us
  waiting for transfers between devices  56.7 us (46%)
  local copies, waits for them, and re-layouts  17.8 us (14%)
  matrix products  16.3 us (13%)
  starting transfers between devices  16.1 us (13%)
  between operations  15.7 us (13%)
  other arithmetic  1.55 us (1%)
    all_gather x1, waiting for transfers between devices, local(): own = lax.all_gather(by_z, 'cy', axis=0, tiled=False)  33.7 us
    ppermute x8, waiting for transfers between devices, shift(): return lax.ppermute(x, axis, [(k, (k + step) % n) for k in range(n)])  23 us
    ppermute x8, starting transfers between devices, shift(): return lax.ppermute(x, axis, [(k, (k + step) % n) for k in range(n)])  16.1 us
    dot_general x1, matrix products, local(): jnp.einsum('crk,kch->rch', pair_interaction, lowered, preferred_element_t...  12.4 us
    gather x2, local copies, waits for them, and re-layouts, local(): chosen = jnp.where((o_c == 0)[..., None, None], own[slot], sibling[slot])  7.26 us
    unnamed x14, local copies, waits for them, and re-layouts  4.26 us
    dot_general x1, matrix products, local(): jnp.einsum('rschk,rchkl->rschl', blocks, chosen, precision=lax.Precision....  3.99 us
  transfers between devices with their start and end apart: 10, of which 8 were waited for; matrix products, arithmetic and copies ran while one was open for 25% of the time, Pallas kernels for 0%

profile of v5, /device:TPU:1, one launch (start us, length us, event | category | flops | bytes accessed | tf_op | source)
XLA Modules:
  0.0 124.2 jit_solution(5851465566149882168)
XLA Ops:
  7.4 6.4 %collective-permute-start = (f32[2,128,128]{2,1,0:T(8,128)}, f32[2,128,128]{2,1,0:T(8,128)S(1)}, u32[]{:S(2)}, u32[]{:S(2)}) collective-permute-start(f32[2,128,128]{2,1,0:T(8,128)} %param.7), channel_id=1, source_target_pairs={{0,56},{8,0},{16,8},{24,16},{32,24},{40,32},{48,40},{56,48},{1,57}... | collective-permute-start | bytes 393224 | tf_op jit(solution)/shard_map/ppermute | solution.py:12
  13.8 1.2 collective-permute-start.1
  14.9 0.4 collective-permute-start.2
  15.4 4.5 %collective-permute-start.3 = (f32[2,128,128]{2,1,0:T(8,128)}, f32[2,128,128]{2,1,0:T(8,128)S(1)}, u32[]{:S(2)}, u32[]{:S(2)}) collective-permute-start(f32[2,128,128]{2,1,0:T(8,128)} %param.7), channel_id=1, source_target_pairs={{0,32},{8,40},{16,48},{24,56},{32,0},{40,8},{48,16},{56,24},{1,33}... | collective-permute-start | bytes 393224 | tf_op jit(solution)/shard_map/ppermute | solution.py:12
  19.9 1.0 bitcast_dynamic-update-slice_fusion.7
  20.9 2.1 %collective-permute-start.5 = (f32[2,128,128]{2,1,0:T(8,128)}, f32[2,128,128]{2,1,0:T(8,128)S(1)}, u32[]{:S(2)}, u32[]{:S(2)}) collective-permute-start(f32[2,128,128]{2,1,0:T(8,128)} %param.7), channel_id=1, source_target_pairs={{0,16},{8,24},{16,32},{24,40},{32,48},{40,56},{48,0},{56,8},{1,17}... | collective-permute-start | bytes 393224 | tf_op jit(solution)/shard_map/ppermute | solution.py:12
  23.0 0.7 collective-permute-done.1
  23.8 0.8 collective-permute-start.6
  24.6 2.2 %collective-permute-done.2 = f32[2,128,128]{2,1,0:T(8,128)S(1)} collective-permute-done((f32[2,128,128]{2,1,0:T(8,128)}, f32[2,128,128]{2,1,0:T(8,128)S(1)}, u32[]{:S(2)}, u32[]{:S(2)}) %collective-permute-start.2) | collective-permute-done | bytes 131104 | tf_op jit(solution)/shard_map/ppermute | solution.py:12
  26.8 2.6 %collective-permute-done.3 = f32[2,128,128]{2,1,0:T(8,128)S(1)} collective-permute-done((f32[2,128,128]{2,1,0:T(8,128)}, f32[2,128,128]{2,1,0:T(8,128)S(1)}, u32[]{:S(2)}, u32[]{:S(2)}) %collective-permute-start.3) | collective-permute-done | bytes 131104 | tf_op jit(solution)/shard_map/ppermute | solution.py:12
  29.4 1.0 collective-permute-done.4
  30.3 8.3 %collective-permute-done.5 = f32[2,128,128]{2,1,0:T(8,128)S(1)} collective-permute-done((f32[2,128,128]{2,1,0:T(8,128)}, f32[2,128,128]{2,1,0:T(8,128)S(1)}, u32[]{:S(2)}, u32[]{:S(2)}) %collective-permute-start.5) | collective-permute-done | bytes 131104 | tf_op jit(solution)/shard_map/ppermute | solution.py:12
  38.6 5.6 %collective-permute-done.6 = f32[2,128,128]{2,1,0:T(8,128)S(1)} collective-permute-done((f32[2,128,128]{2,1,0:T(8,128)}, f32[2,128,128]{2,1,0:T(8,128)S(1)}, u32[]{:S(2)}, u32[]{:S(2)}) %collective-permute-start.6) | collective-permute-done | bytes 131104 | tf_op jit(solution)/shard_map/ppermute | solution.py:12
  44.3 1.0 copy-done
  46.0 1.9 %copy.20 = f32[1152,1,256]{0,2,1:T(8,128)S(1)} copy(f32[1152,1,256]{2,1,0:T(1,128)S(1)} %copy-done.1) | data formatting | bytes 2359296 | tf_op args[0]
  48.1 12.4 %fusion.2 = f32[4608,1,256]{0,2,1:T(8,128)} fusion(bf16[1,4608,1152]{2,1,0:T(8,128)(2,1)} %param.6, f32[1152,1,256]{0,2,1:T(8,128)S(1)} %broadcast_select_fusion), kind=kOutput, calls=%fused_computation.4 | convolution fusion | flops 2718203904 | bytes 16515072 | tf_op jit(solution)/shard_map/crk,kch->rch/dot_general | solution.py:55
  60.5 33.7 %all-gather.3.cloned.1.call-done = f32[32,2,128,128]{3,2,1,0:T(8,128)} async-done(((f32[8,2,128,128]{3,2,1,0:T(8,128)}), f32[32,2,128,128]{3,2,1,0:T(8,128)}) %all-gather.3.cloned.1.call-update) | async-done | bytes 4194320 | tf_op jit(solution)/shard_map/all_gather | solution.py:46
  94.2 0.7 collective-permute-start.7
  94.8 0.4 copy.23
  95.2 0.3 copy-done.2
  95.6 0.1 copy.22
  95.7 0.1 reshape.47
  95.8 0.6 reshape.43
  96.4 0.1 copy.21
  96.5 2.9 %gather_fusion = f32[36,128,128]{2,1,0:T(8,128)S(1)} fusion(f32[64,128,128]{2,1,0:T(8,128)} %bitcast.47, s32[1024]{0:T(1024)S(1)} %pad_clamp_fusion), kind=kCustom, calls=%fused_computation | custom fusion | bytes 4718736 | tf_op jit(solution)/shard_map/gather | solution.py:66
  99.4 2.6 %collective-permute-done.7 = f32[64,128,128]{2,1,0:T(8,128)} collective-permute-done((f32[64,128,128]{2,1,0:T(8,128)}, f32[64,128,128]{2,1,0:T(8,128)}, u32[]{:S(2)}, u32[]{:S(2)}) %collective-permute-start.7) | collective-permute-done | bytes 4194336 | tf_op jit(solution)/shard_map/ppermute | solution.py:12
  102.0 4.4 %gather_fusion.1 = f32[36,128,128]{2,1,0:T(8,128)} fusion(f32[64,128,128]{2,1,0:T(8,128)} %collective-permute-done.7, s32[1024]{0:T(1024)S(1)} %pad_clamp_fusion), kind=kCustom, calls=%fused_computation.1 | custom fusion | bytes 4718736 | tf_op jit(solution)/shard_map/gather | solution.py:66
  106.3 4.0 %fusion.7 = f32[18,64,1,2,128]{4,1,3,0,2:T(8,128)S(1)} fusion(f32[18,2,128,128]{3,2,1,0:T(8,128)S(1)} %bitcast.43, f32[18,2,128,128]{3,2,1,0:T(8,128)} %bitcast.44, f32[18,64,2,128]{3,2,1,0:T(2,128)S(1)} %reshape.43, pred[18,2]{1,0:T(8,128)(4,1)S(1)} %copy.21), kind=kOutput, calls=%fused_computation.7 | convolution fusion | flops 453574656 | bytes 7077924 | tf_op jit(solution)/shard_map/rschk,rchkl->rschl/dot_general | solution.py:67
  110.3 0.9 copy.25
  111.3 1.9 %copy.26 = f32[1152,1,256]{0,2,1:T(8,128)S(1)} copy(f32[1152,1,256]{2,1,0:T(1,128)S(1)} %bitcast.45) | data formatting | bytes 2359296 | tf_op jit(solution)/shard_map/reshape | solution.py:69
  113.2 1.4 %select_add_fusion = f32[1152,1,256]{0,2,1:T(8,128)S(1)} fusion(f32[1152,1,256]{0,2,1:T(8,128)S(1)} %copy.26, f32[1152,1,256]{0,2,1:T(8,128)} %reduce-scatter.2.cloned.1.call-done, pred[1152]{0:T(1024)(128)(4,1)S(1)} %add_compare_fusion), kind=kLoop, calls=%fused_computation.9 | loop fusion | flops 589824 | bytes 3540096 | tf_op jit(solution)/shard_map/add | solution.py:70
  114.6 2.1 %copy.27 = f32[1152,1,256]{2,1,0:T(1,128)} copy(f32[1152,1,256]{0,2,1:T(8,128)S(1)} %select_add_fusion) | data formatting | bytes 2359296 | tf_op jit(solution)/shard_map/add | solution.py:70
  (23 shorter events, 0.3 us)
Async XLA Ops:
  7.4 86.8 %all-gather.3.cloned.1.call-start = ((), (), s32[]{:S(2)}) async-start(), calls=%async_computation.2 | async-start | bytes 5242880 | tf_op jit(solution)/shard_map/all_gather | solution.py:46
  7.4 13.5 %collective-permute-start = (f32[2,128,128]{2,1,0:T(8,128)}, f32[2,128,128]{2,1,0:T(8,128)S(1)}, u32[]{:S(2)}, u32[]{:S(2)}) collective-permute-start(f32[2,128,128]{2,1,0:T(8,128)} %param.7), channel_id=1, source_target_pairs={{0,56},{8,0},{16,8},{24,16},{32,24},{40,32},{48,40},{56,48},{1,57}... | collective-permute-start | bytes 393224 | tf_op jit(solution)/shard_map/ppermute | solution.py:12
  13.8 10.0 %collective-permute-start.1 = (f32[2,128,128]{2,1,0:T(8,128)}, f32[2,128,128]{2,1,0:T(8,128)S(1)}, u32[]{:S(2)}, u32[]{:S(2)}) collective-permute-start(f32[2,128,128]{2,1,0:T(8,128)} %param.7), channel_id=1, source_target_pairs={{0,48},{8,56},{16,0},{24,8},{32,16},{40,24},{48,32},{56,40},{1,49}... | collective-permute-start | bytes 393224 | tf_op jit(solution)/shard_map/ppermute | solution.py:12
  14.9 11.8 %collective-permute-start.2 = (f32[2,128,128]{2,1,0:T(8,128)}, f32[2,128,128]{2,1,0:T(8,128)S(1)}, u32[]{:S(2)}, u32[]{:S(2)}) collective-permute-start(f32[2,128,128]{2,1,0:T(8,128)} %param.7), channel_id=1, source_target_pairs={{0,40},{8,48},{16,56},{24,0},{32,8},{40,16},{48,24},{56,32},{1,41}... | collective-permute-start | bytes 393224 | tf_op jit(solution)/shard_map/ppermute | solution.py:12
  15.4 13.9 %collective-permute-start.3 = (f32[2,128,128]{2,1,0:T(8,128)}, f32[2,128,128]{2,1,0:T(8,128)S(1)}, u32[]{:S(2)}, u32[]{:S(2)}) collective-permute-start(f32[2,128,128]{2,1,0:T(8,128)} %param.7), channel_id=1, source_target_pairs={{0,32},{8,40},{16,48},{24,56},{32,0},{40,8},{48,16},{56,24},{1,33}... | collective-permute-start | bytes 393224 | tf_op jit(solution)/shard_map/ppermute | solution.py:12
  19.9 10.4 %collective-permute-start.4 = (f32[2,128,128]{2,1,0:T(8,128)}, f32[2,128,128]{2,1,0:T(8,128)S(1)}, u32[]{:S(2)}, u32[]{:S(2)}) collective-permute-start(f32[2,128,128]{2,1,0:T(8,128)} %param.7), channel_id=1, source_target_pairs={{0,24},{8,32},{16,40},{24,48},{32,56},{40,0},{48,8},{56,16},{1,25}... | collective-permute-start | bytes 393224 | tf_op jit(solution)/shard_map/ppermute | solution.py:12
  20.9 17.8 %collective-permute-start.5 = (f32[2,128,128]{2,1,0:T(8,128)}, f32[2,128,128]{2,1,0:T(8,128)S(1)}, u32[]{:S(2)}, u32[]{:S(2)}) collective-permute-start(f32[2,128,128]{2,1,0:T(8,128)} %param.7), channel_id=1, source_target_pairs={{0,16},{8,24},{16,32},{24,40},{32,48},{40,56},{48,0},{56,8},{1,17}... | collective-permute-start | bytes 393224 | tf_op jit(solution)/shard_map/ppermute | solution.py:12
  23.8 20.5 %collective-permute-start.6 = (f32[2,128,128]{2,1,0:T(8,128)}, f32[2,128,128]{2,1,0:T(8,128)S(1)}, u32[]{:S(2)}, u32[]{:S(2)}) collective-permute-start(f32[2,128,128]{2,1,0:T(8,128)} %param.7), channel_id=1, source_target_pairs={{0,8},{8,16},{16,24},{24,32},{32,40},{40,48},{48,56},{56,0},{1,9},... | collective-permute-start | bytes 393224 | tf_op jit(solution)/shard_map/ppermute | solution.py:12
  24.6 21.4 %copy-start.1 = (f32[1152,1,256]{2,1,0:T(1,128)S(1)}, f32[1152,1,256]{2,1,0:T(1,128)}, u32[]{:S(2)}) copy-start(f32[1152,1,256]{2,1,0:T(1,128)} %param.5) | copy-start | bytes 3538948
  44.3 1.0 copy-start
  45.3 67.9 %reduce-scatter.2.cloned.1.call-start = ((), (), s32[]{:S(2)}) async-start(), calls=%async_computation.1 | async-start | bytes 5898240 | tf_op jit(solution)/shard_map/reduce_scatter | solution.py:54
  94.2 7.8 %collective-permute-start.7 = (f32[64,128,128]{2,1,0:T(8,128)}, f32[64,128,128]{2,1,0:T(8,128)}, u32[]{:S(2)}, u32[]{:S(2)}) collective-permute-start(f32[64,128,128]{2,1,0:T(8,128)} %bitcast.46), channel_id=1, source_target_pairs={{0,4},{4,0},{1,5},{5,1},{2,6},{6,2},{3,7},{7,3},{8,12},{12,8},{9,1... | collective-permute-start | bytes 12582920 | tf_op jit(solution)/shard_map/ppermute | solution.py:12
  94.8 0.7 copy-start.2
Sparse Core Ops, SparseCore 0:
  45.4 48.6 all-gather.2
Sparse Core Ops, SparseCore 1:
  60.5 51.3 reduce-scatter.1

commit v6 on v1

v6 whole, which is shorter than its diff:
```python
import jax
import jax.numpy as jnp
from jax import lax
from jax.sharding import PartitionSpec as P


def local(amplitudes, pair_interaction, ph_interaction, pp_size, ph_owner):
    row_count, chan_count, hole_width = amplitudes.shape
    row_tiles, _, col_tiles = ph_owner.shape
    tile_rows = row_count // row_tiles
    tile_cols = hole_width // col_tiles
    ph_all = lax.all_gather(ph_interaction, "chan", axis=0, tiled=True)
    offset = lax.axis_index("ctr") * row_count
    positions = offset + jnp.arange(row_count, dtype=jnp.int32)
    live = (positions < pp_size[0] * tile_rows)[:, None]
    flat = amplitudes.reshape(row_count, hole_width)
    masked = jnp.where(live, flat, jnp.zeros_like(flat))
    lowered = masked.astype(jnp.bfloat16)
    ladder = lax.psum_scatter(
        jnp.dot(pair_interaction[0], lowered, preferred_element_type=jnp.float32),
        "ctr",
        scatter_dimension=0,
        tiled=True,
    )
    blocks = masked.reshape(row_tiles, tile_rows, col_tiles, tile_cols)
    chosen = ph_all[ph_owner[:, 0, :]]
    ladder = jnp.where(live, ladder, jnp.zeros_like(ladder))
    ladder = ladder.reshape(row_tiles, tile_rows, col_tiles, tile_cols)
    residual = ladder + jnp.einsum(
        "rshk,rhkl->rshl", blocks, chosen, precision=lax.Precision.HIGHEST
    )
    return residual.reshape(row_count, chan_count, hole_width)


def solution(mesh):
    in_specs = (
        P("ctr", "chan", None),
        P("chan", None, "ctr"),
        P("chan", None, None),
        P("chan"),
        P("ctr", "chan", None),
    )
    out_specs = P("ctr", "chan", None)
    return jax.shard_map(local, mesh=mesh, in_specs=in_specs, out_specs=out_specs, check_vma=False)
```

time: 119 us -> 135 us (1.13)
  waiting for transfers between devices: 73.6 us -> 88.2 us
  local copies, waits for them, and re-layouts: 13.1 us -> 7.25 us
  other arithmetic: 1.5 us -> 6.99 us
  matrix products: 14.6 us -> 16.2 us
    reduce_scatter x1, waiting for transfers between devices: 0.03 us -> 56.7 us  [local(): lax.psum_scatter(jnp.dot(pair_interaction[0], lowered, preferred_element_...]
    all_gather x1, waiting for transfers between devices: 72.8 us -> 30.9 us  [local(): ph_all = lax.all_gather(ph_interaction, 'chan', axis=0, tiled=True)]
    convert_element_type x0 -> x1, other arithmetic: none -> 5.61 us  [local(): lowered = masked.astype(jnp.bfloat16)]
    unnamed x3 -> x2, local copies, waits for them, and re-layouts: 2.91 us -> 0.07 us
    dot_general x2, matrix products: 14.6 us -> 16.2 us  [the longest x1 12.6 us: local(): jnp.dot(pair_interaction[0], lowered, preferred_element_type=jnp.float32)]
    add x1 -> x0, other arithmetic: 1.4 us -> none  [local(): jnp.where(live_mask[:, :, None], ladder, jnp.zeros_like(ladder)) + cycle]
  transfers between devices with their start and end apart: 2 -> 2, of which waited for: 1 -> 2; matrix products, arithmetic and copies ran while one was open for 21% -> 2% of each run, Pallas kernels for 0% -> 0%
where the time goes in v6:
time: 135 us; the launch traced here: 134 us
  waiting for transfers between devices  88.2 us (65%)
  matrix products  16.2 us (12%)
  between operations  15.6 us (12%)
  local copies, waits for them, and re-layouts  7.25 us (5%)
  other arithmetic  6.99 us (5%)
    reduce_scatter x1, waiting for transfers between devices, local(): lax.psum_scatter(jnp.dot(pair_interaction[0], lowered, preferred_element_...  56.7 us
    all_gather x1, waiting for transfers between devices, local(): ph_all = lax.all_gather(ph_interaction, 'chan', axis=0, tiled=True)  30.9 us
    dot_general x1, matrix products, local(): jnp.dot(pair_interaction[0], lowered, preferred_element_type=jnp.float32)  12.6 us
    convert_element_type x1, other arithmetic, local(): lowered = masked.astype(jnp.bfloat16)  5.61 us
    gather x1, local copies, waits for them, and re-layouts, local(): chosen = ph_all[ph_owner[:, 0, :]]  4.08 us
    dot_general x1, matrix products, local(): jnp.einsum('rshk,rhkl->rshl', blocks, chosen, precision=lax.Precision.HIG...  3.55 us
  transfers between devices with their start and end apart: 2, of which 2 were waited for; matrix products, arithmetic and copies ran while one was open for 2% of the time, Pallas kernels for 0%

profile of v6, /device:TPU:1, one launch (start us, length us, event | category | flops | bytes accessed | tf_op | source)
XLA Modules:
  0.0 134.2 jit_solution(2204641694285079015)
XLA Ops:
  7.4 0.0 reduce-scatter.2.cloned.1.call-start
  8.0 5.6 %fusion.6 = bf16[1152,1,256]{2,1,0:T(2,128)(2,1)S(1)} fusion(f32[1152,1,256]{2,1,0:T(1,128)} %param.5, pred[1152]{0:T(1024)(128)(4,1)S(1)} %add_compare_fusion.1), kind=kLoop, calls=%fused_computation.8 | loop fusion | flops 294912 | bytes 1770624 | tf_op jit(solution)/shard_map/convert_element_type | solution.py:18
  13.7 12.6 %fusion.2 = f32[4608,256]{0,1:T(8,128)} fusion(bf16[1,4608,1152]{2,1,0:T(8,128)(2,1)} %param.6, bf16[1152,1,256]{2,1,0:T(2,128)(2,1)S(1)} %fusion.6), kind=kOutput, calls=%fused_computation.3 | convolution fusion | flops 2717908992 | bytes 15925248 | tf_op jit(solution)/shard_map/dot_general | solution.py:20
  26.3 0.0 copy-start
  26.3 0.0 reduce-scatter.2.cloned.1.call-update
  26.3 0.0 all-gather.2.cloned.1.call-start
  26.3 0.5 all-gather.2.cloned.1.call-update
  26.9 0.1 copy-done
  26.9 0.1 copy.16
  27.0 0.1 reshape.64
  27.2 56.7 %reduce-scatter.2.cloned.1.call-done = f32[1152,256]{0,1:T(8,128)} async-done(((f32[4608,256]{0,1:T(8,128)}), f32[1152,256]{0,1:T(8,128)}) %reduce-scatter.2.cloned.1.call-update) | async-done | bytes 1179664 | tf_op jit(solution)/shard_map/reduce_scatter | solution.py:19
  83.9 1.4 %broadcast_select_fusion.1 = f32[1152,256]{0,1:T(8,128)S(1)} fusion(f32[1152,256]{0,1:T(8,128)} %reduce-scatter.2.cloned.1.call-done, pred[1152]{0:T(1024)(128)(4,1)S(1)} %add_compare_fusion.1), kind=kLoop, calls=%fused_computation.12 | loop fusion | flops 294912 | bytes 2360448 | tf_op jit(solution)/shard_map/jit(_where)/select_n | solution.py:27
  85.3 0.4 copy.15
  85.6 0.6 reshape.59
  86.3 30.9 %all-gather.2.cloned.1.call-done = f32[128,128,128]{2,1,0:T(8,128)} async-done(((f32[2,128,128]{2,1,0:T(8,128)}), f32[128,128,128]{2,1,0:T(8,128)}) %all-gather.2.cloned.1.call-update) | async-done | bytes 8388624 | tf_op jit(solution)/shard_map/all_gather | solution.py:12
  117.2 4.1 %gather_fusion = f32[36,128,128]{2,1,0:T(8,128)S(1)} fusion(f32[128,128,128]{2,1,0:T(8,128)} %all-gather.2.cloned.1.call-done, s32[1024]{0:T(1024)S(1)} %pad_clamp_fusion), kind=kCustom, calls=%fused_computation | custom fusion | bytes 4718736 | tf_op jit(solution)/shard_map/gather | solution.py:26
  121.3 3.6 %fusion.5 = f32[18,64,2,128]{3,1,2,0:T(8,128)S(1)} fusion(f32[18,2,128,128]{3,2,1,0:T(8,128)S(1)} %bitcast.23, f32[18,64,2,128]{3,2,1,0:T(2,128)S(1)} %reshape.59, f32[18,64,2,128]{3,2,1,0:T(2,128)} %bitcast.24, pred[18,64]{1,0:T(8,128)(4,1)S(1)} %add_compare_fusion), kind=kOutput, calls=%fused_computation.6 | convolution fusion | flops 453574656 | bytes 5899392 | tf_op jit(solution)/shard_map/rshk,rhkl->rshl/dot_general | solution.py:29
  124.8 1.9 %copy.19 = f32[18,64,2,128]{3,2,1,0:T(2,128)} copy(f32[18,64,2,128]{3,1,2,0:T(8,128)S(1)} %fusion.5) | data formatting | bytes 2359296 | tf_op jit(solution)/shard_map/add | solution.py:29
  (4 shorter events, 0.0 us)
Async XLA Ops:
  7.4 76.5 %reduce-scatter.2.cloned.1.call-start = ((), (), s32[]{:S(2)}) async-start(), calls=%async_computation.1 | async-start | bytes 5898240 | tf_op jit(solution)/shard_map/reduce_scatter | solution.py:19
  26.3 0.7 copy-start
  26.3 90.9 %all-gather.2.cloned.1.call-start = ((), (), s32[]{:S(2)}) async-start(), calls=%async_computation.2 | async-start | bytes 8519680 | tf_op jit(solution)/shard_map/all_gather | solution.py:12
Sparse Core Ops, SparseCore 0:
  26.4 57.4 reduce-scatter.1
Sparse Core Ops, SparseCore 1:
  29.5 87.6 all-gather.1

commit v7 on v5

--- a/solution.py
+++ b/solution.py
@@ -42,8 +42,8 @@
     tile_cols = hole_width // col_tiles
     per_dev = ph_interaction.shape[0]
     ny, nz, nc = lax.axis_size("cy"), lax.axis_size("cz"), lax.axis_size("core")
-    by_z = direct_gather(ph_interaction, "cz")
-    own = lax.all_gather(by_z, "cy", axis=0, tiled=False)
+    by_y = lax.all_gather(ph_interaction, "cy", axis=0, tiled=False)
+    own = lax.all_gather(by_y, "cz", axis=0, tiled=False)
     own = own.reshape((-1,) + ph_interaction.shape[1:])
     sibling = shift(own, "core", 1)
     offset = lax.axis_index("ctr") * row_count
@@ -59,9 +59,9 @@
     )
     owner_dev = ph_owner // per_dev
     o_y = owner_dev // (nz * nc)
-    o_z = (owner_dev // nc % nz - lax.axis_index("cz")) % nz
+    o_z = owner_dev // nc % nz
     o_c = (owner_dev % nc - lax.axis_index("core")) % nc
-    slot = (o_y * nz + o_z) * per_dev + ph_owner % per_dev
+    slot = (o_z * ny + o_y) * per_dev + ph_owner % per_dev
     blocks = masked.reshape(row_tiles, tile_rows, chan_count, col_tiles, tile_cols)
     chosen = jnp.where((o_c == 0)[..., None, None], own[slot], sibling[slot])
     cycle = jnp.einsum(

time: 124 us -> 110 us (0.89)
  starting transfers between devices: 16.1 us -> 0.72 us
  blocking collectives: 0 us -> 13.4 us
  waiting for transfers between devices: 56.7 us -> 46.9 us
  local copies, waits for them, and re-layouts: 17.8 us -> 15.4 us
    ppermute x8 -> x1, waiting for transfers between devices: 23 us -> 2.87 us  [shift(): return lax.ppermute(x, axis, [(k, (k + step) % n) for k in range(n)])]
    ppermute x8 -> x1, starting transfers between devices: 16.1 us -> 0.68 us  [shift(): return lax.ppermute(x, axis, [(k, (k + step) % n) for k in range(n)])]
    all_gather x0 -> x1, blocking collectives: none -> 13.4 us  [local(): by_y = lax.all_gather(ph_interaction, 'cy', axis=0, tiled=False)]
    all_gather x1, waiting for transfers between devices: 33.7 us -> 43.9 us  [local(): own = lax.all_gather(by_y, 'cz', axis=0, tiled=False)]
    unnamed x14 -> x5, local copies, waits for them, and re-layouts: 4.26 us -> 1.96 us
  transfers between devices with their start and end apart: 10 -> 3, of which waited for: 8 -> 2; matrix products, arithmetic and copies ran while one was open for 25% -> 27% of each run, Pallas kernels for 0% -> 0%
where the time goes in v7:
time: 110 us
  waiting for transfers between devices  46.9 us (43%)
  matrix products  16.3 us (15%)
  between operations  15.6 us (14%)
  local copies, waits for them, and re-layouts  15.4 us (14%)
  blocking collectives  13.4 us (12%)
  other arithmetic  1.54 us (1%)
    all_gather x1, waiting for transfers between devices, local(): own = lax.all_gather(by_y, 'cz', axis=0, tiled=False)  43.9 us
    all_gather x1, blocking collectives, local(): by_y = lax.all_gather(ph_interaction, 'cy', axis=0, tiled=False)  13.4 us
    dot_general x1, matrix products, local(): jnp.einsum('crk,kch->rch', pair_interaction, lowered, preferred_element_t...  12.3 us
    gather x2, local copies, waits for them, and re-layouts, local(): chosen = jnp.where((o_c == 0)[..., None, None], own[slot], sibling[slot])  7.21 us
    dot_general x1, matrix products, local(): jnp.einsum('rschk,rchkl->rschl', blocks, chosen, precision=lax.Precision....  3.99 us
    ppermute x1, waiting for transfers between devices, shift(): return lax.ppermute(x, axis, [(k, (k + step) % n) for k in range(n)])  2.87 us
  transfers between devices with their start and end apart: 3, of which 2 were waited for; matrix products, arithmetic and copies ran while one was open for 27% of the time, Pallas kernels for 0%

profile of v7, /device:TPU:1, one launch (start us, length us, event | category | flops | bytes accessed | tf_op | source)
XLA Modules:
  0.0 109.8 jit_solution(13317419034954056674)
XLA Ops:
  7.4 0.0 copy-start
  7.4 0.0 all-gather.4.cloned.1.call-start
  7.4 13.4 %all-gather = f32[8,128,128]{2,1,0:T(8,128)} all-gather(f32[2,128,128]{2,1,0:T(8,128)} %param.7), channel_id=2, replica_groups=mesh['cy'=4,'cz'=8,'core'=2,'ctr'=4] {'cy'}, dimensions={0}, use_global_device_ids=true | all-gather | bytes 655360 | tf_op jit(solution)/shard_map/all_gather | solution.py:45
  20.7 0.0 all-gather.4.cloned.1.call-update
  20.8 0.0 reduce-scatter.2.cloned.1.call-start
  21.5 0.0 copy-done
  21.5 1.9 %copy.20 = f32[1152,1,256]{0,2,1:T(8,128)S(1)} copy(f32[1152,1,256]{2,1,0:T(1,128)S(1)} %copy-done) | data formatting | bytes 2359296 | tf_op args[0]
  23.4 0.1 broadcast_select_fusion
  23.5 12.3 %fusion.2 = f32[4608,1,256]{0,2,1:T(8,128)} fusion(bf16[1,4608,1152]{2,1,0:T(8,128)(2,1)} %param.6, f32[1152,1,256]{0,2,1:T(8,128)S(1)} %broadcast_select_fusion), kind=kOutput, calls=%fused_computation.4 | convolution fusion | flops 2718203904 | bytes 16515072 | tf_op jit(solution)/shard_map/crk,kch->rch/dot_general | solution.py:55
  35.9 0.0 reduce-scatter.2.cloned.1.call-update
  35.9 43.9 %all-gather.4.cloned.1.call-done = f32[32,2,128,128]{3,2,1,0:T(8,128)} async-done(((f32[4,2,128,128]{3,2,1,0:T(8,128)}), f32[32,2,128,128]{3,2,1,0:T(8,128)}) %all-gather.4.cloned.1.call-update) | async-done | bytes 4194320 | tf_op jit(solution)/shard_map/all_gather | solution.py:46
  79.8 0.0 copy-start.1
  79.8 0.7 collective-permute-start
  80.5 0.4 copy.23
  80.9 0.0 copy-done.1
  81.0 0.1 copy.22
  81.1 0.1 reshape.47
  81.2 0.6 reshape.43
  81.8 0.1 copy.21
  81.9 2.9 %gather_fusion = f32[36,128,128]{2,1,0:T(8,128)S(1)} fusion(f32[64,128,128]{2,1,0:T(8,128)} %bitcast.33, s32[1024]{0:T(1024)S(1)} %pad_clamp_fusion), kind=kCustom, calls=%fused_computation | custom fusion | bytes 4718736 | tf_op jit(solution)/shard_map/gather | solution.py:66
  84.8 2.9 %collective-permute-done = f32[64,128,128]{2,1,0:T(8,128)} collective-permute-done((f32[64,128,128]{2,1,0:T(8,128)}, f32[64,128,128]{2,1,0:T(8,128)}, u32[]{:S(2)}, u32[]{:S(2)}) %collective-permute-start) | collective-permute-done | bytes 4194336 | tf_op jit(solution)/shard_map/ppermute | solution.py:12
  87.7 4.3 %gather_fusion.1 = f32[36,128,128]{2,1,0:T(8,128)} fusion(f32[64,128,128]{2,1,0:T(8,128)} %collective-permute-done, s32[1024]{0:T(1024)S(1)} %pad_clamp_fusion), kind=kCustom, calls=%fused_computation.1 | custom fusion | bytes 4718736 | tf_op jit(solution)/shard_map/gather | solution.py:66
  92.0 4.0 %fusion.7 = f32[18,64,1,2,128]{4,1,3,0,2:T(8,128)S(1)} fusion(f32[18,2,128,128]{3,2,1,0:T(8,128)S(1)} %bitcast.28, f32[18,2,128,128]{3,2,1,0:T(8,128)} %bitcast.29, f32[18,64,2,128]{3,2,1,0:T(2,128)S(1)} %reshape.43, pred[18,2]{1,0:T(8,128)(4,1)S(1)} %copy.21), kind=kOutput, calls=%fused_computation.7 | convolution fusion | flops 453574656 | bytes 7077924 | tf_op jit(solution)/shard_map/rschk,rchkl->rschl/dot_general | solution.py:67
  96.0 0.9 copy.25
  96.9 1.9 %copy.26 = f32[1152,1,256]{0,2,1:T(8,128)S(1)} copy(f32[1152,1,256]{2,1,0:T(1,128)S(1)} %bitcast.30) | data formatting | bytes 2359296 | tf_op jit(solution)/shard_map/reshape | solution.py:69
  98.9 0.0 reduce-scatter.2.cloned.1.call-done
  98.9 1.4 %select_add_fusion = f32[1152,1,256]{0,2,1:T(8,128)S(1)} fusion(f32[1152,1,256]{0,2,1:T(8,128)S(1)} %copy.26, f32[1152,1,256]{0,2,1:T(8,128)} %reduce-scatter.2.cloned.1.call-done, pred[1152]{0:T(1024)(128)(4,1)S(1)} %add_compare_fusion), kind=kLoop, calls=%fused_computation.9 | loop fusion | flops 589824 | bytes 3540096 | tf_op jit(solution)/shard_map/add | solution.py:70
  100.3 2.1 %copy.27 = f32[1152,1,256]{2,1,0:T(1,128)} copy(f32[1152,1,256]{0,2,1:T(8,128)S(1)} %select_add_fusion) | data formatting | bytes 2359296 | tf_op jit(solution)/shard_map/add | solution.py:70
  (4 shorter events, 0.1 us)
Async XLA Ops:
  7.4 14.1 %copy-start = (f32[1152,1,256]{2,1,0:T(1,128)S(1)}, f32[1152,1,256]{2,1,0:T(1,128)}, u32[]{:S(2)}) copy-start(f32[1152,1,256]{2,1,0:T(1,128)} %param.5) | copy-start | bytes 3538948
  7.4 72.5 %all-gather.4.cloned.1.call-start = ((), (), s32[]{:S(2)}) async-start(), calls=%async_computation.2 | async-start | bytes 4718592 | tf_op jit(solution)/shard_map/all_gather | solution.py:46
  20.8 78.1 %reduce-scatter.2.cloned.1.call-start = ((), (), s32[]{:S(2)}) async-start(), calls=%async_computation.1 | async-start | bytes 5898240 | tf_op jit(solution)/shard_map/reduce_scatter | solution.py:54
  79.8 1.1 copy-start.1
  79.8 7.8 %collective-permute-start = (f32[64,128,128]{2,1,0:T(8,128)}, f32[64,128,128]{2,1,0:T(8,128)}, u32[]{:S(2)}, u32[]{:S(2)}) collective-permute-start(f32[64,128,128]{2,1,0:T(8,128)} %bitcast.32), channel_id=1, source_target_pairs={{0,4},{4,0},{1,5},{5,1},{2,6},{6,2},{3,7},{7,3},{8,12},{12,8},{9,1... | collective-permute-start | bytes 12582920 | tf_op jit(solution)/shard_map/ppermute | solution.py:12
Sparse Core Ops, SparseCore 0:
  20.9 58.9 all-gather.3
Sparse Core Ops, SparseCore 1:
  36.0 57.6 reduce-scatter.1

commit v8 on v7

--- a/solution.py
+++ b/solution.py
@@ -42,7 +42,7 @@
     tile_cols = hole_width // col_tiles
     per_dev = ph_interaction.shape[0]
     ny, nz, nc = lax.axis_size("cy"), lax.axis_size("cz"), lax.axis_size("core")
-    by_y = lax.all_gather(ph_interaction, "cy", axis=0, tiled=False)
+    by_y = lax.all_gather(ph_interaction, ("cy", "ctr"), axis=0, tiled=False).reshape((-1, 4) + ph_interaction.shape)[:, 0]
     own = lax.all_gather(by_y, "cz", axis=0, tiled=False)
     own = own.reshape((-1,) + ph_interaction.shape[1:])
     sibling = shift(own, "core", 1)

time: 110 us -> 151 us (1.37)
  waiting for transfers between devices: 46.9 us -> 99.2 us
  blocking collectives: 13.4 us -> 0 us
  local copies, waits for them, and re-layouts: 15.4 us -> 17.3 us
    all_gather x0 -> x1, waiting for transfers between devices: none -> 55.4 us  [local(): lax.all_gather(ph_interaction, ('cy', 'ctr'), axis=0, tiled=False)]
    all_gather x1 -> x0, blocking collectives: 13.4 us -> none  [local(): by_y = lax.all_gather(ph_interaction, 'cy', axis=0, tiled=False)]
    all_gather x1, waiting for transfers between devices: 43.9 us -> 40.1 us  [local(): own = lax.all_gather(by_y, 'cz', axis=0, tiled=False)]
    slice x0 -> x1, local copies, waits for them, and re-layouts: none -> 1.87 us  [local(): lax.all_gather(ph_interaction, ('cy', 'ctr'), axis=0, tiled=False)]
  transfers between devices with their start and end apart: 3 -> 4, of which waited for: 2 -> 3; matrix products, arithmetic and copies ran while one was open for 27% -> 20% of each run, Pallas kernels for 0% -> 0%
where the time goes in v8:
time: 151 us
  waiting for transfers between devices  99.2 us (66%)
  local copies, waits for them, and re-layouts  17.3 us (11%)
  matrix products  16.3 us (11%)
  between operations  15.6 us (10%)
  other arithmetic  1.54 us (1%)
    all_gather x1, waiting for transfers between devices, local(): lax.all_gather(ph_interaction, ('cy', 'ctr'), axis=0, tiled=False)  55.4 us
    all_gather x1, waiting for transfers between devices, local(): own = lax.all_gather(by_y, 'cz', axis=0, tiled=False)  40.1 us
    dot_general x1, matrix products, local(): jnp.einsum('crk,kch->rch', pair_interaction, lowered, preferred_element_t...  12.3 us
    gather x2, local copies, waits for them, and re-layouts, local(): chosen = jnp.where((o_c == 0)[..., None, None], own[slot], sibling[slot])  7.2 us
    dot_general x1, matrix products, local(): jnp.einsum('rschk,rchkl->rschl', blocks, chosen, precision=lax.Precision....  3.99 us
  transfers between devices with their start and end apart: 4, of which 3 were waited for; matrix products, arithmetic and copies ran while one was open for 20% of the time, Pallas kernels for 0%

profile of v8, /device:TPU:1, one launch (start us, length us, event | category | flops | bytes accessed | tf_op | source)
XLA Modules:
  0.0 150.7 jit_solution(8495077305542493040)
XLA Ops:
  7.4 0.0 copy-start
  7.4 0.0 all-gather.5.cloned.1.call-start
  7.4 0.7 all-gather.5.cloned.1.call-update
  8.1 0.0 all-gather.7.cloned.1.call-start
  8.1 55.4 %all-gather.5.cloned.1.call-done = f32[32,128,128]{2,1,0:T(8,128)} async-done(((f32[2,128,128]{2,1,0:T(8,128)}), f32[32,128,128]{2,1,0:T(8,128)}) %all-gather.5.cloned.1.call-update) | async-done | bytes 2097168 | tf_op jit(solution)/shard_map/all_gather | solution.py:45
  63.6 1.9 %slice.8 = f32[4,1,2,128,128]{4,3,2,1,0:T(8,128)} slice(f32[4,4,2,128,128]{4,3,2,1,0:T(8,128)} %bitcast.33), slice={[0:4], [0:1], [0:2], [0:128], [0:128]} | slice | bytes 1048576 | tf_op jit(solution)/shard_map/slice | solution.py:45
  65.4 0.0 all-gather.7.cloned.1.call-update
  65.5 0.0 reduce-scatter.2.cloned.1.call-start
  66.2 0.0 copy-done
  66.2 1.9 %copy.20 = f32[1152,1,256]{0,2,1:T(8,128)S(1)} copy(f32[1152,1,256]{2,1,0:T(1,128)S(1)} %copy-done) | data formatting | bytes 2359296 | tf_op args[0]
  68.2 0.1 broadcast_select_fusion
  68.2 12.3 %fusion.2 = f32[4608,1,256]{0,2,1:T(8,128)} fusion(bf16[1,4608,1152]{2,1,0:T(8,128)(2,1)} %param.6, f32[1152,1,256]{0,2,1:T(8,128)S(1)} %broadcast_select_fusion), kind=kOutput, calls=%fused_computation.4 | convolution fusion | flops 2718203904 | bytes 16515072 | tf_op jit(solution)/shard_map/crk,kch->rch/dot_general | solution.py:55
  80.6 0.0 reduce-scatter.2.cloned.1.call-update
  80.6 40.1 %all-gather.7.cloned.1.call-done = f32[32,1,2,128,128]{4,3,2,1,0:T(8,128)} async-done(((f32[4,1,2,128,128]{4,3,2,1,0:T(8,128)}), f32[32,1,2,128,128]{4,3,2,1,0:T(8,128)}) %all-gather.7.cloned.1.call-update) | async-done | bytes 4194320 | tf_op jit(solution)/shard_map/all_gather | solution.py:46
  120.7 0.0 copy-start.1
  120.7 0.7 collective-permute-start
  121.4 0.4 copy.23
  121.7 0.0 copy-done.1
  121.8 0.1 copy.22
  121.9 0.1 reshape.51
  122.0 0.6 reshape.47
  122.6 0.1 copy.21
  122.7 2.9 %gather_fusion = f32[36,128,128]{2,1,0:T(8,128)S(1)} fusion(f32[64,128,128]{2,1,0:T(8,128)} %bitcast.32, s32[1024]{0:T(1024)S(1)} %pad_clamp_fusion), kind=kCustom, calls=%fused_computation | custom fusion | bytes 4718736 | tf_op jit(solution)/shard_map/gather | solution.py:66
  125.6 2.9 %collective-permute-done = f32[64,128,128]{2,1,0:T(8,128)} collective-permute-done((f32[64,128,128]{2,1,0:T(8,128)}, f32[64,128,128]{2,1,0:T(8,128)}, u32[]{:S(2)}, u32[]{:S(2)}) %collective-permute-start) | collective-permute-done | bytes 4194336 | tf_op jit(solution)/shard_map/ppermute | solution.py:12
  128.5 4.3 %gather_fusion.1 = f32[36,128,128]{2,1,0:T(8,128)} fusion(f32[64,128,128]{2,1,0:T(8,128)} %collective-permute-done, s32[1024]{0:T(1024)S(1)} %pad_clamp_fusion), kind=kCustom, calls=%fused_computation.1 | custom fusion | bytes 4718736 | tf_op jit(solution)/shard_map/gather | solution.py:66
  132.8 4.0 %fusion.7 = f32[18,64,1,2,128]{4,1,3,0,2:T(8,128)S(1)} fusion(f32[18,2,128,128]{3,2,1,0:T(8,128)S(1)} %bitcast.28, f32[18,2,128,128]{3,2,1,0:T(8,128)} %bitcast.29, f32[18,64,2,128]{3,2,1,0:T(2,128)S(1)} %reshape.47, pred[18,2]{1,0:T(8,128)(4,1)S(1)} %copy.21), kind=kOutput, calls=%fused_computation.7 | convolution fusion | flops 453574656 | bytes 7077924 | tf_op jit(solution)/shard_map/rschk,rchkl->rschl/dot_general | solution.py:67
  136.8 0.9 copy.25
  137.7 1.9 %copy.26 = f32[1152,1,256]{0,2,1:T(8,128)S(1)} copy(f32[1152,1,256]{2,1,0:T(1,128)S(1)} %bitcast.30) | data formatting | bytes 2359296 | tf_op jit(solution)/shard_map/reshape | solution.py:69
  139.7 0.0 reduce-scatter.2.cloned.1.call-done
  139.7 1.4 select_add_fusion
  141.1 2.1 %copy.27 = f32[1152,1,256]{2,1,0:T(1,128)} copy(f32[1152,1,256]{0,2,1:T(8,128)S(1)} %select_add_fusion) | data formatting | bytes 2359296 | tf_op jit(solution)/shard_map/add | solution.py:70
  (4 shorter events, 0.1 us)
Async XLA Ops:
  7.4 58.8 %copy-start = (f32[1152,1,256]{2,1,0:T(1,128)S(1)}, f32[1152,1,256]{2,1,0:T(1,128)}, u32[]{:S(2)}) copy-start(f32[1152,1,256]{2,1,0:T(1,128)} %param.5) | copy-start | bytes 3538948
  7.4 56.2 %all-gather.5.cloned.1.call-start = ((), (), s32[]{:S(2)}) async-start(), calls=%async_computation.2 | async-start | bytes 2228224 | tf_op jit(solution)/shard_map/all_gather | solution.py:45
  8.1 112.6 %all-gather.7.cloned.1.call-start = ((), (), s32[]{:S(2)}) async-start(), calls=%async_computation.3 | async-start | bytes 4718592 | tf_op jit(solution)/shard_map/all_gather | solution.py:46
  65.5 74.3 %reduce-scatter.2.cloned.1.call-start = ((), (), s32[]{:S(2)}) async-start(), calls=%async_computation.1 | async-start | bytes 5898240 | tf_op jit(solution)/shard_map/reduce_scatter | solution.py:54
  120.7 1.1 copy-start.1
  120.7 7.8 %collective-permute-start = (f32[64,128,128]{2,1,0:T(8,128)}, f32[64,128,128]{2,1,0:T(8,128)}, u32[]{:S(2)}, u32[]{:S(2)}) collective-permute-start(f32[64,128,128]{2,1,0:T(8,128)} %bitcast.31), channel_id=1, source_target_pairs={{0,4},{4,0},{1,5},{5,1},{2,6},{6,2},{3,7},{7,3},{8,12},{12,8},{9,1... | collective-permute-start | bytes 12582920 | tf_op jit(solution)/shard_map/ppermute | solution.py:12
Sparse Core Ops, SparseCore 0:
  10.6 52.8 all-gather.4
  65.6 55.0 all-gather.6
Sparse Core Ops, SparseCore 1:
  80.7 53.7 reduce-scatter.1

commit v9 on v7

--- a/solution.py
+++ b/solution.py
@@ -1,6 +1,7 @@
 import jax
 import jax.numpy as jnp
 from jax import lax
+from jax.experimental import pallas as pl
 from jax.sharding import Mesh
 from jax.sharding import PartitionSpec as P
 
@@ -35,6 +36,30 @@
     return jnp.stack([x] + [shift(x, axis, -o) for o in range(1, n)], axis=0)
 
 
+def ladder_kernel(p_ref, l_ref, o_ref):
+    o_ref[...] = jnp.dot(p_ref[...], l_ref[...], preferred_element_type=jnp.float32)
+
+
+def ladder_matmul(weights, lowered, block=512):
+    rows, depth = weights.shape
+    width = lowered.shape[1]
+    return pl.pallas_call(
+        ladder_kernel,
+        grid=(rows // block,),
+        in_specs=[
+            pl.BlockSpec((block, depth), lambda i: (i, 0)),
+            pl.BlockSpec((depth, width), lambda i: (0, 0)),
+        ],
+        out_specs=pl.BlockSpec((block, width), lambda i: (i, 0)),
+        out_shape=jax.ShapeDtypeStruct((rows, width), jnp.float32),
+        cost_estimate=pl.CostEstimate(
+            flops=2 * rows * depth * width,
+            bytes_accessed=2 * rows * depth + 2 * depth * width + 4 * rows * width,
+            transcendentals=0,
+        ),
+    )(weights, lowered)
+
+
 def local(amplitudes, pair_interaction, ph_interaction, pp_size, ph_owner):
     row_count, chan_count, hole_width = amplitudes.shape
     row_tiles, _, col_tiles = ph_owner.shape
@@ -50,13 +75,13 @@
     positions = offset + jnp.arange(row_count, dtype=jnp.int32)
     live_mask = positions[:, None] < (pp_size * tile_rows)[None, :]
     masked = jnp.where(live_mask[:, :, None], amplitudes, jnp.zeros_like(amplitudes))
-    lowered = masked.astype(jnp.bfloat16)
+    lowered = masked.reshape(row_count, hole_width).astype(jnp.bfloat16)
     ladder = lax.psum_scatter(
-        jnp.einsum("crk,kch->rch", pair_interaction, lowered, preferred_element_type=jnp.float32),
+        ladder_matmul(pair_interaction[0], lowered),
         "ctr",
         scatter_dimension=0,
         tiled=True,
-    )
+    ).reshape(row_count, chan_count, hole_width)
     owner_dev = ph_owner // per_dev
     o_y = owner_dev // (nz * nc)
     o_z = owner_dev // nc % nz

time: 110 us -> 112 us (1.018)
  matrix products: 16.3 us -> 3.99 us
  Pallas kernels: 0 us -> 10.8 us
  waiting for transfers between devices: 46.9 us -> 49.8 us
    dot_general x1 -> x0, matrix products: 12.3 us -> none  [local(): jnp.einsum('crk,kch->rch', pair_interaction, lowered, preferred_element_t...]
    pallas_call x0 -> x1, Pallas kernels: none -> 10.8 us  [ladder_matmul(): pl.pallas_call(ladder_kernel, grid=(rows // block,), in_specs=[pl.BlockSp...]
    add x1, local copies, waits for them, and re-layouts: 2.1 us -> 5.99 us  [local(): jnp.where(live_mask[:, :, None], ladder, jnp.zeros_like(ladder)) + cycle]
    all_gather x1, waiting for transfers between devices: 43.9 us -> 46.5 us  [local(): own = lax.all_gather(by_y, 'cz', axis=0, tiled=False)]
    reshape x1 -> x0, local copies, waits for them, and re-layouts: 1.95 us -> none  [local(): cycle = jnp.einsum('rschk,rchkl->rschl', blocks, chosen, precision=lax.Pr...]
    unnamed x5 -> x4, local copies, waits for them, and re-layouts: 1.96 us -> 0.01 us
  transfers between devices with their start and end apart: 3 -> 3, of which waited for: 2 -> 2; matrix products, arithmetic and copies ran while one was open for 27% -> 13% of each run, Pallas kernels for 0% -> 10%
where the time goes in v9:
time: 112 us
  waiting for transfers between devices  49.8 us (44%)
  between operations  15.6 us (14%)
  local copies, waits for them, and re-layouts  15 us (13%)
  blocking collectives  13.4 us (12%)
  Pallas kernels  10.8 us (10%)
  matrix products  3.99 us (4%)
  other arithmetic  2.59 us (2%)
    all_gather x1, waiting for transfers between devices, local(): own = lax.all_gather(by_y, 'cz', axis=0, tiled=False)  46.5 us
    all_gather x1, blocking collectives, local(): by_y = lax.all_gather(ph_interaction, 'cy', axis=0, tiled=False)  13.4 us
    pallas_call x1, Pallas kernels, ladder_matmul(): pl.pallas_call(ladder_kernel, grid=(rows // block,), in_specs=[pl.BlockSp...  10.8 us
    gather x2, local copies, waits for them, and re-layouts, local(): chosen = jnp.where((o_c == 0)[..., None, None], own[slot], sibling[slot])  7.22 us
    add x1, local copies, waits for them, and re-layouts, local(): jnp.where(live_mask[:, :, None], ladder, jnp.zeros_like(ladder)) + cycle  5.99 us
    dot_general x1, matrix products, local(): jnp.einsum('rschk,rchkl->rschl', blocks, chosen, precision=lax.Precision....  3.99 us
    ppermute x1, waiting for transfers between devices, shift(): return lax.ppermute(x, axis, [(k, (k + step) % n) for k in range(n)])  3.25 us
  transfers between devices with their start and end apart: 3, of which 2 were waited for; matrix products, arithmetic and copies ran while one was open for 13% of the time, Pallas kernels for 10%

profile of v9, /device:TPU:1, one launch (start us, length us, event | category | flops | bytes accessed | tf_op | source)
XLA Modules:
  0.0 111.9 jit_solution(16883983942721843629)
XLA Ops:
  7.4 0.0 copy-start
  7.4 0.0 all-gather.4.cloned.1.call-start
  7.4 13.4 %all-gather = f32[8,128,128]{2,1,0:T(8,128)} all-gather(f32[2,128,128]{2,1,0:T(8,128)} %param.7), channel_id=2, replica_groups=mesh['cy'=4,'cz'=8,'core'=2,'ctr'=4] {'cy'}, dimensions={0}, use_global_device_ids=true | all-gather | bytes 655360 | tf_op jit(solution)/shard_map/all_gather | solution.py:70
  20.7 0.0 all-gather.4.cloned.1.call-update
  20.8 0.0 reduce-scatter.2.cloned.1.call-start
  21.5 0.0 copy-done
  21.5 1.0 convert_bitcast_fusion
  22.5 10.8 %shard_map.55 = f32[4608,256]{1,0:T(8,128)} custom-call(bf16[4608,1152]{1,0:T(8,128)(2,1)} %bitcast.27, bf16[1152,256]{1,0:T(8,128)(2,1)} %get-tuple-element.5.l_ref), custom_call_target="tpu_custom_call" | custom-call | flops 2717908992 | bytes 15925248 | tf_op jit(solution)/shard_map/pallas_call | solution.py:46
  33.3 0.0 copy-start.1
  33.3 0.0 reduce-scatter.2.cloned.1.call-update
  33.4 46.5 %all-gather.4.cloned.1.call-done = f32[32,2,128,128]{3,2,1,0:T(8,128)} async-done(((f32[4,2,128,128]{3,2,1,0:T(8,128)}), f32[32,2,128,128]{3,2,1,0:T(8,128)}) %all-gather.4.cloned.1.call-update) | async-done | bytes 4194320 | tf_op jit(solution)/shard_map/all_gather | solution.py:71
  79.8 0.7 collective-permute-start
  80.5 0.0 copy-done.1
  80.6 0.1 copy.20
  80.7 0.1 reshape.44
  80.8 0.6 reshape.40
  81.4 0.1 copy.19
  81.5 2.9 %gather_fusion = f32[36,128,128]{2,1,0:T(8,128)S(1)} fusion(f32[64,128,128]{2,1,0:T(8,128)} %bitcast.33, s32[1024]{0:T(1024)S(1)} %pad_clamp_fusion), kind=kCustom, calls=%fused_computation | custom fusion | bytes 4718736 | tf_op jit(solution)/shard_map/gather | solution.py:91
  84.4 3.3 %collective-permute-done = f32[64,128,128]{2,1,0:T(8,128)} collective-permute-done((f32[64,128,128]{2,1,0:T(8,128)}, f32[64,128,128]{2,1,0:T(8,128)}, u32[]{:S(2)}, u32[]{:S(2)}) %collective-permute-start) | collective-permute-done | bytes 4194336 | tf_op jit(solution)/shard_map/ppermute | solution.py:13
  87.6 4.3 %gather_fusion.1 = f32[36,128,128]{2,1,0:T(8,128)} fusion(f32[64,128,128]{2,1,0:T(8,128)} %collective-permute-done, s32[1024]{0:T(1024)S(1)} %pad_clamp_fusion), kind=kCustom, calls=%fused_computation.1 | custom fusion | bytes 4718736 | tf_op jit(solution)/shard_map/gather | solution.py:91
  92.0 4.0 %fusion.2 = f32[18,64,1,2,128]{4,1,3,0,2:T(8,128)S(1)} fusion(f32[18,2,128,128]{3,2,1,0:T(8,128)S(1)} %bitcast.28, f32[18,2,128,128]{3,2,1,0:T(8,128)} %bitcast.29, f32[18,64,2,128]{3,2,1,0:T(2,128)S(1)} %reshape.40, pred[18,2]{1,0:T(8,128)(4,1)S(1)} %copy.19), kind=kOutput, calls=%fused_computation.4 | convolution fusion | flops 453574656 | bytes 7077924 | tf_op jit(solution)/shard_map/rschk,rchkl->rschl/dot_general | solution.py:92
  96.0 0.9 copy.22
  96.9 0.0 reduce-scatter.2.cloned.1.call-done
  96.9 1.5 %fusion.5 = f32[1152,1,256]{2,0,1:T(8,128)S(1)} fusion(f32[144,8,2,128]{3,2,1,0:T(2,128)S(1)} %bitcast.30, f32[1152,256]{1,0:T(8,128)} %reduce-scatter.2.cloned.1.call-done, pred[1152]{0:T(1024)(128)(4,1)S(1)} %add_compare_fusion), kind=kLoop, calls=%fused_computation.6 | loop fusion | flops 589824 | bytes 3540096 | tf_op jit(solution)/shard_map/add | solution.py:95
  98.4 6.0 %copy.23 = f32[1152,1,256]{2,1,0:T(1,128)} copy(f32[1152,1,256]{2,0,1:T(8,128)S(1)} %fusion.5) | data formatting | bytes 2359296 | tf_op jit(solution)/shard_map/add | solution.py:95
  (4 shorter events, 0.1 us)
Async XLA Ops:
  7.4 14.1 %copy-start = (f32[1152,1,256]{2,1,0:T(1,128)S(1)}, f32[1152,1,256]{2,1,0:T(1,128)}, u32[]{:S(2)}) copy-start(f32[1152,1,256]{2,1,0:T(1,128)} %param.5) | copy-start | bytes 3538948
  7.4 72.5 %all-gather.4.cloned.1.call-start = ((), (), s32[]{:S(2)}) async-start(), calls=%async_computation.2 | async-start | bytes 4718592 | tf_op jit(solution)/shard_map/all_gather | solution.py:71
  20.8 76.2 %reduce-scatter.2.cloned.1.call-start = ((), (), s32[]{:S(2)}) async-start(), calls=%async_computation.1 | async-start | bytes 5898240 | tf_op jit(solution)/shard_map/reduce_scatter | solution.py:79
  33.3 47.2 %copy-start.1 = (s32[18,1,2]{0,2,1:T(2,128)S(1)}, s32[18,1,2]{0,2,1:T(2,128)}, u32[]{:S(2)}) copy-start(s32[18,1,2]{0,2,1:T(2,128)} %param.9) | copy-start | bytes 436
  79.8 7.8 %collective-permute-start = (f32[64,128,128]{2,1,0:T(8,128)}, f32[64,128,128]{2,1,0:T(8,128)}, u32[]{:S(2)}, u32[]{:S(2)}) collective-permute-start(f32[64,128,128]{2,1,0:T(8,128)} %bitcast.32), channel_id=1, source_target_pairs={{0,4},{4,0},{1,5},{5,1},{2,6},{6,2},{3,7},{7,3},{8,12},{12,8},{9,1... | collective-permute-start | bytes 12582920 | tf_op jit(solution)/shard_map/ppermute | solution.py:13
Sparse Core Ops, SparseCore 0:
  20.9 58.9 all-gather.3
Sparse Core Ops, SparseCore 1:
  33.5 57.6 reduce-scatter.1

commit v10 on v8

--- a/solution.py
+++ b/solution.py
@@ -42,7 +42,7 @@
     tile_cols = hole_width // col_tiles
     per_dev = ph_interaction.shape[0]
     ny, nz, nc = lax.axis_size("cy"), lax.axis_size("cz"), lax.axis_size("core")
-    by_y = lax.all_gather(ph_interaction, ("cy", "ctr"), axis=0, tiled=False).reshape((-1, 4) + ph_interaction.shape)[:, 0]
+    by_y = ring_gather(ph_interaction, "cy")
     own = lax.all_gather(by_y, "cz", axis=0, tiled=False)
     own = own.reshape((-1,) + ph_interaction.shape[1:])
     sibling = shift(own, "core", 1)
@@ -58,7 +58,7 @@
         tiled=True,
     )
     owner_dev = ph_owner // per_dev
-    o_y = owner_dev // (nz * nc)
+    o_y = (owner_dev // (nz * nc) - lax.axis_index("cy")) % ny
     o_z = owner_dev // nc % nz
     o_c = (owner_dev % nc - lax.axis_index("core")) % nc
     slot = (o_z * ny + o_y) * per_dev + ph_owner % per_dev

time: 151 us -> 111 us (0.74)
  waiting for transfers between devices: 99.2 us -> 52.2 us
  starting transfers between devices: 0.76 us -> 7.68 us
  local copies, waits for them, and re-layouts: 17.3 us -> 15.4 us
  other arithmetic: 1.54 us -> 3.3 us
    all_gather x1 -> x0, waiting for transfers between devices: 55.4 us -> none  [local(): lax.all_gather(ph_interaction, ('cy', 'ctr'), axis=0, tiled=False)]
    ppermute x1 -> x5, starting transfers between devices: 0.68 us -> 7.64 us  [shift(): return lax.ppermute(x, axis, [(k, (k + step) % n) for k in range(n)])]
    ppermute x1 -> x5, waiting for transfers between devices: 2.87 us -> 9.66 us  [shift(): return lax.ppermute(x, axis, [(k, (k + step) % n) for k in range(n)])]
    all_gather x1, waiting for transfers between devices: 40.1 us -> 42.5 us  [local(): own = lax.all_gather(by_y, 'cz', axis=0, tiled=False)]
    slice x1 -> x2, local copies, waits for them, and re-layouts: 1.87 us -> 0.01 us  [the longest x1 0.01 us: ring_gather(): down[-1][cut:]]
    another operation x0 -> x2, other arithmetic: none -> 1.75 us  [ring_gather(): return jnp.stack(pieces, axis=0)]
  transfers between devices with their start and end apart: 4 -> 7, of which waited for: 3 -> 5; matrix products, arithmetic and copies ran while one was open for 20% -> 27% of each run, Pallas kernels for 0% -> 0%
where the time goes in v10:
time: 111 us
  waiting for transfers between devices  52.2 us (47%)
  matrix products  16.3 us (15%)
  between operations  15.6 us (14%)
  local copies, waits for them, and re-layouts  15.4 us (14%)
  starting transfers between devices  7.68 us (7%)
  other arithmetic  3.3 us (3%)
    all_gather x1, waiting for transfers between devices, local(): own = lax.all_gather(by_y, 'cz', axis=0, tiled=False)  42.5 us
    dot_general x1, matrix products, local(): jnp.einsum('crk,kch->rch', pair_interaction, lowered, preferred_element_t...  12.3 us
    ppermute x5, waiting for transfers between devices, shift(): return lax.ppermute(x, axis, [(k, (k + step) % n) for k in range(n)])  9.66 us
    ppermute x5, starting transfers between devices, shift(): return lax.ppermute(x, axis, [(k, (k + step) % n) for k in range(n)])  7.64 us
    gather x2, local copies, waits for them, and re-layouts, local(): chosen = jnp.where((o_c == 0)[..., None, None], own[slot], sibling[slot])  7.19 us
    dot_general x1, matrix products, local(): jnp.einsum('rschk,rchkl->rschl', blocks, chosen, precision=lax.Precision....  3.99 us
  transfers between devices with their start and end apart: 7, of which 5 were waited for; matrix products, arithmetic and copies ran while one was open for 27% of the time, Pallas kernels for 0%

profile of v10, /device:TPU:1, one launch (start us, length us, event | category | flops | bytes accessed | tf_op | source)
XLA Modules:
  0.0 110.5 jit_solution(10956241798471401526)
XLA Ops:
  7.4 3.6 %collective-permute-start = (f32[2,128,128]{2,1,0:T(8,128)}, f32[2,128,128]{2,1,0:T(8,128)S(1)}, u32[]{:S(2)}, u32[]{:S(2)}) collective-permute-start(f32[2,128,128]{2,1,0:T(8,128)} %param.7), channel_id=1, source_target_pairs={{0,192},{64,0},{128,64},{192,128},{1,193},{65,1},{129,65},{193,129... | collective-permute-start | bytes 393224 | tf_op jit(solution)/shard_map/ppermute | solution.py:12
  10.9 0.0 collective-permute-start.2
  10.9 2.5 %collective-permute-done = f32[2,128,128]{2,1,0:T(8,128)S(1)} collective-permute-done((f32[2,128,128]{2,1,0:T(8,128)}, f32[2,128,128]{2,1,0:T(8,128)S(1)}, u32[]{:S(2)}, u32[]{:S(2)}) %collective-permute-start) | collective-permute-done | bytes 131104 | tf_op jit(solution)/shard_map/ppermute | solution.py:12
  13.4 3.3 %collective-permute-start.1 = (f32[1,128,128]{2,1,0:T(8,128)S(1)}, f32[1,128,128]{2,1,0:T(8,128)S(1)}, u32[]{:S(2)}, u32[]{:S(2)}) collective-permute-start(f32[1,128,128]{2,1,0:T(8,128)S(1)} %slice.12), channel_id=1, source_target_pairs={{0,192},{64,0},{128,64},{192,128},{1,193},{65,1},{129,65},{193,129... | collective-permute-start | bytes 196616 | tf_op jit(solution)/shard_map/ppermute | solution.py:12
  16.7 0.0 collective-permute-done.2
  16.7 0.1 collective-permute-start.3
  16.8 1.2 %collective-permute-done.1 = f32[1,128,128]{2,1,0:T(8,128)S(1)} collective-permute-done((f32[1,128,128]{2,1,0:T(8,128)S(1)}, f32[1,128,128]{2,1,0:T(8,128)S(1)}, u32[]{:S(2)}, u32[]{:S(2)}) %collective-permute-start.1) | collective-permute-done | bytes 65568 | tf_op jit(solution)/shard_map/ppermute | solution.py:12
  18.1 3.1 %collective-permute-done.3 = f32[1,128,128]{2,1,0:T(8,128)S(1)} collective-permute-done((f32[1,128,128]{2,1,0:T(8,128)S(1)}, f32[1,128,128]{2,1,0:T(8,128)S(1)}, u32[]{:S(2)}, u32[]{:S(2)}) %collective-permute-start.3) | collective-permute-done | bytes 65568 | tf_op jit(solution)/shard_map/ppermute | solution.py:12
  21.2 1.7 %pad_maximum_fusion = f32[4,2,128,128]{3,2,1,0:T(8,128)} fusion(f32[1,2,128,128]{3,2,1,0:T(8,128)S(1)} %bitcast.38, f32[1,2,128,128]{3,2,1,0:T(8,128)S(1)} %maximum_bitcast_fusion, f32[1,2,128,128]{3,2,1,0:T(8,128)S(1)} %bitcast.37, f32[1,2,128,128]{3,2,1,0:T(8,128)} %bitcast.39), kind=kLoop, calls=%fused_computation.14 | loop fusion | flops 393216 | bytes 1048576 | tf_op jit(solution)/shard_map/stack | solution.py:30
  22.9 0.0 all-gather.3.cloned.1.call-update
  22.9 0.0 reduce-scatter.2.cloned.1.call-start
  23.6 1.9 %copy.20 = f32[1152,1,256]{0,2,1:T(8,128)S(1)} copy(f32[1152,1,256]{2,1,0:T(1,128)S(1)} %copy-done) | data formatting | bytes 2359296 | tf_op args[0]
  25.6 0.1 broadcast_select_fusion
  25.7 12.3 %fusion.2 = f32[4608,1,256]{0,2,1:T(8,128)} fusion(bf16[1,4608,1152]{2,1,0:T(8,128)(2,1)} %param.6, f32[1152,1,256]{0,2,1:T(8,128)S(1)} %broadcast_select_fusion), kind=kOutput, calls=%fused_computation.4 | convolution fusion | flops 2718203904 | bytes 16515072 | tf_op jit(solution)/shard_map/crk,kch->rch/dot_general | solution.py:55
  38.1 0.0 reduce-scatter.2.cloned.1.call-update
  38.1 42.5 %all-gather.3.cloned.1.call-done = f32[32,2,128,128]{3,2,1,0:T(8,128)} async-done(((f32[4,2,128,128]{3,2,1,0:T(8,128)}), f32[32,2,128,128]{3,2,1,0:T(8,128)}) %all-gather.3.cloned.1.call-update) | async-done | bytes 4194320 | tf_op jit(solution)/shard_map/all_gather | solution.py:46
  80.5 0.7 collective-permute-start.4
  81.2 0.4 copy.23
  81.6 0.0 copy-done.1
  81.7 0.1 copy.22
  81.8 0.1 reshape.47
  81.9 0.6 reshape.43
  82.5 0.1 copy.21
  82.6 2.9 %gather_fusion = f32[36,128,128]{2,1,0:T(8,128)S(1)} fusion(f32[64,128,128]{2,1,0:T(8,128)} %bitcast.36, s32[1024]{0:T(1024)S(1)} %pad_clamp_fusion), kind=kCustom, calls=%fused_computation | custom fusion | bytes 4718736 | tf_op jit(solution)/shard_map/gather | solution.py:66
  85.5 2.9 %collective-permute-done.4 = f32[64,128,128]{2,1,0:T(8,128)} collective-permute-done((f32[64,128,128]{2,1,0:T(8,128)}, f32[64,128,128]{2,1,0:T(8,128)}, u32[]{:S(2)}, u32[]{:S(2)}) %collective-permute-start.4) | collective-permute-done | bytes 4194336 | tf_op jit(solution)/shard_map/ppermute | solution.py:12
  88.4 4.3 %gather_fusion.1 = f32[36,128,128]{2,1,0:T(8,128)} fusion(f32[64,128,128]{2,1,0:T(8,128)} %collective-permute-done.4, s32[1024]{0:T(1024)S(1)} %pad_clamp_fusion), kind=kCustom, calls=%fused_computation.1 | custom fusion | bytes 4718736 | tf_op jit(solution)/shard_map/gather | solution.py:66
  92.7 4.0 %fusion.7 = f32[18,64,1,2,128]{4,1,3,0,2:T(8,128)S(1)} fusion(f32[18,2,128,128]{3,2,1,0:T(8,128)S(1)} %bitcast.32, f32[18,2,128,128]{3,2,1,0:T(8,128)} %bitcast.33, f32[18,64,2,128]{3,2,1,0:T(2,128)S(1)} %reshape.43, pred[18,2]{1,0:T(8,128)(4,1)S(1)} %copy.21), kind=kOutput, calls=%fused_computation.7 | convolution fusion | flops 453574656 | bytes 7077924 | tf_op jit(solution)/shard_map/rschk,rchkl->rschl/dot_general | solution.py:67
  96.7 0.9 copy.25
  97.6 1.9 %copy.26 = f32[1152,1,256]{0,2,1:T(8,128)S(1)} copy(f32[1152,1,256]{2,1,0:T(1,128)S(1)} %bitcast.34) | data formatting | bytes 2359296 | tf_op jit(solution)/shard_map/reshape | solution.py:69
  99.5 0.0 reduce-scatter.2.cloned.1.call-done
  99.6 1.4 %select_add_fusion = f32[1152,1,256]{0,2,1:T(8,128)S(1)} fusion(f32[1152,1,256]{0,2,1:T(8,128)S(1)} %copy.26, f32[1152,1,256]{0,2,1:T(8,128)} %reduce-scatter.2.cloned.1.call-done, pred[1152]{0:T(1024)(128)(4,1)S(1)} %add_compare_fusion), kind=kLoop, calls=%fused_computation.9 | loop fusion | flops 589824 | bytes 3540096 | tf_op jit(solution)/shard_map/add | solution.py:70
  101.0 2.1 %copy.27 = f32[1152,1,256]{2,1,0:T(1,128)} copy(f32[1152,1,256]{0,2,1:T(8,128)S(1)} %select_add_fusion) | data formatting | bytes 2359296 | tf_op jit(solution)/shard_map/add | solution.py:70
  (11 shorter events, 0.1 us)
Async XLA Ops:
  7.4 16.3 %copy-start = (f32[1152,1,256]{2,1,0:T(1,128)S(1)}, f32[1152,1,256]{2,1,0:T(1,128)}, u32[]{:S(2)}) copy-start(f32[1152,1,256]{2,1,0:T(1,128)} %param.5) | copy-start | bytes 3538948
  7.4 73.2 %all-gather.3.cloned.1.call-start = ((), (), s32[]{:S(2)}) async-start(), calls=%async_computation.2 | async-start | bytes 4718592 | tf_op jit(solution)/shard_map/all_gather | solution.py:46
  7.4 6.0 %collective-permute-start = (f32[2,128,128]{2,1,0:T(8,128)}, f32[2,128,128]{2,1,0:T(8,128)S(1)}, u32[]{:S(2)}, u32[]{:S(2)}) collective-permute-start(f32[2,128,128]{2,1,0:T(8,128)} %param.7), channel_id=1, source_target_pairs={{0,192},{64,0},{128,64},{192,128},{1,193},{65,1},{129,65},{193,129... | collective-permute-start | bytes 393224 | tf_op jit(solution)/shard_map/ppermute | solution.py:12
  10.9 5.8 %collective-permute-start.2 = (f32[2,128,128]{2,1,0:T(8,128)}, f32[2,128,128]{2,1,0:T(8,128)S(1)}, u32[]{:S(2)}, u32[]{:S(2)}) collective-permute-start(f32[2,128,128]{2,1,0:T(8,128)} %param.7), channel_id=1, source_target_pairs={{0,64},{64,128},{128,192},{192,0},{1,65},{65,129},{129,193},{193,1... | collective-permute-start | bytes 393224 | tf_op jit(solution)/shard_map/ppermute | solution.py:12
  13.4 4.6 %collective-permute-start.1 = (f32[1,128,128]{2,1,0:T(8,128)S(1)}, f32[1,128,128]{2,1,0:T(8,128)S(1)}, u32[]{:S(2)}, u32[]{:S(2)}) collective-permute-start(f32[1,128,128]{2,1,0:T(8,128)S(1)} %slice.12), channel_id=1, source_target_pairs={{0,192},{64,0},{128,64},{192,128},{1,193},{65,1},{129,65},{193,129... | collective-permute-start | bytes 196616 | tf_op jit(solution)/shard_map/ppermute | solution.py:12
  16.7 4.4 %collective-permute-start.3 = (f32[1,128,128]{2,1,0:T(8,128)S(1)}, f32[1,128,128]{2,1,0:T(8,128)S(1)}, u32[]{:S(2)}, u32[]{:S(2)}) collective-permute-start(f32[1,128,128]{2,1,0:T(8,128)S(1)} %slice.13), channel_id=1, source_target_pairs={{0,64},{64,128},{128,192},{192,0},{1,65},{65,129},{129,193},{193,1... | collective-permute-start | bytes 196616 | tf_op jit(solution)/shard_map/ppermute | solution.py:12
  22.9 76.6 %reduce-scatter.2.cloned.1.call-start = ((), (), s32[]{:S(2)}) async-start(), calls=%async_computation.1 | async-start | bytes 5898240 | tf_op jit(solution)/shard_map/reduce_scatter | solution.py:54
  80.5 1.1 copy-start.1
  80.5 7.8 %collective-permute-start.4 = (f32[64,128,128]{2,1,0:T(8,128)}, f32[64,128,128]{2,1,0:T(8,128)}, u32[]{:S(2)}, u32[]{:S(2)}) collective-permute-start(f32[64,128,128]{2,1,0:T(8,128)} %bitcast.35), channel_id=1, source_target_pairs={{0,4},{4,0},{1,5},{5,1},{2,6},{6,2},{3,7},{7,3},{8,12},{12,8},{9,1... | collective-permute-start | bytes 12582920 | tf_op jit(solution)/shard_map/ppermute | solution.py:12
Sparse Core Ops, SparseCore 0:
  23.0 57.4 all-gather.2
Sparse Core Ops, SparseCore 1:
  38.2 56.1 reduce-scatter.1

commit v11 on v7

--- a/solution.py
+++ b/solution.py
@@ -45,25 +45,30 @@
     by_y = lax.all_gather(ph_interaction, "cy", axis=0, tiled=False)
     own = lax.all_gather(by_y, "cz", axis=0, tiled=False)
     own = own.reshape((-1,) + ph_interaction.shape[1:])
-    sibling = shift(own, "core", 1)
     offset = lax.axis_index("ctr") * row_count
     positions = offset + jnp.arange(row_count, dtype=jnp.int32)
     live_mask = positions[:, None] < (pp_size * tile_rows)[None, :]
     masked = jnp.where(live_mask[:, :, None], amplitudes, jnp.zeros_like(amplitudes))
     lowered = masked.astype(jnp.bfloat16)
+    my_core = lax.axis_index("core")
+
+    def place(owner):
+        dev = owner // per_dev
+        here = ((dev // nc % nz) * ny + dev // (nz * nc)) * per_dev + owner % per_dev
+        return here, dev % nc
+
+    slot, owner_core = place(ph_owner)
+    sib_slot, _ = place(shift(ph_owner, "core", 1))
+    blocks = masked.reshape(row_tiles, tile_rows, chan_count, col_tiles, tile_cols)
+    slot, sib_slot, blocks, lowered = lax.optimization_barrier((slot, sib_slot, blocks, lowered))
     ladder = lax.psum_scatter(
         jnp.einsum("crk,kch->rch", pair_interaction, lowered, preferred_element_type=jnp.float32),
         "ctr",
         scatter_dimension=0,
         tiled=True,
     )
-    owner_dev = ph_owner // per_dev
-    o_y = owner_dev // (nz * nc)
-    o_z = owner_dev // nc % nz
-    o_c = (owner_dev % nc - lax.axis_index("core")) % nc
-    slot = (o_z * ny + o_y) * per_dev + ph_owner % per_dev
-    blocks = masked.reshape(row_tiles, tile_rows, chan_count, col_tiles, tile_cols)
-    chosen = jnp.where((o_c == 0)[..., None, None], own[slot], sibling[slot])
+    from_sibling = shift(own[sib_slot], "core", 1)
+    chosen = jnp.where((owner_core == my_core)[..., None, None], own[slot], from_sibling)
     cycle = jnp.einsum(
         "rschk,rchkl->rschl", blocks, chosen, precision=lax.Precision.HIGHEST
     ).reshape(row_count, chan_count, hole_width)

time: 110 us -> 108 us (0.982)
  waiting for transfers between devices: 46.9 us -> 38.3 us
  starting transfers between devices: 0.72 us -> 4.81 us
  local copies, waits for them, and re-layouts: 15.4 us -> 17.4 us
    all_gather x1, waiting for transfers between devices: 43.9 us -> 36.8 us  [local(): own = lax.all_gather(by_y, 'cz', axis=0, tiled=False)]
    ppermute x1 -> x2, starting transfers between devices: 0.68 us -> 4.76 us  [shift(): return lax.ppermute(x, axis, [(k, (k + step) % n) for k in range(n)])]
    ppermute x1 -> x2, waiting for transfers between devices: 2.87 us -> 1.24 us  [shift(): return lax.ppermute(x, axis, [(k, (k + step) % n) for k in range(n)])]
    select_n x1, local copies, waits for them, and re-layouts: 0.36 us -> 1.96 us  [local(): jnp.where(live_mask[:, :, None], amplitudes, jnp.zeros_like(amplitudes))]
    unnamed x5 -> x3, local copies, waits for them, and re-layouts: 1.96 us -> 2.6 us
  transfers between devices with their start and end apart: 3 -> 4, of which waited for: 2 -> 3; matrix products, arithmetic and copies ran while one was open for 27% -> 30% of each run, Pallas kernels for 0% -> 0%
where the time goes in v11:
time: 108 us
  waiting for transfers between devices  38.3 us (35%)
  local copies, waits for them, and re-layouts  17.4 us (16%)
  matrix products  16.5 us (15%)
  between operations  15.6 us (14%)
  blocking collectives  13.4 us (12%)
  starting transfers between devices  4.81 us (4%)
  other arithmetic  1.61 us (1%)
    all_gather x1, waiting for transfers between devices, local(): own = lax.all_gather(by_y, 'cz', axis=0, tiled=False)  36.8 us
    all_gather x1, blocking collectives, local(): by_y = lax.all_gather(ph_interaction, 'cy', axis=0, tiled=False)  13.4 us
    dot_general x1, matrix products, local(): jnp.einsum('crk,kch->rch', pair_interaction, lowered, preferred_element_t...  12.4 us
    ppermute x2, starting transfers between devices, shift(): return lax.ppermute(x, axis, [(k, (k + step) % n) for k in range(n)])  4.76 us
    gather x1, local copies, waits for them, and re-layouts, local(): from_sibling = shift(own[sib_slot], 'core', 1)  4.43 us
    dot_general x1, matrix products, local(): jnp.einsum('rschk,rchkl->rschl', blocks, chosen, precision=lax.Precision....  4.08 us
    gather x1, local copies, waits for them, and re-layouts, local(): own[slot]  2.94 us
    unnamed x3, local copies, waits for them, and re-layouts  2.6 us
  transfers between devices with their start and end apart: 4, of which 3 were waited for; matrix products, arithmetic and copies ran while one was open for 30% of the time, Pallas kernels for 0%

profile of v11, /device:TPU:1, one launch (start us, length us, event | category | flops | bytes accessed | tf_op | source)
XLA Modules:
  0.0 107.5 jit_solution(8316021060811271842)
XLA Ops:
  7.4 0.0 copy-start
  7.4 0.0 all-gather.4.cloned.1.call-start
  7.4 13.4 %all-gather = f32[8,128,128]{2,1,0:T(8,128)} all-gather(f32[2,128,128]{2,1,0:T(8,128)} %param.7), channel_id=2, replica_groups=mesh['cy'=4,'cz'=8,'core'=2,'ctr'=4] {'cy'}, dimensions={0}, use_global_device_ids=true | all-gather | bytes 655360 | tf_op jit(solution)/shard_map/all_gather | solution.py:45
  20.7 0.0 all-gather.4.cloned.1.call-update
  20.8 0.0 reduce-scatter.2.cloned.1.call-start
  20.8 4.1 %collective-permute-start = (s32[18,1,2]{0,2,1:T(2,128)}, s32[18,1,2]{0,2,1:T(2,128)S(1)}, u32[]{:S(2)}, u32[]{:S(2)}) collective-permute-start(s32[18,1,2]{0,2,1:T(2,128)} %param.9), channel_id=1, source_target_pairs={{0,4},{4,0},{1,5},{5,1},{2,6},{6,2},{3,7},{7,3},{8,12},{12,8},{9,1... | collective-permute-start | bytes 440 | tf_op jit(solution)/shard_map/ppermute | solution.py:12
  24.9 2.6 %copy.22 = f32[1152,1,256]{0,2,1:T(8,128)S(1)} copy(f32[1152,1,256]{2,1,0:T(1,128)} %param.5) | data formatting | bytes 2359296 | tf_op args[0]
  28.2 0.0 copy-done
  28.2 0.1 fusion.22
  28.4 2.0 %copy.23 = f32[1152,1,256]{2,1,0:T(1,128)S(1)} copy(f32[1152,1,256]{0,2,1:T(8,128)S(1)} %get-tuple-element.16) | data formatting | bytes 2359296 | tf_op jit(solution)/shard_map/jit(_where)/select_n | solution.py:51
  30.3 0.0 collective-permute-done
  30.4 12.4 %fusion.2 = f32[4608,1,256]{0,2,1:T(8,128)} fusion(bf16[1,4608,1152]{2,1,0:T(8,128)(2,1)} %param.6, bf16[1152,1,256]{0,2,1:T(8,128)(2,1)S(1)} %get-tuple-element.9), kind=kOutput, calls=%fused_computation.4 | convolution fusion | flops 2717908992 | bytes 15925248 | tf_op jit(solution)/shard_map/crk,kch->rch/dot_general | solution.py:65
  42.8 0.0 reduce-scatter.2.cloned.1.call-update
  42.8 0.1 copy.26
  42.9 0.1 reshape.55
  43.0 36.8 %all-gather.4.cloned.1.call-done = f32[32,2,128,128]{3,2,1,0:T(8,128)} async-done(((f32[4,2,128,128]{3,2,1,0:T(8,128)}), f32[32,2,128,128]{3,2,1,0:T(8,128)}) %all-gather.4.cloned.1.call-update) | async-done | bytes 4194320 | tf_op jit(solution)/shard_map/all_gather | solution.py:46
  79.8 4.4 %gather_fusion.1 = f32[36,128,128]{2,1,0:T(8,128)} fusion(f32[64,128,128]{2,1,0:T(8,128)} %bitcast.36, s32[1024]{0:T(1024)S(1)} %pad_clamp_fusion), kind=kCustom, calls=%fused_computation.1 | custom fusion | bytes 4718736 | tf_op jit(solution)/shard_map/gather | solution.py:70
  84.3 0.7 collective-permute-start.1
  84.9 0.1 copy.24
  85.1 0.1 copy.25
  85.2 0.1 reshape.47
  85.3 2.9 %gather_fusion = f32[36,128,128]{2,1,0:T(8,128)S(1)} fusion(f32[64,128,128]{2,1,0:T(8,128)} %bitcast.37, s32[1024]{0:T(1024)S(1)} %pad_clamp_fusion.1), kind=kCustom, calls=%fused_computation | custom fusion | bytes 4718736 | tf_op jit(solution)/shard_map/gather | solution.py:71
  88.2 1.2 %collective-permute-done.1 = f32[18,1,2,128,128]{4,3,2,0,1:T(8,128)} collective-permute-done((f32[18,1,2,128,128]{4,3,2,0,1:T(8,128)}, f32[18,1,2,128,128]{4,3,2,0,1:T(8,128)}, u32[]{:S(2)}, u32[]{:S(2)}) %collective-permute-start.1) | collective-permute-done | bytes 2359328 | tf_op jit(solution)/shard_map/ppermute | solution.py:12
  89.5 4.1 %fusion.8 = f32[18,64,1,2,128]{4,1,3,0,2:T(8,128)S(1)} fusion(f32[18,1,2,128,128]{4,3,2,0,1:T(8,128)S(1)} %bitcast.35, f32[18,1,2,128,128]{4,3,2,0,1:T(8,128)} %collective-permute-done.1, f32[18,64,2,128]{3,2,1,0:T(2,128)S(1)} %bitcast.39, pred[18,2]{1,0:T(8,128)(4,1)S(1)} %copy.24), kind=kOutput, calls=%fused_computation.8 | convolution fusion | flops 453574656 | bytes 7077924 | tf_op jit(solution)/shard_map/rschk,rchkl->rschl/dot_general | solution.py:72
  93.5 0.9 copy.28
  94.5 1.9 %copy.29 = f32[1152,1,256]{0,2,1:T(8,128)S(1)} copy(f32[1152,1,256]{2,1,0:T(1,128)S(1)} %bitcast.38) | data formatting | bytes 2359296 | tf_op jit(solution)/shard_map/reshape | solution.py:74
  96.4 0.2 reduce-scatter.2.cloned.1.call-done
  96.6 1.4 %select_add_fusion = f32[1152,1,256]{0,2,1:T(8,128)S(1)} fusion(f32[1152,1,256]{0,2,1:T(8,128)S(1)} %copy.29, f32[1152,1,256]{0,2,1:T(8,128)} %reduce-scatter.2.cloned.1.call-done, pred[1152]{0:T(1024)(128)(4,1)S(1)} %add_compare_fusion), kind=kLoop, calls=%fused_computation.10 | loop fusion | flops 589824 | bytes 3540096 | tf_op jit(solution)/shard_map/add | solution.py:75
  98.0 2.1 %copy.30 = f32[1152,1,256]{2,1,0:T(1,128)} copy(f32[1152,1,256]{0,2,1:T(8,128)S(1)} %select_add_fusion) | data formatting | bytes 2359296 | tf_op jit(solution)/shard_map/add | solution.py:75
  (7 shorter events, 0.1 us)
Async XLA Ops:
  7.4 20.8 %copy-start = (s32[18,1,2]{0,2,1:T(2,128)S(1)}, s32[18,1,2]{0,2,1:T(2,128)}, u32[]{:S(2)}) copy-start(s32[18,1,2]{0,2,1:T(2,128)} %param.9) | copy-start | bytes 436
  7.4 72.5 %all-gather.4.cloned.1.call-start = ((), (), s32[]{:S(2)}) async-start(), calls=%async_computation.2 | async-start | bytes 4718592 | tf_op jit(solution)/shard_map/all_gather | solution.py:46
  20.8 75.8 %reduce-scatter.2.cloned.1.call-start = ((), (), s32[]{:S(2)}) async-start(), calls=%async_computation.1 | async-start | bytes 5898240 | tf_op jit(solution)/shard_map/reduce_scatter | solution.py:64
  20.8 9.5 %collective-permute-start = (s32[18,1,2]{0,2,1:T(2,128)}, s32[18,1,2]{0,2,1:T(2,128)S(1)}, u32[]{:S(2)}, u32[]{:S(2)}) collective-permute-start(s32[18,1,2]{0,2,1:T(2,128)} %param.9), channel_id=1, source_target_pairs={{0,4},{4,0},{1,5},{5,1},{2,6},{6,2},{3,7},{7,3},{8,12},{12,8},{9,1... | collective-permute-start | bytes 440 | tf_op jit(solution)/shard_map/ppermute | solution.py:12
  84.3 5.2 %collective-permute-start.1 = (f32[18,1,2,128,128]{4,3,2,0,1:T(8,128)}, f32[18,1,2,128,128]{4,3,2,0,1:T(8,128)}, u32[]{:S(2)}, u32[]{:S(2)}) collective-permute-start(f32[18,1,2,128,128]{4,3,2,0,1:T(8,128)} %bitcast.10), channel_id=1, source_target_pairs={{0,4},{4,0},{1,5},{5,1},{2,6},{6,2},{3,7},{7,3},{8,12},{12,8},{9,1... | collective-permute-start | bytes 7077896 | tf_op jit(solution)/shard_map/ppermute | solution.py:12
Sparse Core Ops, SparseCore 0:
  20.9 58.9 all-gather.3
Sparse Core Ops, SparseCore 1:
  42.9 53.7 reduce-scatter.1

commit v12 on v11

--- a/solution.py
+++ b/solution.py
@@ -42,8 +42,7 @@
     tile_cols = hole_width // col_tiles
     per_dev = ph_interaction.shape[0]
     ny, nz, nc = lax.axis_size("cy"), lax.axis_size("cz"), lax.axis_size("core")
-    by_y = lax.all_gather(ph_interaction, "cy", axis=0, tiled=False)
-    own = lax.all_gather(by_y, "cz", axis=0, tiled=False)
+    own = lax.all_gather(ph_interaction, ("cz", "cy"), axis=0, tiled=False)
     own = own.reshape((-1,) + ph_interaction.shape[1:])
     offset = lax.axis_index("ctr") * row_count
     positions = offset + jnp.arange(row_count, dtype=jnp.int32)

time: 108 us -> 124 us (1.15)
  waiting for transfers between devices: 38.3 us -> 66.3 us
  blocking collectives: 13.4 us -> 0 us
  starting transfers between devices: 4.81 us -> 6.68 us
    all_gather x1, waiting for transfers between devices: 36.8 us -> 64.3 us  [local(): own = lax.all_gather(ph_interaction, ('cz', 'cy'), axis=0, tiled=False)]
    all_gather x1 -> x0, blocking collectives: 13.4 us -> none  [local(): by_y = lax.all_gather(ph_interaction, 'cy', axis=0, tiled=False)]
    ppermute x2, starting transfers between devices: 4.76 us -> 6.64 us  [shift(): return lax.ppermute(x, axis, [(k, (k + step) % n) for k in range(n)])]
  transfers between devices with their start and end apart: 4 -> 4, of which waited for: 3 -> 2; matrix products, arithmetic and copies ran while one was open for 30% -> 26% of each run, Pallas kernels for 0% -> 0%
where the time goes in v12:
time: 124 us
  waiting for transfers between devices  66.3 us (53%)
  local copies, waits for them, and re-layouts  17.2 us (14%)
  matrix products  16.4 us (13%)
  between operations  15.6 us (13%)
  starting transfers between devices  6.68 us (5%)
  other arithmetic  1.62 us (1%)
    all_gather x1, waiting for transfers between devices, local(): own = lax.all_gather(ph_interaction, ('cz', 'cy'), axis=0, tiled=False)  64.3 us
    dot_general x1, matrix products, local(): jnp.einsum('crk,kch->rch', pair_interaction, lowered, preferred_element_t...  12.4 us
    ppermute x2, starting transfers between devices, shift(): return lax.ppermute(x, axis, [(k, (k + step) % n) for k in range(n)])  6.64 us
    gather x1, local copies, waits for them, and re-layouts, local(): from_sibling = shift(own[sib_slot], 'core', 1)  4.33 us
    dot_general x1, matrix products, local(): jnp.einsum('rschk,rchkl->rschl', blocks, chosen, precision=lax.Precision....  3.99 us
    gather x1, local copies, waits for them, and re-layouts, local(): own[slot]  2.89 us
    unnamed x3, local copies, waits for them, and re-layouts  2.6 us
  transfers between devices with their start and end apart: 4, of which 2 were waited for; matrix products, arithmetic and copies ran while one was open for 26% of the time, Pallas kernels for 0%

profile of v12, /device:TPU:1, one launch (start us, length us, event | category | flops | bytes accessed | tf_op | source)
XLA Modules:
  0.0 123.8 jit_solution(10420094170855274683)
XLA Ops:
  7.4 0.0 copy-start
  7.4 0.0 all-gather.3.cloned.1.call-start
  7.4 0.7 all-gather.3.cloned.1.call-update
  8.1 0.0 reduce-scatter.2.cloned.1.call-start
  8.1 3.3 %collective-permute-start = (s32[18,1,2]{0,2,1:T(2,128)}, s32[18,1,2]{0,2,1:T(2,128)S(1)}, u32[]{:S(2)}, u32[]{:S(2)}) collective-permute-start(s32[18,1,2]{0,2,1:T(2,128)} %param.9), channel_id=1, source_target_pairs={{0,4},{4,0},{1,5},{5,1},{2,6},{6,2},{3,7},{7,3},{8,12},{12,8},{9,1... | collective-permute-start | bytes 440 | tf_op jit(solution)/shard_map/ppermute | solution.py:12
  11.5 2.6 %copy.22 = f32[1152,1,256]{0,2,1:T(8,128)S(1)} copy(f32[1152,1,256]{2,1,0:T(1,128)} %param.5) | data formatting | bytes 2359296 | tf_op args[0]
  14.7 0.0 copy-done
  14.8 0.1 fusion.22
  14.9 2.0 %copy.23 = f32[1152,1,256]{2,1,0:T(1,128)S(1)} copy(f32[1152,1,256]{0,2,1:T(8,128)S(1)} %get-tuple-element.16) | data formatting | bytes 2359296 | tf_op jit(solution)/shard_map/jit(_where)/select_n | solution.py:50
  16.9 0.0 collective-permute-done
  16.9 12.4 %fusion.2 = f32[4608,1,256]{0,2,1:T(8,128)} fusion(bf16[1,4608,1152]{2,1,0:T(8,128)(2,1)} %param.6, bf16[1152,1,256]{0,2,1:T(8,128)(2,1)S(1)} %get-tuple-element.9), kind=kOutput, calls=%fused_computation.4 | convolution fusion | flops 2717908992 | bytes 15925248 | tf_op jit(solution)/shard_map/crk,kch->rch/dot_general | solution.py:64
  29.3 0.0 reduce-scatter.2.cloned.1.call-update
  29.4 0.1 copy.26
  29.5 0.1 reshape.55
  29.6 64.3 %all-gather.3.cloned.1.call-done = f32[64,128,128]{2,1,0:T(8,128)} async-done(((f32[2,128,128]{2,1,0:T(8,128)}), f32[64,128,128]{2,1,0:T(8,128)}) %all-gather.3.cloned.1.call-update) | async-done | bytes 4194320 | tf_op jit(solution)/shard_map/all_gather | solution.py:45
  93.8 4.3 %gather_fusion.1 = f32[36,128,128]{2,1,0:T(8,128)} fusion(f32[64,128,128]{2,1,0:T(8,128)} %all-gather.3.cloned.1.call-done, s32[1024]{0:T(1024)S(1)} %pad_clamp_fusion), kind=kCustom, calls=%fused_computation.1 | custom fusion | bytes 4718736 | tf_op jit(solution)/shard_map/gather | solution.py:69
  98.2 3.3 %collective-permute-start.1 = (f32[18,1,2,128,128]{4,3,2,0,1:T(8,128)}, f32[18,1,2,128,128]{4,3,2,0,1:T(8,128)}, u32[]{:S(2)}, u32[]{:S(2)}) collective-permute-start(f32[18,1,2,128,128]{4,3,2,0,1:T(8,128)} %bitcast.8), channel_id=1, source_target_pairs={{0,4},{4,0},{1,5},{5,1},{2,6},{6,2},{3,7},{7,3},{8,12},{12,8},{9,1... | collective-permute-start | bytes 7077896 | tf_op jit(solution)/shard_map/ppermute | solution.py:12
  101.5 0.1 copy.24
  101.6 0.1 copy.25
  101.7 0.1 reshape.47
  101.8 2.9 %gather_fusion = f32[36,128,128]{2,1,0:T(8,128)S(1)} fusion(f32[64,128,128]{2,1,0:T(8,128)} %all-gather.3.cloned.1.call-done, s32[1024]{0:T(1024)S(1)} %pad_clamp_fusion.1), kind=kCustom, calls=%fused_computation | custom fusion | bytes 4718736 | tf_op jit(solution)/shard_map/gather | solution.py:70
  104.7 1.3 %collective-permute-done.1 = f32[18,1,2,128,128]{4,3,2,0,1:T(8,128)} collective-permute-done((f32[18,1,2,128,128]{4,3,2,0,1:T(8,128)}, f32[18,1,2,128,128]{4,3,2,0,1:T(8,128)}, u32[]{:S(2)}, u32[]{:S(2)}) %collective-permute-start.1) | collective-permute-done | bytes 2359328 | tf_op jit(solution)/shard_map/ppermute | solution.py:12
  106.0 4.0 %fusion.8 = f32[18,64,1,2,128]{4,1,3,0,2:T(8,128)S(1)} fusion(f32[18,1,2,128,128]{4,3,2,0,1:T(8,128)S(1)} %bitcast.33, f32[18,1,2,128,128]{4,3,2,0,1:T(8,128)} %collective-permute-done.1, f32[18,64,2,128]{3,2,1,0:T(2,128)S(1)} %bitcast.35, pred[18,2]{1,0:T(8,128)(4,1)S(1)} %copy.24), kind=kOutput, calls=%fused_computation.8 | convolution fusion | flops 453574656 | bytes 7077924 | tf_op jit(solution)/shard_map/rschk,rchkl->rschl/dot_general | solution.py:71
  110.0 0.9 copy.28
  110.9 1.9 %copy.29 = f32[1152,1,256]{0,2,1:T(8,128)S(1)} copy(f32[1152,1,256]{2,1,0:T(1,128)S(1)} %bitcast.34) | data formatting | bytes 2359296 | tf_op jit(solution)/shard_map/reshape | solution.py:73
  112.9 0.0 reduce-scatter.2.cloned.1.call-done
  112.9 1.4 %select_add_fusion = f32[1152,1,256]{0,2,1:T(8,128)S(1)} fusion(f32[1152,1,256]{0,2,1:T(8,128)S(1)} %copy.29, f32[1152,1,256]{0,2,1:T(8,128)} %reduce-scatter.2.cloned.1.call-done, pred[1152]{0:T(1024)(128)(4,1)S(1)} %add_compare_fusion), kind=kLoop, calls=%fused_computation.10 | loop fusion | flops 589824 | bytes 3540096 | tf_op jit(solution)/shard_map/add | solution.py:74
  114.3 2.1 %copy.30 = f32[1152,1,256]{2,1,0:T(1,128)} copy(f32[1152,1,256]{0,2,1:T(8,128)S(1)} %select_add_fusion) | data formatting | bytes 2359296 | tf_op jit(solution)/shard_map/add | solution.py:74
  (7 shorter events, 0.1 us)
Async XLA Ops:
  7.4 7.4 %copy-start = (s32[18,1,2]{0,2,1:T(2,128)S(1)}, s32[18,1,2]{0,2,1:T(2,128)}, u32[]{:S(2)}) copy-start(s32[18,1,2]{0,2,1:T(2,128)} %param.9) | copy-start | bytes 436
  7.4 86.5 %all-gather.3.cloned.1.call-start = ((), (), s32[]{:S(2)}) async-start(), calls=%async_computation.2 | async-start | bytes 4325376 | tf_op jit(solution)/shard_map/all_gather | solution.py:45
  8.1 104.8 %reduce-scatter.2.cloned.1.call-start = ((), (), s32[]{:S(2)}) async-start(), calls=%async_computation.1 | async-start | bytes 5898240 | tf_op jit(solution)/shard_map/reduce_scatter | solution.py:63
  8.1 8.8 %collective-permute-start = (s32[18,1,2]{0,2,1:T(2,128)}, s32[18,1,2]{0,2,1:T(2,128)S(1)}, u32[]{:S(2)}, u32[]{:S(2)}) collective-permute-start(s32[18,1,2]{0,2,1:T(2,128)} %param.9), channel_id=1, source_target_pairs={{0,4},{4,0},{1,5},{5,1},{2,6},{6,2},{3,7},{7,3},{8,12},{12,8},{9,1... | collective-permute-start | bytes 440 | tf_op jit(solution)/shard_map/ppermute | solution.py:12
  98.2 7.8 %collective-permute-start.1 = (f32[18,1,2,128,128]{4,3,2,0,1:T(8,128)}, f32[18,1,2,128,128]{4,3,2,0,1:T(8,128)}, u32[]{:S(2)}, u32[]{:S(2)}) collective-permute-start(f32[18,1,2,128,128]{4,3,2,0,1:T(8,128)} %bitcast.8), channel_id=1, source_target_pairs={{0,4},{4,0},{1,5},{5,1},{2,6},{6,2},{3,7},{7,3},{8,12},{12,8},{9,1... | collective-permute-start | bytes 7077896 | tf_op jit(solution)/shard_map/ppermute | solution.py:12
Sparse Core Ops, SparseCore 0:
  10.8 83.0 all-gather.2
Sparse Core Ops, SparseCore 1:
  29.4 54.1 reduce-scatter.1

commit v13 on v11

--- a/solution.py
+++ b/solution.py
@@ -60,7 +60,7 @@
     slot, owner_core = place(ph_owner)
     sib_slot, _ = place(shift(ph_owner, "core", 1))
     blocks = masked.reshape(row_tiles, tile_rows, chan_count, col_tiles, tile_cols)
-    slot, sib_slot, blocks, lowered = lax.optimization_barrier((slot, sib_slot, blocks, lowered))
+    slot, sib_slot, lowered = lax.optimization_barrier((slot, sib_slot, lowered))
     ladder = lax.psum_scatter(
         jnp.einsum("crk,kch->rch", pair_interaction, lowered, preferred_element_type=jnp.float32),
         "ctr",

time: 108 us -> 108 us (level)
  local copies, waits for them, and re-layouts: 17.4 us -> 16.2 us
    all_gather x1, waiting for transfers between devices: 36.8 us -> 38.8 us  [local(): own = lax.all_gather(by_y, 'cz', axis=0, tiled=False)]
    select_n x1, local copies, waits for them, and re-layouts: 1.96 us -> 0.36 us  [local(): jnp.where(live_mask[:, :, None], amplitudes, jnp.zeros_like(amplitudes))]
  transfers between devices with their start and end apart: 4 -> 4, of which waited for: 3 -> 2; matrix products, arithmetic and copies ran while one was open for 30% -> 29% of each run, Pallas kernels for 0% -> 0%
where the time goes in v13:
time: 108 us; the launch traced here: 107 us
  waiting for transfers between devices  39.2 us (36%)
  matrix products  16.4 us (15%)
  local copies, waits for them, and re-layouts  16.2 us (15%)
  between operations  15.6 us (14%)
  blocking collectives  13.4 us (12%)
  starting transfers between devices  4.81 us (4%)
  other arithmetic  1.62 us (2%)
    all_gather x1, waiting for transfers between devices, local(): own = lax.all_gather(by_y, 'cz', axis=0, tiled=False)  38.8 us
    all_gather x1, blocking collectives, local(): by_y = lax.all_gather(ph_interaction, 'cy', axis=0, tiled=False)  13.4 us
    dot_general x1, matrix products, local(): jnp.einsum('crk,kch->rch', pair_interaction, lowered, preferred_element_t...  12.4 us
    ppermute x2, starting transfers between devices, shift(): return lax.ppermute(x, axis, [(k, (k + step) % n) for k in range(n)])  4.77 us
    gather x1, local copies, waits for them, and re-layouts, local(): from_sibling = shift(own[sib_slot], 'core', 1)  4.33 us
    dot_general x1, matrix products, local(): jnp.einsum('rschk,rchkl->rschl', blocks, chosen, precision=lax.Precision....  3.99 us
    gather x1, local copies, waits for them, and re-layouts, local(): own[slot]  2.89 us
    unnamed x3, local copies, waits for them, and re-layouts  2.6 us
  transfers between devices with their start and end apart: 4, of which 2 were waited for; matrix products, arithmetic and copies ran while one was open for 29% of the time, Pallas kernels for 0%

profile of v13, /device:TPU:1, one launch (start us, length us, event | category | flops | bytes accessed | tf_op | source)
XLA Modules:
  0.0 107.2 jit_solution(18032673946081049355)
XLA Ops:
  7.4 0.0 copy-start
  7.4 0.0 all-gather.4.cloned.1.call-start
  7.4 13.4 %all-gather = f32[8,128,128]{2,1,0:T(8,128)} all-gather(f32[2,128,128]{2,1,0:T(8,128)} %param.7), channel_id=2, replica_groups=mesh['cy'=4,'cz'=8,'core'=2,'ctr'=4] {'cy'}, dimensions={0}, use_global_device_ids=true | all-gather | bytes 655360 | tf_op jit(solution)/shard_map/all_gather | solution.py:45
  20.7 0.0 all-gather.4.cloned.1.call-update
  20.8 0.0 reduce-scatter.2.cloned.1.call-start
  20.8 4.1 %collective-permute-start = (s32[18,1,2]{0,2,1:T(2,128)}, s32[18,1,2]{0,2,1:T(2,128)S(1)}, u32[]{:S(2)}, u32[]{:S(2)}) collective-permute-start(s32[18,1,2]{0,2,1:T(2,128)} %param.9), channel_id=1, source_target_pairs={{0,4},{4,0},{1,5},{5,1},{2,6},{6,2},{3,7},{7,3},{8,12},{12,8},{9,1... | collective-permute-start | bytes 440 | tf_op jit(solution)/shard_map/ppermute | solution.py:12
  24.9 2.6 %copy.22 = f32[1152,1,256]{0,2,1:T(8,128)S(1)} copy(f32[1152,1,256]{2,1,0:T(1,128)} %param.5) | data formatting | bytes 2359296 | tf_op args[0]
  28.2 0.0 copy-done
  28.2 0.1 fusion.22
  28.4 0.0 collective-permute-done
  28.4 12.4 %fusion.2 = f32[4608,1,256]{0,2,1:T(8,128)} fusion(bf16[1,4608,1152]{2,1,0:T(8,128)(2,1)} %param.6, bf16[1152,1,256]{0,2,1:T(8,128)(2,1)S(1)} %get-tuple-element.8), kind=kOutput, calls=%fused_computation.4 | convolution fusion | flops 2717908992 | bytes 15925248 | tf_op jit(solution)/shard_map/crk,kch->rch/dot_general | solution.py:65
  40.8 0.0 reduce-scatter.2.cloned.1.call-update
  40.9 0.1 copy.25
  41.0 0.1 reshape.53
  41.1 38.8 %all-gather.4.cloned.1.call-done = f32[32,2,128,128]{3,2,1,0:T(8,128)} async-done(((f32[4,2,128,128]{3,2,1,0:T(8,128)}), f32[32,2,128,128]{3,2,1,0:T(8,128)}) %all-gather.4.cloned.1.call-update) | async-done | bytes 4194320 | tf_op jit(solution)/shard_map/all_gather | solution.py:46
  79.8 4.3 %gather_fusion.1 = f32[36,128,128]{2,1,0:T(8,128)} fusion(f32[64,128,128]{2,1,0:T(8,128)} %bitcast.36, s32[1024]{0:T(1024)S(1)} %pad_clamp_fusion), kind=kCustom, calls=%fused_computation.1 | custom fusion | bytes 4718736 | tf_op jit(solution)/shard_map/gather | solution.py:70
  84.2 0.7 collective-permute-start.1
  84.8 0.4 copy.26
  85.2 0.6 reshape.41
  85.8 0.1 copy.23
  85.9 0.1 copy.24
  86.0 0.1 reshape.45
  86.2 2.9 %gather_fusion = f32[36,128,128]{2,1,0:T(8,128)S(1)} fusion(f32[64,128,128]{2,1,0:T(8,128)} %bitcast.37, s32[1024]{0:T(1024)S(1)} %pad_clamp_fusion.1), kind=kCustom, calls=%fused_computation | custom fusion | bytes 4718736 | tf_op jit(solution)/shard_map/gather | solution.py:71
  89.0 0.3 collective-permute-done.1
  89.4 4.0 %fusion.8 = f32[18,64,1,2,128]{4,1,3,0,2:T(8,128)S(1)} fusion(f32[18,1,2,128,128]{4,3,2,0,1:T(8,128)S(1)} %bitcast.35, f32[18,1,2,128,128]{4,3,2,0,1:T(8,128)} %collective-permute-done.1, f32[18,64,2,128]{3,2,1,0:T(2,128)S(1)} %reshape.41, pred[18,2]{1,0:T(8,128)(4,1)S(1)} %copy.23), kind=kOutput, calls=%fused_computation.8 | convolution fusion | flops 453574656 | bytes 7077924 | tf_op jit(solution)/shard_map/rschk,rchkl->rschl/dot_general | solution.py:72
  93.4 0.9 copy.28
  94.3 1.9 %copy.29 = f32[1152,1,256]{0,2,1:T(8,128)S(1)} copy(f32[1152,1,256]{2,1,0:T(1,128)S(1)} %bitcast.38) | data formatting | bytes 2359296 | tf_op jit(solution)/shard_map/reshape | solution.py:74
  96.2 0.0 reduce-scatter.2.cloned.1.call-done
  96.3 1.4 %select_add_fusion = f32[1152,1,256]{0,2,1:T(8,128)S(1)} fusion(f32[1152,1,256]{0,2,1:T(8,128)S(1)} %copy.29, f32[1152,1,256]{0,2,1:T(8,128)} %reduce-scatter.2.cloned.1.call-done, pred[1152]{0:T(1024)(128)(4,1)S(1)} %add_compare_fusion), kind=kLoop, calls=%fused_computation.10 | loop fusion | flops 589824 | bytes 3540096 | tf_op jit(solution)/shard_map/add | solution.py:75
  97.7 2.1 %copy.30 = f32[1152,1,256]{2,1,0:T(1,128)} copy(f32[1152,1,256]{0,2,1:T(8,128)S(1)} %select_add_fusion) | data formatting | bytes 2359296 | tf_op jit(solution)/shard_map/add | solution.py:75
  (7 shorter events, 0.1 us)
Async XLA Ops:
  7.4 20.8 %copy-start = (s32[18,1,2]{0,2,1:T(2,128)S(1)}, s32[18,1,2]{0,2,1:T(2,128)}, u32[]{:S(2)}) copy-start(s32[18,1,2]{0,2,1:T(2,128)} %param.9) | copy-start | bytes 436
  7.4 72.5 %all-gather.4.cloned.1.call-start = ((), (), s32[]{:S(2)}) async-start(), calls=%async_computation.2 | async-start | bytes 4718592 | tf_op jit(solution)/shard_map/all_gather | solution.py:46
  20.8 75.5 %reduce-scatter.2.cloned.1.call-start = ((), (), s32[]{:S(2)}) async-start(), calls=%async_computation.1 | async-start | bytes 5898240 | tf_op jit(solution)/shard_map/reduce_scatter | solution.py:64
  20.8 7.5 %collective-permute-start = (s32[18,1,2]{0,2,1:T(2,128)}, s32[18,1,2]{0,2,1:T(2,128)S(1)}, u32[]{:S(2)}, u32[]{:S(2)}) collective-permute-start(s32[18,1,2]{0,2,1:T(2,128)} %param.9), channel_id=1, source_target_pairs={{0,4},{4,0},{1,5},{5,1},{2,6},{6,2},{3,7},{7,3},{8,12},{12,8},{9,1... | collective-permute-start | bytes 440 | tf_op jit(solution)/shard_map/ppermute | solution.py:12
  84.2 5.2 %collective-permute-start.1 = (f32[18,1,2,128,128]{4,3,2,0,1:T(8,128)}, f32[18,1,2,128,128]{4,3,2,0,1:T(8,128)}, u32[]{:S(2)}, u32[]{:S(2)}) collective-permute-start(f32[18,1,2,128,128]{4,3,2,0,1:T(8,128)} %bitcast.9), channel_id=1, source_target_pairs={{0,4},{4,0},{1,5},{5,1},{2,6},{6,2},{3,7},{7,3},{8,12},{12,8},{9,1... | collective-permute-start | bytes 7077896 | tf_op jit(solution)/shard_map/ppermute | solution.py:12
Sparse Core Ops, SparseCore 0:
  20.9 58.9 all-gather.3
Sparse Core Ops, SparseCore 1:
  40.9 53.7 reduce-scatter.1

commit v14 on v13

--- a/solution.py
+++ b/solution.py
@@ -70,7 +70,7 @@
     from_sibling = shift(own[sib_slot], "core", 1)
     chosen = jnp.where((owner_core == my_core)[..., None, None], own[slot], from_sibling)
     cycle = jnp.einsum(
-        "rschk,rchkl->rschl", blocks, chosen, precision=lax.Precision.HIGHEST
+        "rschk,rchkl->rschl", blocks, chosen, precision=lax.Precision.HIGH
     ).reshape(row_count, chan_count, hole_width)
     return jnp.where(live_mask[:, :, None], ladder, jnp.zeros_like(ladder)) + cycle
 

time: 108 us -> 106 us (0.981)
  matrix products: 16.4 us -> 15.3 us
    dot_general x1, matrix products: 3.99 us -> 2.85 us  [local(): jnp.einsum('rschk,rchkl->rschl', blocks, chosen, precision=lax.Precision....]
  transfers between devices with their start and end apart: 4 -> 4, of which waited for: 2 -> 2; matrix products, arithmetic and copies ran while one was open for 29% -> 28% of each run, Pallas kernels for 0% -> 0%
where the time goes in v14:
time: 106 us
  waiting for transfers between devices  39.2 us (37%)
  local copies, waits for them, and re-layouts  16.2 us (15%)
  between operations  15.6 us (15%)
  matrix products  15.3 us (14%)
  blocking collectives  13.4 us (13%)
  starting transfers between devices  4.81 us (5%)
  other arithmetic  1.62 us (2%)
    all_gather x1, waiting for transfers between devices, local(): own = lax.all_gather(by_y, 'cz', axis=0, tiled=False)  38.8 us
    all_gather x1, blocking collectives, local(): by_y = lax.all_gather(ph_interaction, 'cy', axis=0, tiled=False)  13.4 us
    dot_general x1, matrix products, local(): jnp.einsum('crk,kch->rch', pair_interaction, lowered, preferred_element_t...  12.4 us
    ppermute x2, starting transfers between devices, shift(): return lax.ppermute(x, axis, [(k, (k + step) % n) for k in range(n)])  4.77 us
    gather x1, local copies, waits for them, and re-layouts, local(): from_sibling = shift(own[sib_slot], 'core', 1)  4.33 us
    gather x1, local copies, waits for them, and re-layouts, local(): own[slot]  2.89 us
    dot_general x1, matrix products, local(): jnp.einsum('rschk,rchkl->rschl', blocks, chosen, precision=lax.Precision....  2.85 us
    unnamed x3, local copies, waits for them, and re-layouts  2.6 us
  transfers between devices with their start and end apart: 4, of which 2 were waited for; matrix products, arithmetic and copies ran while one was open for 28% of the time, Pallas kernels for 0%

profile of v14, /device:TPU:1, one launch (start us, length us, event | category | flops | bytes accessed | tf_op | source)
XLA Modules:
  0.0 106.1 jit_solution(3548832733472365329)
XLA Ops:
  7.4 0.0 copy-start
  7.4 0.0 all-gather.4.cloned.1.call-start
  7.4 13.4 %all-gather = f32[8,128,128]{2,1,0:T(8,128)} all-gather(f32[2,128,128]{2,1,0:T(8,128)} %param.7), channel_id=2, replica_groups=mesh['cy'=4,'cz'=8,'core'=2,'ctr'=4] {'cy'}, dimensions={0}, use_global_device_ids=true | all-gather | bytes 655360 | tf_op jit(solution)/shard_map/all_gather | solution.py:45
  20.7 0.0 all-gather.4.cloned.1.call-update
  20.8 0.0 reduce-scatter.2.cloned.1.call-start
  20.8 4.1 %collective-permute-start = (s32[18,1,2]{0,2,1:T(2,128)}, s32[18,1,2]{0,2,1:T(2,128)S(1)}, u32[]{:S(2)}, u32[]{:S(2)}) collective-permute-start(s32[18,1,2]{0,2,1:T(2,128)} %param.9), channel_id=1, source_target_pairs={{0,4},{4,0},{1,5},{5,1},{2,6},{6,2},{3,7},{7,3},{8,12},{12,8},{9,1... | collective-permute-start | bytes 440 | tf_op jit(solution)/shard_map/ppermute | solution.py:12
  24.9 2.6 %copy.22 = f32[1152,1,256]{0,2,1:T(8,128)S(1)} copy(f32[1152,1,256]{2,1,0:T(1,128)} %param.5) | data formatting | bytes 2359296 | tf_op args[0]
  28.2 0.0 copy-done
  28.2 0.1 fusion.22
  28.4 0.0 collective-permute-done
  28.4 12.4 %fusion.2 = f32[4608,1,256]{0,2,1:T(8,128)} fusion(bf16[1,4608,1152]{2,1,0:T(8,128)(2,1)} %param.6, bf16[1152,1,256]{0,2,1:T(8,128)(2,1)S(1)} %get-tuple-element.8), kind=kOutput, calls=%fused_computation.4 | convolution fusion | flops 2717908992 | bytes 15925248 | tf_op jit(solution)/shard_map/crk,kch->rch/dot_general | solution.py:65
  40.8 0.0 reduce-scatter.2.cloned.1.call-update
  40.9 0.1 copy.25
  41.0 0.1 reshape.53
  41.1 38.8 %all-gather.4.cloned.1.call-done = f32[32,2,128,128]{3,2,1,0:T(8,128)} async-done(((f32[4,2,128,128]{3,2,1,0:T(8,128)}), f32[32,2,128,128]{3,2,1,0:T(8,128)}) %all-gather.4.cloned.1.call-update) | async-done | bytes 4194320 | tf_op jit(solution)/shard_map/all_gather | solution.py:46
  79.8 4.3 %gather_fusion.1 = f32[36,128,128]{2,1,0:T(8,128)} fusion(f32[64,128,128]{2,1,0:T(8,128)} %bitcast.36, s32[1024]{0:T(1024)S(1)} %pad_clamp_fusion), kind=kCustom, calls=%fused_computation.1 | custom fusion | bytes 4718736 | tf_op jit(solution)/shard_map/gather | solution.py:70
  84.2 0.7 collective-permute-start.1
  84.8 0.4 copy.26
  85.2 0.6 reshape.41
  85.8 0.1 copy.23
  85.9 0.1 copy.24
  86.0 0.1 reshape.45
  86.2 2.9 %gather_fusion = f32[36,128,128]{2,1,0:T(8,128)S(1)} fusion(f32[64,128,128]{2,1,0:T(8,128)} %bitcast.37, s32[1024]{0:T(1024)S(1)} %pad_clamp_fusion.1), kind=kCustom, calls=%fused_computation | custom fusion | bytes 4718736 | tf_op jit(solution)/shard_map/gather | solution.py:71
  89.0 0.3 collective-permute-done.1
  89.4 2.8 %fusion.8 = f32[18,64,1,2,128]{4,1,3,0,2:T(8,128)S(1)} fusion(f32[18,1,2,128,128]{4,3,2,0,1:T(8,128)S(1)} %bitcast.35, f32[18,1,2,128,128]{4,3,2,0,1:T(8,128)} %collective-permute-done.1, f32[18,64,2,128]{3,2,1,0:T(2,128)S(1)} %reshape.41, pred[18,2]{1,0:T(8,128)(4,1)S(1)} %copy.23), kind=kOutput, calls=%fused_computation.8 | convolution fusion | flops 227082240 | bytes 7077924 | tf_op jit(solution)/shard_map/rschk,rchkl->rschl/dot_general | solution.py:72
  92.2 0.9 copy.28
  93.1 1.9 %copy.29 = f32[1152,1,256]{0,2,1:T(8,128)S(1)} copy(f32[1152,1,256]{2,1,0:T(1,128)S(1)} %bitcast.38) | data formatting | bytes 2359296 | tf_op jit(solution)/shard_map/reshape | solution.py:74
  95.1 0.0 reduce-scatter.2.cloned.1.call-done
  95.1 1.4 %select_add_fusion = f32[1152,1,256]{0,2,1:T(8,128)S(1)} fusion(f32[1152,1,256]{0,2,1:T(8,128)S(1)} %copy.29, f32[1152,1,256]{0,2,1:T(8,128)} %reduce-scatter.2.cloned.1.call-done, pred[1152]{0:T(1024)(128)(4,1)S(1)} %add_compare_fusion), kind=kLoop, calls=%fused_computation.10 | loop fusion | flops 589824 | bytes 3540096 | tf_op jit(solution)/shard_map/add | solution.py:75
  96.5 2.1 %copy.30 = f32[1152,1,256]{2,1,0:T(1,128)} copy(f32[1152,1,256]{0,2,1:T(8,128)S(1)} %select_add_fusion) | data formatting | bytes 2359296 | tf_op jit(solution)/shard_map/add | solution.py:75
  (7 shorter events, 0.1 us)
Async XLA Ops:
  7.4 20.8 %copy-start = (s32[18,1,2]{0,2,1:T(2,128)S(1)}, s32[18,1,2]{0,2,1:T(2,128)}, u32[]{:S(2)}) copy-start(s32[18,1,2]{0,2,1:T(2,128)} %param.9) | copy-start | bytes 436
  7.4 72.5 %all-gather.4.cloned.1.call-start = ((), (), s32[]{:S(2)}) async-start(), calls=%async_computation.2 | async-start | bytes 4718592 | tf_op jit(solution)/shard_map/all_gather | solution.py:46
  20.8 74.4 %reduce-scatter.2.cloned.1.call-start = ((), (), s32[]{:S(2)}) async-start(), calls=%async_computation.1 | async-start | bytes 5898240 | tf_op jit(solution)/shard_map/reduce_scatter | solution.py:64
  20.8 7.5 %collective-permute-start = (s32[18,1,2]{0,2,1:T(2,128)}, s32[18,1,2]{0,2,1:T(2,128)S(1)}, u32[]{:S(2)}, u32[]{:S(2)}) collective-permute-start(s32[18,1,2]{0,2,1:T(2,128)} %param.9), channel_id=1, source_target_pairs={{0,4},{4,0},{1,5},{5,1},{2,6},{6,2},{3,7},{7,3},{8,12},{12,8},{9,1... | collective-permute-start | bytes 440 | tf_op jit(solution)/shard_map/ppermute | solution.py:12
  84.2 5.2 %collective-permute-start.1 = (f32[18,1,2,128,128]{4,3,2,0,1:T(8,128)}, f32[18,1,2,128,128]{4,3,2,0,1:T(8,128)}, u32[]{:S(2)}, u32[]{:S(2)}) collective-permute-start(f32[18,1,2,128,128]{4,3,2,0,1:T(8,128)} %bitcast.9), channel_id=1, source_target_pairs={{0,4},{4,0},{1,5},{5,1},{2,6},{6,2},{3,7},{7,3},{8,12},{12,8},{9,1... | collective-permute-start | bytes 7077896 | tf_op jit(solution)/shard_map/ppermute | solution.py:12
Sparse Core Ops, SparseCore 0:
  20.9 58.9 all-gather.3
Sparse Core Ops, SparseCore 1:
  40.9 53.7 reduce-scatter.1

commit v15 on v14

--- a/solution.py
+++ b/solution.py
@@ -4,7 +4,7 @@
 from jax.sharding import Mesh
 from jax.sharding import PartitionSpec as P
 
-CHAN = ("cy", "cz", "core")
+CHAN = ("cy", "czh", "czl", "core")
 
 
 def shift(x, axis, step):
@@ -41,9 +41,11 @@
     tile_rows = row_count // row_tiles
     tile_cols = hole_width // col_tiles
     per_dev = ph_interaction.shape[0]
-    ny, nz, nc = lax.axis_size("cy"), lax.axis_size("cz"), lax.axis_size("core")
+    ny, nc = lax.axis_size("cy"), lax.axis_size("core")
+    nz = lax.axis_size("czh") * lax.axis_size("czl")
     by_y = lax.all_gather(ph_interaction, "cy", axis=0, tiled=False)
-    own = lax.all_gather(by_y, "cz", axis=0, tiled=False)
+    near = lax.all_gather(by_y, "czl", axis=0, tiled=False)
+    own = lax.all_gather(near, "czh", axis=0, tiled=False)
     own = own.reshape((-1,) + ph_interaction.shape[1:])
     offset = lax.axis_index("ctr") * row_count
     positions = offset + jnp.arange(row_count, dtype=jnp.int32)
@@ -80,7 +82,7 @@
     cores = 2
     cz = 8
     fine = Mesh(
-        mesh.devices.reshape(chan_size // (cz * cores), cz, cores, ctr_size),
+        mesh.devices.reshape(chan_size // (cz * cores), 2, cz // 2, cores, ctr_size),
         CHAN + ("ctr",),
     )
     in_specs = (

time: 106 us -> 215 us (2.03)
  waiting for transfers between devices: 39.2 us -> 152 us
  starting transfers between devices: 4.81 us -> 1.84 us
    all_gather x1 -> x2, waiting for transfers between devices: 38.8 us -> 151 us  [the longest x1 96.9 us: local(): own = lax.all_gather(near, 'czh', axis=0, tiled=False)]
    ppermute x2, starting transfers between devices: 4.77 us -> 1.75 us  [shift(): return lax.ppermute(x, axis, [(k, (k + step) % n) for k in range(n)])]
  transfers between devices with their start and end apart: 4 -> 5, of which waited for: 2 -> 3; matrix products, arithmetic and copies ran while one was open for 28% -> 13% of each run, Pallas kernels for 0% -> 0%
where the time goes in v15:
time: 215 us
  waiting for transfers between devices  152 us (71%)
  local copies, waits for them, and re-layouts  15.6 us (7%)
  between operations  15.6 us (7%)
  matrix products  15.3 us (7%)
  blocking collectives  13.4 us (6%)
    all_gather x1, waiting for transfers between devices, local(): own = lax.all_gather(near, 'czh', axis=0, tiled=False)  96.9 us
    all_gather x1, waiting for transfers between devices, local(): near = lax.all_gather(by_y, 'czl', axis=0, tiled=False)  54.3 us
    all_gather x1, blocking collectives, local(): by_y = lax.all_gather(ph_interaction, 'cy', axis=0, tiled=False)  13.4 us
    dot_general x1, matrix products, local(): jnp.einsum('crk,kch->rch', pair_interaction, lowered, preferred_element_t...  12.4 us
    gather x1, local copies, waits for them, and re-layouts, local(): from_sibling = shift(own[sib_slot], 'core', 1)  4.31 us
  transfers between devices with their start and end apart: 5, of which 3 were waited for; matrix products, arithmetic and copies ran while one was open for 13% of the time, Pallas kernels for 0%

profile of v15, /device:TPU:1, one launch (start us, length us, event | category | flops | bytes accessed | tf_op | source)
XLA Modules:
  0.0 214.8 jit_solution(2840389412022251161)
XLA Ops:
  7.4 0.0 all-gather.6.cloned.1.call-start
  7.4 13.4 %all-gather = f32[8,128,128]{2,1,0:T(8,128)} all-gather(f32[2,128,128]{2,1,0:T(8,128)} %param.7), channel_id=2, replica_groups=mesh['cy'=4,'czh'=2,'czl'=4,'core'=2,'ctr'=4] {'cy'}, dimensions={0}, use_global_device_ids=true | all-gather | bytes 655360 | tf_op jit(solution)/shard_map/all_gather | solution.py:46
  20.7 0.0 all-gather.6.cloned.1.call-update
  20.8 0.0 all-gather.8.cloned.1.call-start
  20.8 54.3 %all-gather.6.cloned.1.call-done = f32[16,2,128,128]{3,2,1,0:T(8,128)} async-done(((f32[4,2,128,128]{3,2,1,0:T(8,128)}), f32[16,2,128,128]{3,2,1,0:T(8,128)}) %all-gather.6.cloned.1.call-update) | async-done | bytes 2097168 | tf_op jit(solution)/shard_map/all_gather | solution.py:47
  75.1 0.0 all-gather.8.cloned.1.call-update
  75.1 0.0 reduce-scatter.2.cloned.1.call-start
  75.1 0.0 copy-done.1
  75.2 1.1 collective-permute-start
  76.2 1.9 copy.22
  78.8 0.1 fusion.22
  79.0 0.0 collective-permute-done
  79.0 12.4 %fusion.2 = f32[4608,1,256]{0,2,1:T(8,128)} fusion(bf16[1,4608,1152]{2,1,0:T(8,128)(2,1)} %param.6, bf16[1152,1,256]{0,2,1:T(8,128)(2,1)S(1)} %get-tuple-element.8), kind=kOutput, calls=%fused_computation.4 | convolution fusion | flops 2717908992 | bytes 15925248 | tf_op jit(solution)/shard_map/crk,kch->rch/dot_general | solution.py:67
  91.5 0.0 reduce-scatter.2.cloned.1.call-update
  91.5 0.1 copy.25
  91.6 0.1 reshape.53
  91.7 96.9 %all-gather.8.cloned.1.call-done = f32[8,4,2,128,128]{4,3,2,1,0:T(8,128)} async-done(((f32[4,4,2,128,128]{4,3,2,1,0:T(8,128)}), f32[8,4,2,128,128]{4,3,2,1,0:T(8,128)}) %all-gather.8.cloned.1.call-update) | async-done | bytes 4194320 | tf_op jit(solution)/shard_map/all_gather | solution.py:48
  188.6 4.3 %gather_fusion.1 = f32[36,128,128]{2,1,0:T(8,128)} fusion(f32[64,128,128]{2,1,0:T(8,128)} %bitcast.37, s32[1024]{0:T(1024)S(1)} %pad_clamp_fusion), kind=kCustom, calls=%fused_computation.1 | custom fusion | bytes 4718736 | tf_op jit(solution)/shard_map/gather | solution.py:72
  192.9 0.7 collective-permute-start.1
  193.6 0.4 copy.26
  194.0 0.6 reshape.41
  194.6 0.1 copy.23
  194.7 0.1 copy.24
  194.8 0.1 reshape.45
  194.9 2.9 %gather_fusion = f32[36,128,128]{2,1,0:T(8,128)S(1)} fusion(f32[64,128,128]{2,1,0:T(8,128)} %bitcast.38, s32[1024]{0:T(1024)S(1)} %pad_clamp_fusion.1), kind=kCustom, calls=%fused_computation | custom fusion | bytes 4718736 | tf_op jit(solution)/shard_map/gather | solution.py:73
  197.8 0.3 collective-permute-done.1
  198.1 2.8 %fusion.8 = f32[18,64,1,2,128]{4,1,3,0,2:T(8,128)S(1)} fusion(f32[18,1,2,128,128]{4,3,2,0,1:T(8,128)S(1)} %bitcast.36, f32[18,1,2,128,128]{4,3,2,0,1:T(8,128)} %collective-permute-done.1, f32[18,64,2,128]{3,2,1,0:T(2,128)S(1)} %reshape.41, pred[18,2]{1,0:T(8,128)(4,1)S(1)} %copy.23), kind=kOutput, calls=%fused_computation.8 | convolution fusion | flops 227082240 | bytes 7077924 | tf_op jit(solution)/shard_map/rschk,rchkl->rschl/dot_general | solution.py:74
  201.0 0.9 copy.28
  201.9 1.9 copy.29
  203.9 0.0 reduce-scatter.2.cloned.1.call-done
  203.9 1.4 select_add_fusion
  205.3 2.1 copy.30
  (10 shorter events, 0.1 us)
Async XLA Ops:
  7.4 67.8 %copy-start.1 = (s32[18,1,2]{0,2,1:T(2,128)S(1)}, s32[18,1,2]{0,2,1:T(2,128)}, u32[]{:S(2)}) copy-start(s32[18,1,2]{0,2,1:T(2,128)} %param.9) | copy-start | bytes 436
  7.4 68.9 %copy-start = (f32[1152,1,256]{2,1,0:T(1,128)S(1)}, f32[1152,1,256]{2,1,0:T(1,128)}, u32[]{:S(2)}) copy-start(f32[1152,1,256]{2,1,0:T(1,128)} %param.5) | copy-start | bytes 3538948
  7.4 67.7 %all-gather.6.cloned.1.call-start = ((), (), s32[]{:S(2)}) async-start(), calls=%async_computation.2 | async-start | bytes 2621440 | tf_op jit(solution)/shard_map/all_gather | solution.py:47
  20.8 167.9 %all-gather.8.cloned.1.call-start = ((), (), s32[]{:S(2)}) async-start(), calls=%async_computation.3 | async-start | bytes 6291456 | tf_op jit(solution)/shard_map/all_gather | solution.py:48
  75.1 128.8 %reduce-scatter.2.cloned.1.call-start = ((), (), s32[]{:S(2)}) async-start(), calls=%async_computation.1 | async-start | bytes 5898240 | tf_op jit(solution)/shard_map/reduce_scatter | solution.py:66
  75.2 3.8 %collective-permute-start = (s32[18,1,2]{0,2,1:T(2,128)S(1)}, s32[18,1,2]{0,2,1:T(2,128)S(1)}, u32[]{:S(2)}, u32[]{:S(2)}) collective-permute-start(s32[18,1,2]{0,2,1:T(2,128)S(1)} %copy-done.1), channel_id=1, source_target_pairs={{0,4},{4,0},{1,5},{5,1},{2,6},{6,2},{3,7},{7,3},{8,12},{12,8},{9,1... | collective-permute-start | bytes 440 | tf_op jit(solution)/shard_map/ppermute | solution.py:12
  192.9 5.2 %collective-permute-start.1 = (f32[18,1,2,128,128]{4,3,2,0,1:T(8,128)}, f32[18,1,2,128,128]{4,3,2,0,1:T(8,128)}, u32[]{:S(2)}, u32[]{:S(2)}) collective-permute-start(f32[18,1,2,128,128]{4,3,2,0,1:T(8,128)} %bitcast.10), channel_id=1, source_target_pairs={{0,4},{4,0},{1,5},{5,1},{2,6},{6,2},{3,7},{7,3},{8,12},{12,8},{9,1... | collective-permute-start | bytes 7077896 | tf_op jit(solution)/shard_map/ppermute | solution.py:12
Sparse Core Ops, SparseCore 0:
  20.9 54.1 all-gather.5
  76.9 111.7 all-gather.7
Sparse Core Ops, SparseCore 1:
  91.6 52.3 reduce-scatter.1

commit v16 on v14

--- a/solution.py
+++ b/solution.py
@@ -42,7 +42,8 @@
     tile_cols = hole_width // col_tiles
     per_dev = ph_interaction.shape[0]
     ny, nz, nc = lax.axis_size("cy"), lax.axis_size("cz"), lax.axis_size("core")
-    by_y = lax.all_gather(ph_interaction, "cy", axis=0, tiled=False)
+    spread = jnp.zeros((ny,) + ph_interaction.shape, ph_interaction.dtype)
+    by_y = lax.psum(spread.at[lax.axis_index("cy")].set(ph_interaction), "cy")
     own = lax.all_gather(by_y, "cz", axis=0, tiled=False)
     own = own.reshape((-1,) + ph_interaction.shape[1:])
     offset = lax.axis_index("ctr") * row_count

time: 106 us -> 147 us (1.39)
  waiting for transfers between devices: 39.2 us -> 91.5 us
  blocking collectives: 13.4 us -> 0 us
  other arithmetic: 1.62 us -> 4.75 us
    psum x0 -> x1, waiting for transfers between devices: none -> 50.2 us  [local(): by_y = lax.psum(spread.at[lax.axis_index('cy')].set(ph_interaction), 'cy')]
    all_gather x1 -> x0, blocking collectives: 13.4 us -> none  [local(): by_y = lax.all_gather(ph_interaction, 'cy', axis=0, tiled=False)]
    all_gather x1, waiting for transfers between devices: 38.8 us -> 40.9 us  [local(): own = lax.all_gather(by_y, 'cz', axis=0, tiled=False)]
    scatter x0 -> x1, other arithmetic: none -> 1.6 us  [local(): by_y = lax.psum(spread.at[lax.axis_index('cy')].set(ph_interaction), 'cy')]
    another operation x0 -> x1, other arithmetic: none -> 1.53 us
    ppermute x2, starting transfers between devices: 4.77 us -> 3.25 us  [shift(): return lax.ppermute(x, axis, [(k, (k + step) % n) for k in range(n)])]
  transfers between devices with their start and end apart: 4 -> 5, of which waited for: 2 -> 3; matrix products, arithmetic and copies ran while one was open for 28% -> 20% of each run, Pallas kernels for 0% -> 0%
where the time goes in v16:
time: 147 us
  waiting for transfers between devices  91.5 us (62%)
  local copies, waits for them, and re-layouts  16.4 us (11%)
  between operations  15.6 us (11%)
  matrix products  15.3 us (10%)
  other arithmetic  4.75 us (3%)
  starting transfers between devices  3.34 us (2%)
    psum x1, waiting for transfers between devices, local(): by_y = lax.psum(spread.at[lax.axis_index('cy')].set(ph_interaction), 'cy')  50.2 us
    all_gather x1, waiting for transfers between devices, local(): own = lax.all_gather(by_y, 'cz', axis=0, tiled=False)  40.9 us
    dot_general x1, matrix products, local(): jnp.einsum('crk,kch->rch', pair_interaction, lowered, preferred_element_t...  12.4 us
    gather x1, local copies, waits for them, and re-layouts, local(): from_sibling = shift(own[sib_slot], 'core', 1)  4.35 us
    ppermute x2, starting transfers between devices, shift(): return lax.ppermute(x, axis, [(k, (k + step) % n) for k in range(n)])  3.25 us
  transfers between devices with their start and end apart: 5, of which 3 were waited for; matrix products, arithmetic and copies ran while one was open for 20% of the time, Pallas kernels for 0%

profile of v16, /device:TPU:1, one launch (start us, length us, event | category | flops | bytes accessed | tf_op | source)
XLA Modules:
  0.0 147.0 jit_solution(13383341050325717593)
XLA Ops:
  7.4 1.5 %and_reduce_fusion = pred[]{:T(512)} fusion(s32[4]{0:T(128)} %constant.137.clone.1, s32[1]{0:T(128)} %constant.136.clone.1, s32[1]{0:T(128)} %bitcast.6), kind=kLoop, calls=%fused_computation.24 | loop fusion | flops 27 | bytes 25 | tf_op jit(solution)/shard_map/reduce.1
  8.9 1.6 %bitcast_dynamic-update-slice_fusion = f32[1,4,2,128,128]{4,3,2,1,0:T(8,128)S(1)} fusion(f32[1,4,2,128,128]{4,3,2,1,0:T(8,128)S(1)} %broadcast.106, s32[]{:T(128)} %select_n.78, f32[2,128,128]{2,1,0:T(8,128)} %param.9, pred[]{:T(512)} %and_reduce_fusion), kind=kLoop, calls=%fused_computation.14 | loop fusion | flops 32768 | bytes 262149 | tf_op jit(solution)/shard_map/scatter | solution.py:46
  10.6 0.0 copy-start
  10.6 0.8 copy-done
  11.3 0.0 all-reduce.2.cloned.1.call-update
  11.4 0.0 all-gather.2.cloned.1.call-start
  11.4 50.2 %all-reduce.2.cloned.1.call-done = f32[1,4,2,128,128]{4,3,2,1,0:T(8,128)} async-done(((f32[1,4,2,128,128]{4,3,2,1,0:T(8,128)}), f32[1,4,2,128,128]{4,3,2,1,0:T(8,128)}) %all-reduce.2.cloned.1.call-update) | async-done | bytes 524304 | tf_op jit(solution)/shard_map/psum | solution.py:46
  61.6 0.0 all-gather.2.cloned.1.call-update
  61.7 0.0 reduce-scatter.2.cloned.1.call-start
  61.7 2.6 %collective-permute-start = (s32[18,1,2]{0,2,1:T(2,128)}, s32[18,1,2]{0,2,1:T(2,128)S(1)}, u32[]{:S(2)}, u32[]{:S(2)}) collective-permute-start(s32[18,1,2]{0,2,1:T(2,128)} %param.11), channel_id=1, source_target_pairs={{0,4},{4,0},{1,5},{5,1},{2,6},{6,2},{3,7},{7,3},{8,12},{12,8},{9,1... | collective-permute-start | bytes 440 | tf_op jit(solution)/shard_map/ppermute | solution.py:12
  64.3 1.9 %copy.22 = f32[1152,1,256]{0,2,1:T(8,128)S(1)} copy(f32[1152,1,256]{2,1,0:T(1,128)S(1)} %copy-done.1) | data formatting | bytes 2359296 | tf_op args[0]
  66.9 0.1 fusion.22
  67.1 12.4 %fusion.2 = f32[4608,1,256]{0,2,1:T(8,128)} fusion(bf16[1,4608,1152]{2,1,0:T(8,128)(2,1)} %param.8, bf16[1152,1,256]{0,2,1:T(8,128)(2,1)S(1)} %get-tuple-element.20), kind=kOutput, calls=%fused_computation.4 | convolution fusion | flops 2717908992 | bytes 15925248 | tf_op jit(solution)/shard_map/crk,kch->rch/dot_general | solution.py:66
  79.6 0.0 reduce-scatter.2.cloned.1.call-update
  79.6 0.1 copy.25
  79.7 0.1 reshape.97
  79.8 40.9 %all-gather.2.cloned.1.call-done = f32[8,4,2,128,128]{4,3,2,1,0:T(8,128)} async-done(((f32[1,4,2,128,128]{4,3,2,1,0:T(8,128)}), f32[8,4,2,128,128]{4,3,2,1,0:T(8,128)}) %all-gather.2.cloned.1.call-update) | async-done | bytes 4194320 | tf_op jit(solution)/shard_map/all_gather | solution.py:47
  120.7 4.3 %gather_fusion.1 = f32[36,128,128]{2,1,0:T(8,128)} fusion(f32[64,128,128]{2,1,0:T(8,128)} %bitcast.38, s32[1024]{0:T(1024)S(1)} %pad_clamp_fusion), kind=kCustom, calls=%fused_computation.1 | custom fusion | bytes 4718736 | tf_op jit(solution)/shard_map/gather | solution.py:71
  125.1 0.7 collective-permute-start.1
  125.8 0.4 copy.26
  126.1 0.6 reshape.82
  126.7 0.1 copy.23
  126.9 0.1 copy.24
  127.0 0.1 reshape.89
  127.1 2.9 %gather_fusion = f32[36,128,128]{2,1,0:T(8,128)S(1)} fusion(f32[64,128,128]{2,1,0:T(8,128)} %bitcast.39, s32[1024]{0:T(1024)S(1)} %pad_clamp_fusion.1), kind=kCustom, calls=%fused_computation | custom fusion | bytes 4718736 | tf_op jit(solution)/shard_map/gather | solution.py:72
  130.0 0.3 collective-permute-done.1
  130.3 2.8 %fusion.8 = f32[18,64,1,2,128]{4,1,3,0,2:T(8,128)S(1)} fusion(f32[18,1,2,128,128]{4,3,2,0,1:T(8,128)S(1)} %bitcast.37, f32[18,1,2,128,128]{4,3,2,0,1:T(8,128)} %collective-permute-done.1, f32[18,64,2,128]{3,2,1,0:T(2,128)S(1)} %reshape.82, pred[18,2]{1,0:T(8,128)(4,1)S(1)} %copy.23), kind=kOutput, calls=%fused_computation.8 | convolution fusion | flops 227082240 | bytes 7077924 | tf_op jit(solution)/shard_map/rschk,rchkl->rschl/dot_general | solution.py:73
  133.1 0.9 copy.28
  134.0 1.9 %copy.29 = f32[1152,1,256]{0,2,1:T(8,128)S(1)} copy(f32[1152,1,256]{2,1,0:T(1,128)S(1)} %bitcast.40) | data formatting | bytes 2359296 | tf_op jit(solution)/shard_map/reshape | solution.py:75
  136.0 0.0 reduce-scatter.2.cloned.1.call-done
  136.0 1.4 select_add_fusion
  137.4 2.1 %copy.30 = f32[1152,1,256]{2,1,0:T(1,128)} copy(f32[1152,1,256]{0,2,1:T(8,128)S(1)} %select_add_fusion) | data formatting | bytes 2359296 | tf_op jit(solution)/shard_map/add | solution.py:76
  (14 shorter events, 0.1 us)
Async XLA Ops:
  7.4 59.5 %copy-start.2 = (s32[18,1,2]{0,2,1:T(2,128)S(1)}, s32[18,1,2]{0,2,1:T(2,128)}, u32[]{:S(2)}) copy-start(s32[18,1,2]{0,2,1:T(2,128)} %param.11) | copy-start | bytes 436
  7.4 56.9 %copy-start.1 = (f32[1152,1,256]{2,1,0:T(1,128)S(1)}, f32[1152,1,256]{2,1,0:T(1,128)}, u32[]{:S(2)}) copy-start(f32[1152,1,256]{2,1,0:T(1,128)} %param.7) | copy-start | bytes 3538948
  7.4 54.3 %all-reduce.2.cloned.1.call-start = ((), (), s32[]{:S(2)}) async-start(), calls=%async_computation.2 | async-start | bytes 1048576 | tf_op jit(solution)/shard_map/psum | solution.py:46
  10.6 0.8 copy-start
  11.4 109.4 %all-gather.2.cloned.1.call-start = ((), (), s32[]{:S(2)}) async-start(), calls=%async_computation.3 | async-start | bytes 4718592 | tf_op jit(solution)/shard_map/all_gather | solution.py:47
  61.7 74.4 %reduce-scatter.2.cloned.1.call-start = ((), (), s32[]{:S(2)}) async-start(), calls=%async_computation.1 | async-start | bytes 5898240 | tf_op jit(solution)/shard_map/reduce_scatter | solution.py:65
  61.7 5.4 %collective-permute-start = (s32[18,1,2]{0,2,1:T(2,128)}, s32[18,1,2]{0,2,1:T(2,128)S(1)}, u32[]{:S(2)}, u32[]{:S(2)}) collective-permute-start(s32[18,1,2]{0,2,1:T(2,128)} %param.11), channel_id=1, source_target_pairs={{0,4},{4,0},{1,5},{5,1},{2,6},{6,2},{3,7},{7,3},{8,12},{12,8},{9,1... | collective-permute-start | bytes 440 | tf_op jit(solution)/shard_map/ppermute | solution.py:12
  125.1 5.2 %collective-permute-start.1 = (f32[18,1,2,128,128]{4,3,2,0,1:T(8,128)}, f32[18,1,2,128,128]{4,3,2,0,1:T(8,128)}, u32[]{:S(2)}, u32[]{:S(2)}) collective-permute-start(f32[18,1,2,128,128]{4,3,2,0,1:T(8,128)} %bitcast.10), channel_id=1, source_target_pairs={{0,4},{4,0},{1,5},{5,1},{2,6},{6,2},{3,7},{7,3},{8,12},{12,8},{9,1... | collective-permute-start | bytes 7077896 | tf_op jit(solution)/shard_map/ppermute | solution.py:12
Sparse Core Ops, SparseCore 0:
  11.5 50.1 all-reduce.1
  63.4 57.2 all-gather.1
Sparse Core Ops, SparseCore 1:
  79.7 53.5 reduce-scatter.1

commit v17 on v14

--- a/solution.py
+++ b/solution.py
@@ -61,11 +61,18 @@
     sib_slot, _ = place(shift(ph_owner, "core", 1))
     blocks = masked.reshape(row_tiles, tile_rows, chan_count, col_tiles, tile_cols)
     slot, sib_slot, lowered = lax.optimization_barrier((slot, sib_slot, lowered))
-    ladder = lax.psum_scatter(
-        jnp.einsum("crk,kch->rch", pair_interaction, lowered, preferred_element_type=jnp.float32),
-        "ctr",
-        scatter_dimension=0,
-        tiled=True,
+    half = hole_width // 2
+    parts = [
+        jnp.einsum(
+            "crk,kch->rch", pair_interaction, lowered[:, :, s : s + half],
+            preferred_element_type=jnp.float32,
+        )
+        for s in (0, half)
+    ]
+    parts[0], masked_late = lax.optimization_barrier((parts[0], masked))
+    blocks = masked_late.reshape(row_tiles, tile_rows, chan_count, col_tiles, tile_cols)
+    ladder = jnp.concatenate(
+        [lax.psum_scatter(p, "ctr", scatter_dimension=0, tiled=True) for p in parts], axis=2
     )
     from_sibling = shift(own[sib_slot], "core", 1)
     chosen = jnp.where((owner_core == my_core)[..., None, None], own[slot], from_sibling)

time: 106 us -> 120 us (1.13)
  waiting for transfers between devices: 39.2 us -> 46.9 us
  matrix products: 15.3 us -> 20.7 us
    reduce_scatter x1 -> x2, waiting for transfers between devices: 0.03 us -> 13.3 us  [local(): lax.psum_scatter(p, 'ctr', scatter_dimension=0, tiled=True)]
    all_gather x1, waiting for transfers between devices: 38.8 us -> 33.2 us  [local(): own = lax.all_gather(by_y, 'cz', axis=0, tiled=False)]
    dot_general x1 -> x2, matrix products: 12.4 us -> 17.9 us  [local(): jnp.einsum('crk,kch->rch', pair_interaction, lowered[:, :, s:s + half], p...]
  transfers between devices with their start and end apart: 4 -> 5, of which waited for: 2 -> 3; matrix products, arithmetic and copies ran while one was open for 28% -> 29% of each run, Pallas kernels for 0% -> 0%
where the time goes in v17:
time: 120 us; the launch traced here: 119 us
  waiting for transfers between devices  46.9 us (39%)
  matrix products  20.7 us (17%)
  local copies, waits for them, and re-layouts  16.2 us (14%)
  between operations  15.6 us (13%)
  blocking collectives  13.4 us (11%)
  starting transfers between devices  4.86 us (4%)
  other arithmetic  1.59 us (1%)
    all_gather x1, waiting for transfers between devices, local(): own = lax.all_gather(by_y, 'cz', axis=0, tiled=False)  33.2 us
    dot_general x2, matrix products, local(): jnp.einsum('crk,kch->rch', pair_interaction, lowered[:, :, s:s + half], p...  17.9 us
    all_gather x1, blocking collectives, local(): by_y = lax.all_gather(ph_interaction, 'cy', axis=0, tiled=False)  13.4 us
    reduce_scatter x2, waiting for transfers between devices, local(): lax.psum_scatter(p, 'ctr', scatter_dimension=0, tiled=True)  13.3 us
    ppermute x2, starting transfers between devices, shift(): return lax.ppermute(x, axis, [(k, (k + step) % n) for k in range(n)])  4.77 us
    gather x1, local copies, waits for them, and re-layouts, local(): from_sibling = shift(own[sib_slot], 'core', 1)  4.33 us
    gather x1, local copies, waits for them, and re-layouts, local(): own[slot]  2.89 us
    dot_general x1, matrix products, local(): jnp.einsum('rschk,rchkl->rschl', blocks, chosen, precision=lax.Precision....  2.85 us
  transfers between devices with their start and end apart: 5, of which 3 were waited for; matrix products, arithmetic and copies ran while one was open for 29% of the time, Pallas kernels for 0%

profile of v17, /device:TPU:1, one launch (start us, length us, event | category | flops | bytes accessed | tf_op | source)
XLA Modules:
  0.0 119.3 jit_solution(14255985405871735731)
XLA Ops:
  7.4 0.0 all-gather.4.cloned.1.call-start
  7.4 13.4 %all-gather = f32[8,128,128]{2,1,0:T(8,128)} all-gather(f32[2,128,128]{2,1,0:T(8,128)} %param.7), channel_id=2, replica_groups=mesh['cy'=4,'cz'=8,'core'=2,'ctr'=4] {'cy'}, dimensions={0}, use_global_device_ids=true | all-gather | bytes 655360 | tf_op jit(solution)/shard_map/all_gather | solution.py:45
  20.7 0.0 all-gather.4.cloned.1.call-update
  20.8 0.0 reduce-scatter.5.cloned.1.call-start
  20.8 4.1 %collective-permute-start = (s32[18,1,2]{0,2,1:T(2,128)}, s32[18,1,2]{0,2,1:T(2,128)S(1)}, u32[]{:S(2)}, u32[]{:S(2)}) collective-permute-start(s32[18,1,2]{0,2,1:T(2,128)} %param.9), channel_id=1, source_target_pairs={{0,4},{4,0},{1,5},{5,1},{2,6},{6,2},{3,7},{7,3},{8,12},{12,8},{9,1... | collective-permute-start | bytes 440 | tf_op jit(solution)/shard_map/ppermute | solution.py:12
  24.9 2.6 %copy.22 = f32[1152,1,256]{0,2,1:T(8,128)S(1)} copy(f32[1152,1,256]{2,1,0:T(1,128)} %param.5) | data formatting | bytes 2359296 | tf_op args[0]
  28.2 0.1 fusion.31
  28.4 0.0 collective-permute-done
  28.4 8.9 %fusion.7 = f32[4608,1,128]{0,2,1:T(8,128)} fusion(bf16[1,4608,1152]{2,1,0:T(8,128)(2,1)} %param.6, bf16[1152,1,256]{0,2,1:T(8,128)(2,1)S(1)} %get-tuple-element.10), kind=kOutput, calls=%fused_computation.7 | convolution fusion | flops 1358954496 | bytes 13271040 | tf_op jit(solution)/shard_map/crk,kch->rch/dot_general | solution.py:66
  37.3 0.0 reduce-scatter.5.cloned.1.call-update
  37.3 0.0 reduce-scatter.3.cloned.1.call-start
  37.4 9.0 %fusion.4 = f32[4608,1,128]{0,2,1:T(8,128)} fusion(bf16[1,4608,1152]{2,1,0:T(8,128)(2,1)} %param.6, bf16[1152,1,256]{0,2,1:T(8,128)(2,1)S(1)} %get-tuple-element.10), kind=kOutput, calls=%fused_computation.6 | convolution fusion | flops 1358954496 | bytes 13271040 | tf_op jit(solution)/shard_map/crk,kch->rch/dot_general | solution.py:66
  46.4 0.0 reduce-scatter.3.cloned.1.call-update
  46.4 0.1 copy.25
  46.5 0.1 reshape.118
  46.6 33.2 %all-gather.4.cloned.1.call-done = f32[32,2,128,128]{3,2,1,0:T(8,128)} async-done(((f32[4,2,128,128]{3,2,1,0:T(8,128)}), f32[32,2,128,128]{3,2,1,0:T(8,128)}) %all-gather.4.cloned.1.call-update) | async-done | bytes 4194320 | tf_op jit(solution)/shard_map/all_gather | solution.py:46
  79.8 4.3 %gather_fusion.1 = f32[36,128,128]{2,1,0:T(8,128)} fusion(f32[64,128,128]{2,1,0:T(8,128)} %bitcast.47, s32[1024]{0:T(1024)S(1)} %pad_clamp_fusion), kind=kCustom, calls=%fused_computation.1 | custom fusion | bytes 4718736 | tf_op jit(solution)/shard_map/gather | solution.py:77
  84.2 0.7 collective-permute-start.1
  84.9 0.1 copy.23
  85.0 0.1 copy.24
  85.1 0.1 reshape.110
  85.2 0.4 copy.26
  85.5 0.6 reshape.106
  86.2 2.9 %gather_fusion = f32[36,128,128]{2,1,0:T(8,128)S(1)} fusion(f32[64,128,128]{2,1,0:T(8,128)} %bitcast.48, s32[1024]{0:T(1024)S(1)} %pad_clamp_fusion.1), kind=kCustom, calls=%fused_computation | custom fusion | bytes 4718736 | tf_op jit(solution)/shard_map/gather | solution.py:78
  89.1 0.3 collective-permute-done.1
  89.4 2.8 %fusion.13 = f32[18,64,1,2,128]{4,1,3,0,2:T(8,128)S(1)} fusion(f32[18,1,2,128,128]{4,3,2,0,1:T(8,128)S(1)} %bitcast.46, f32[18,1,2,128,128]{4,3,2,0,1:T(8,128)} %collective-permute-done.1, f32[18,64,2,128]{3,2,1,0:T(2,128)S(1)} %reshape.106, pred[18,2]{1,0:T(8,128)(4,1)S(1)} %copy.23), kind=kOutput, calls=%fused_computation.11 | convolution fusion | flops 227082240 | bytes 7077924 | tf_op jit(solution)/shard_map/rschk,rchkl->rschl/dot_general | solution.py:79
  92.2 0.9 copy.28
  93.1 1.9 %copy.29 = f32[1152,1,256]{0,2,1:T(8,128)S(1)} copy(f32[1152,1,256]{2,1,0:T(1,128)S(1)} %bitcast.49) | data formatting | bytes 2359296 | tf_op jit(solution)/shard_map/reshape | solution.py:81
  95.1 0.0 reduce-scatter.5.cloned.1.call-done
  95.1 13.3 %reduce-scatter.3.cloned.1.call-done = f32[1152,1,128]{0,2,1:T(8,128)} async-done(((f32[4608,1,128]{0,2,1:T(8,128)}), f32[1152,1,128]{0,2,1:T(8,128)}) %reduce-scatter.3.cloned.1.call-update) | async-done | bytes 589840 | tf_op jit(solution)/shard_map/reduce_scatter | solution.py:75
  108.4 1.4 %fusion.16 = f32[1152,1,256]{0,2,1:T(8,128)S(1)} fusion(f32[1152,1,256]{0,2,1:T(8,128)S(1)} %copy.29, f32[1152,1,128]{0,2,1:T(8,128)} %reduce-scatter.5.cloned.1.call-done, f32[1152,1,128]{0,2,1:T(8,128)} %reduce-scatter.3.cloned.1.call-done, pred[1152]{0:T(1024)(128)(4,1)S(1)} %add_compare_fusion), kind=kLoop, calls=%fused_computation.13 | loop fusion | flops 884736 | bytes 3540096 | tf_op jit(solution)/shard_map/add | solution.py:82
  109.8 2.1 %copy.30 = f32[1152,1,256]{2,1,0:T(1,128)} copy(f32[1152,1,256]{0,2,1:T(8,128)S(1)} %fusion.16) | data formatting | bytes 2359296 | tf_op jit(solution)/shard_map/add | solution.py:82
  (9 shorter events, 0.1 us)
Async XLA Ops:
  7.4 20.8 %copy-start = (s32[18,1,2]{0,2,1:T(2,128)S(1)}, s32[18,1,2]{0,2,1:T(2,128)}, u32[]{:S(2)}) copy-start(s32[18,1,2]{0,2,1:T(2,128)} %param.9) | copy-start | bytes 436
  7.4 72.5 %all-gather.4.cloned.1.call-start = ((), (), s32[]{:S(2)}) async-start(), calls=%async_computation.4 | async-start | bytes 4718592 | tf_op jit(solution)/shard_map/all_gather | solution.py:46
  20.8 74.4 %reduce-scatter.5.cloned.1.call-start = ((), (), s32[]{:S(2)}) async-start(), calls=%async_computation.3 | async-start | bytes 2949120 | tf_op jit(solution)/shard_map/reduce_scatter | solution.py:75
  20.8 7.5 %collective-permute-start = (s32[18,1,2]{0,2,1:T(2,128)}, s32[18,1,2]{0,2,1:T(2,128)S(1)}, u32[]{:S(2)}, u32[]{:S(2)}) collective-permute-start(s32[18,1,2]{0,2,1:T(2,128)} %param.9), channel_id=1, source_target_pairs={{0,4},{4,0},{1,5},{5,1},{2,6},{6,2},{3,7},{7,3},{8,12},{12,8},{9,1... | collective-permute-start | bytes 440 | tf_op jit(solution)/shard_map/ppermute | solution.py:12
  37.3 71.1 %reduce-scatter.3.cloned.1.call-start = ((), (), s32[]{:S(2)}) async-start(), calls=%async_computation.2 | async-start | bytes 2949120 | tf_op jit(solution)/shard_map/reduce_scatter | solution.py:75
  84.2 5.2 %collective-permute-start.1 = (f32[18,1,2,128,128]{4,3,2,0,1:T(8,128)}, f32[18,1,2,128,128]{4,3,2,0,1:T(8,128)}, u32[]{:S(2)}, u32[]{:S(2)}) collective-permute-start(f32[18,1,2,128,128]{4,3,2,0,1:T(8,128)} %bitcast.12), channel_id=1, source_target_pairs={{0,4},{4,0},{1,5},{5,1},{2,6},{6,2},{3,7},{7,3},{8,12},{12,8},{9,1... | collective-permute-start | bytes 7077896 | tf_op jit(solution)/shard_map/ppermute | solution.py:12
Sparse Core Ops, SparseCore 0:
  20.9 58.9 all-gather.3
Sparse Core Ops, SparseCore 1:
  37.4 34.4 reduce-scatter.4
  74.3 34.1 reduce-scatter.2

commit v18 on v14

--- a/solution.py
+++ b/solution.py
@@ -1,6 +1,7 @@
 import jax
 import jax.numpy as jnp
 from jax import lax
+from jax.experimental import pallas as pl
 from jax.sharding import Mesh
 from jax.sharding import PartitionSpec as P
 
@@ -35,6 +36,32 @@
     return jnp.stack([x] + [shift(x, axis, -o) for o in range(1, n)], axis=0)
 
 
+def ladder_kernel(lt_ref, p_ref, o_ref):
+    o_ref[...] = lax.dot_general(
+        lt_ref[...], p_ref[...], (((1,), (1,)), ((), ())), preferred_element_type=jnp.float32
+    )
+
+
+def ladder_matmul_t(lowered_t, weights, block=512):
+    width, depth = lowered_t.shape
+    rows = weights.shape[0]
+    return pl.pallas_call(
+        ladder_kernel,
+        grid=(rows // block,),
+        in_specs=[
+            pl.BlockSpec((width, depth), lambda i: (0, 0)),
+            pl.BlockSpec((block, depth), lambda i: (i, 0)),
+        ],
+        out_specs=pl.BlockSpec((width, block), lambda i: (0, i)),
+        out_shape=jax.ShapeDtypeStruct((width, rows), jnp.float32),
+        cost_estimate=pl.CostEstimate(
+            flops=2 * rows * depth * width,
+            bytes_accessed=2 * rows * depth + 2 * depth * width + 4 * rows * width,
+            transcendentals=0,
+        ),
+    )(lowered_t, weights)
+
+
 def local(amplitudes, pair_interaction, ph_interaction, pp_size, ph_owner):
     row_count, chan_count, hole_width = amplitudes.shape
     row_tiles, _, col_tiles = ph_owner.shape
@@ -62,7 +89,9 @@
     blocks = masked.reshape(row_tiles, tile_rows, chan_count, col_tiles, tile_cols)
     slot, sib_slot, lowered = lax.optimization_barrier((slot, sib_slot, lowered))
     ladder = lax.psum_scatter(
-        jnp.einsum("crk,kch->rch", pair_interaction, lowered, preferred_element_type=jnp.float32),
+        jnp.transpose(
+            ladder_matmul_t(lowered[:, 0, :].T, pair_interaction[0])
+        )[:, None, :],
         "ctr",
         scatter_dimension=0,
         tiled=True,

time: 106 us -> 107 us (level)
  matrix products: 15.3 us -> 2.95 us
  Pallas kernels: 0 us -> 11 us
  waiting for transfers between devices: 39.2 us -> 40.3 us
    dot_general x1 -> x0, matrix products: 12.4 us -> none  [local(): jnp.einsum('crk,kch->rch', pair_interaction, lowered, preferred_element_t...]
    pallas_call x0 -> x1, Pallas kernels: none -> 11 us  [ladder_matmul_t(): pl.pallas_call(ladder_kernel, grid=(rows // block,), in_specs=[pl.BlockSp...]
    all_gather x1, waiting for transfers between devices: 38.8 us -> 40.1 us  [local(): own = lax.all_gather(by_y, 'cz', axis=0, tiled=False)]
    unnamed x3 -> x5, local copies, waits for them, and re-layouts: 2.6 us -> 1.94 us
  transfers between devices with their start and end apart: 4 -> 4, of which waited for: 2 -> 2; matrix products, arithmetic and copies ran while one was open for 28% -> 17% of each run, Pallas kernels for 0% -> 10%
where the time goes in v18:
time: 107 us; the launch traced here: 106 us
  waiting for transfers between devices  40.3 us (38%)
  local copies, waits for them, and re-layouts  15.7 us (15%)
  between operations  15.6 us (15%)
  blocking collectives  13.4 us (13%)
  Pallas kernels  11 us (10%)
  starting transfers between devices  4.8 us (4%)
  matrix products  2.95 us (3%)
  other arithmetic  2.43 us (2%)
    all_gather x1, waiting for transfers between devices, local(): own = lax.all_gather(by_y, 'cz', axis=0, tiled=False)  40.1 us
    all_gather x1, blocking collectives, local(): by_y = lax.all_gather(ph_interaction, 'cy', axis=0, tiled=False)  13.4 us
    pallas_call x1, Pallas kernels, ladder_matmul_t(): pl.pallas_call(ladder_kernel, grid=(rows // block,), in_specs=[pl.BlockSp...  11 us
    ppermute x2, starting transfers between devices, shift(): return lax.ppermute(x, axis, [(k, (k + step) % n) for k in range(n)])  4.75 us
    gather x1, local copies, waits for them, and re-layouts, local(): from_sibling = shift(own[sib_slot], 'core', 1)  4.33 us
    gather x1, local copies, waits for them, and re-layouts, local(): own[slot]  2.99 us
    dot_general x1, matrix products, local(): jnp.einsum('rschk,rchkl->rschl', blocks, chosen, precision=lax.Precision....  2.95 us
  transfers between devices with their start and end apart: 4, of which 2 were waited for; matrix products, arithmetic and copies ran while one was open for 17% of the time, Pallas kernels for 10%

profile of v18, /device:TPU:1, one launch (start us, length us, event | category | flops | bytes accessed | tf_op | source)
XLA Modules:
  0.0 106.2 jit_solution(5833269450783067697)
XLA Ops:
  7.4 0.0 copy-start.1
  7.4 0.0 copy-start
  7.4 0.0 all-gather.4.cloned.1.call-start
  7.4 13.4 %all-gather = f32[8,128,128]{2,1,0:T(8,128)} all-gather(f32[2,128,128]{2,1,0:T(8,128)} %param.7), channel_id=2, replica_groups=mesh['cy'=4,'cz'=8,'core'=2,'ctr'=4] {'cy'}, dimensions={0}, use_global_device_ids=true | all-gather | bytes 655360 | tf_op jit(solution)/shard_map/all_gather | solution.py:72
  20.7 0.0 all-gather.4.cloned.1.call-update
  20.8 0.0 reduce-scatter.2.cloned.1.call-start
  20.8 0.0 copy-done.1
  20.8 4.1 %collective-permute-start = (s32[18,1,2]{0,2,1:T(2,128)S(1)}, s32[18,1,2]{0,2,1:T(2,128)S(1)}, u32[]{:S(2)}, u32[]{:S(2)}) collective-permute-start(s32[18,1,2]{0,2,1:T(2,128)S(1)} %copy-done.1), channel_id=1, source_target_pairs={{0,4},{4,0},{1,5},{5,1},{2,6},{6,2},{3,7},{7,3},{8,12},{12,8},{9,1... | collective-permute-start | bytes 440 | tf_op jit(solution)/shard_map/ppermute | solution.py:13
  24.9 0.0 copy-done
  24.9 1.9 %copy.22 = f32[1152,1,256]{0,2,1:T(8,128)S(1)} copy(f32[1152,1,256]{2,1,0:T(1,128)S(1)} %copy-done) | data formatting | bytes 2359296 | tf_op args[0]
  27.5 0.9 fusion.16
  28.5 0.0 collective-permute-done
  28.5 11.0 %shard_map.55 = f32[256,4608]{1,0:T(8,128)} custom-call(bf16[256,1152]{1,0:T(8,128)(2,1)} %bitcast.36, bf16[4608,1152]{1,0:T(8,128)(2,1)} %bitcast.31), custom_call_target="tpu_custom_call" | custom-call | flops 2717908992 | bytes 15925248 | tf_op jit(solution)/shard_map/pallas_call | solution.py:48
  39.5 0.0 reduce-scatter.2.cloned.1.call-update
  39.6 0.1 copy.25
  39.7 0.1 reshape.44
  39.8 40.1 %all-gather.4.cloned.1.call-done = f32[32,2,128,128]{3,2,1,0:T(8,128)} async-done(((f32[4,2,128,128]{3,2,1,0:T(8,128)}), f32[32,2,128,128]{3,2,1,0:T(8,128)}) %all-gather.4.cloned.1.call-update) | async-done | bytes 4194320 | tf_op jit(solution)/shard_map/all_gather | solution.py:73
  79.8 4.3 %gather_fusion.1 = f32[36,128,128]{2,1,0:T(8,128)} fusion(f32[64,128,128]{2,1,0:T(8,128)} %bitcast.33, s32[1024]{0:T(1024)S(1)} %pad_clamp_fusion), kind=kCustom, calls=%fused_computation.1 | custom fusion | bytes 4718736 | tf_op jit(solution)/shard_map/gather | solution.py:99
  84.2 0.7 collective-permute-start.1
  84.9 0.4 copy.26
  85.2 0.6 reshape.32
  85.8 0.1 copy.23
  86.0 0.1 copy.24
  86.0 0.1 reshape.36
  86.2 3.0 %gather_fusion = f32[36,128,128]{2,1,0:T(8,128)S(1)} fusion(f32[64,128,128]{2,1,0:T(8,128)} %bitcast.34, s32[1024]{0:T(1024)S(1)} %pad_clamp_fusion.1), kind=kCustom, calls=%fused_computation | custom fusion | bytes 4718736 | tf_op jit(solution)/shard_map/gather | solution.py:100
  89.2 0.2 collective-permute-done.1
  89.4 2.9 %fusion.3 = f32[18,64,1,2,128]{4,1,3,0,2:T(8,128)S(1)} fusion(f32[18,1,2,128,128]{4,3,2,0,1:T(8,128)S(1)} %bitcast.32, f32[18,1,2,128,128]{4,3,2,0,1:T(8,128)} %collective-permute-done.1, f32[18,64,2,128]{3,2,1,0:T(2,128)S(1)} %reshape.32, pred[18,2]{1,0:T(8,128)(4,1)S(1)} %copy.23), kind=kOutput, calls=%fused_computation.5 | convolution fusion | flops 227082240 | bytes 7077924 | tf_op jit(solution)/shard_map/rschk,rchkl->rschl/dot_general | solution.py:101
  92.3 0.9 copy.28
  93.2 1.9 %copy.29 = f32[1152,1,256]{0,2,1:T(8,128)S(1)} copy(f32[1152,1,256]{2,1,0:T(1,128)S(1)} %bitcast.35) | data formatting | bytes 2359296 | tf_op jit(solution)/shard_map/reshape | solution.py:103
  95.2 0.0 reduce-scatter.2.cloned.1.call-done
  95.2 1.4 %select_add_fusion = f32[1152,1,256]{0,2,1:T(8,128)S(1)} fusion(f32[1152,1,256]{0,2,1:T(8,128)S(1)} %copy.29, f32[1152,1,256]{0,2,1:T(8,128)} %reduce-scatter.2.cloned.1.call-done, pred[1152]{0:T(1024)(128)(4,1)S(1)} %add_compare_fusion), kind=kLoop, calls=%fused_computation.7 | loop fusion | flops 589824 | bytes 3540096 | tf_op jit(solution)/shard_map/add | solution.py:104
  96.6 2.1 %copy.30 = f32[1152,1,256]{2,1,0:T(1,128)} copy(f32[1152,1,256]{0,2,1:T(8,128)S(1)} %select_add_fusion) | data formatting | bytes 2359296 | tf_op jit(solution)/shard_map/add | solution.py:104
  (7 shorter events, 0.1 us)
Async XLA Ops:
  7.4 13.5 %copy-start.1 = (s32[18,1,2]{0,2,1:T(2,128)S(1)}, s32[18,1,2]{0,2,1:T(2,128)}, u32[]{:S(2)}) copy-start(s32[18,1,2]{0,2,1:T(2,128)} %param.9) | copy-start | bytes 436
  7.4 17.5 %copy-start = (f32[1152,1,256]{2,1,0:T(1,128)S(1)}, f32[1152,1,256]{2,1,0:T(1,128)}, u32[]{:S(2)}) copy-start(f32[1152,1,256]{2,1,0:T(1,128)} %param.5) | copy-start | bytes 3538948
  7.4 72.5 %all-gather.4.cloned.1.call-start = ((), (), s32[]{:S(2)}) async-start(), calls=%async_computation.2 | async-start | bytes 4718592 | tf_op jit(solution)/shard_map/all_gather | solution.py:73
  20.8 74.4 %reduce-scatter.2.cloned.1.call-start = ((), (), s32[]{:S(2)}) async-start(), calls=%async_computation.1 | async-start | bytes 5898240 | tf_op jit(solution)/shard_map/reduce_scatter | solution.py:91
  20.8 7.7 %collective-permute-start = (s32[18,1,2]{0,2,1:T(2,128)S(1)}, s32[18,1,2]{0,2,1:T(2,128)S(1)}, u32[]{:S(2)}, u32[]{:S(2)}) collective-permute-start(s32[18,1,2]{0,2,1:T(2,128)S(1)} %copy-done.1), channel_id=1, source_target_pairs={{0,4},{4,0},{1,5},{5,1},{2,6},{6,2},{3,7},{7,3},{8,12},{12,8},{9,1... | collective-permute-start | bytes 440 | tf_op jit(solution)/shard_map/ppermute | solution.py:13
  84.2 5.2 %collective-permute-start.1 = (f32[18,1,2,128,128]{4,3,2,0,1:T(8,128)}, f32[18,1,2,128,128]{4,3,2,0,1:T(8,128)}, u32[]{:S(2)}, u32[]{:S(2)}) collective-permute-start(f32[18,1,2,128,128]{4,3,2,0,1:T(8,128)} %bitcast.10), channel_id=1, source_target_pairs={{0,4},{4,0},{1,5},{5,1},{2,6},{6,2},{3,7},{7,3},{8,12},{12,8},{9,1... | collective-permute-start | bytes 7077896 | tf_op jit(solution)/shard_map/ppermute | solution.py:13
Sparse Core Ops, SparseCore 0:
  20.9 58.9 all-gather.3
Sparse Core Ops, SparseCore 1:
  39.7 53.7 reduce-scatter.1

commit v19 on v18

--- a/solution.py
+++ b/solution.py
@@ -86,12 +86,13 @@
 
     slot, owner_core = place(ph_owner)
     sib_slot, _ = place(shift(ph_owner, "core", 1))
-    blocks = masked.reshape(row_tiles, tile_rows, chan_count, col_tiles, tile_cols)
     slot, sib_slot, lowered = lax.optimization_barrier((slot, sib_slot, lowered))
+    partial = ladder_matmul_t(lowered[:, 0, :].T, pair_interaction[0])
+    partial, masked_late = lax.optimization_barrier((partial, masked))
+    blocks = masked_late.reshape(row_tiles, tile_rows, chan_count, col_tiles, tile_cols)
+    blocks, own = lax.optimization_barrier((blocks, own))
     ladder = lax.psum_scatter(
-        jnp.transpose(
-            ladder_matmul_t(lowered[:, 0, :].T, pair_interaction[0])
-        )[:, None, :],
+        jnp.transpose(partial)[:, None, :],
         "ctr",
         scatter_dimension=0,
         tiled=True,

time: 107 us -> 107 us (level)
    all_gather x1, waiting for transfers between devices: 40.1 us -> 38 us  [local(): own = lax.all_gather(by_y, 'cz', axis=0, tiled=False)]
    optimization_barrier x0 -> x1, local copies, waits for them, and re-layouts: none -> 1.96 us  [local(): partial, masked_late = lax.optimization_barrier((partial, masked))]
where the time goes in v19:
time: 107 us; the launch traced here: 106 us
  waiting for transfers between devices  39.4 us (37%)
  local copies, waits for them, and re-layouts  16.6 us (16%)
  between operations  15.6 us (15%)
  blocking collectives  13.4 us (13%)
  Pallas kernels  11 us (10%)
  starting transfers between devices  4.8 us (4%)
  matrix products  2.95 us (3%)
  other arithmetic  2.43 us (2%)
    all_gather x1, waiting for transfers between devices, local(): own = lax.all_gather(by_y, 'cz', axis=0, tiled=False)  38 us
    all_gather x1, blocking collectives, local(): by_y = lax.all_gather(ph_interaction, 'cy', axis=0, tiled=False)  13.4 us
    pallas_call x1, Pallas kernels, ladder_matmul_t(): pl.pallas_call(ladder_kernel, grid=(rows // block,), in_specs=[pl.BlockSp...  11 us
    ppermute x2, starting transfers between devices, shift(): return lax.ppermute(x, axis, [(k, (k + step) % n) for k in range(n)])  4.75 us
    gather x1, local copies, waits for them, and re-layouts, local(): from_sibling = shift(own[sib_slot], 'core', 1)  4.33 us
    dot_general x1, matrix products, local(): jnp.einsum('rschk,rchkl->rschl', blocks, chosen, precision=lax.Precision....  2.95 us
    gather x1, local copies, waits for them, and re-layouts, local(): own[slot]  2.93 us
  transfers between devices with their start and end apart: 4, of which 2 were waited for; matrix products, arithmetic and copies ran while one was open for 17% of the time, Pallas kernels for 10%

profile of v19, /device:TPU:1, one launch (start us, length us, event | category | flops | bytes accessed | tf_op | source)
XLA Modules:
  0.0 106.2 jit_solution(10290042997111962488)
XLA Ops:
  7.4 0.0 copy-start.1
  7.4 0.0 copy-start
  7.4 0.0 all-gather.4.cloned.1.call-start
  7.4 13.4 %all-gather = f32[8,128,128]{2,1,0:T(8,128)} all-gather(f32[2,128,128]{2,1,0:T(8,128)} %param.7), channel_id=2, replica_groups=mesh['cy'=4,'cz'=8,'core'=2,'ctr'=4] {'cy'}, dimensions={0}, use_global_device_ids=true | all-gather | bytes 655360 | tf_op jit(solution)/shard_map/all_gather | solution.py:72
  20.7 0.0 all-gather.4.cloned.1.call-update
  20.8 0.0 reduce-scatter.2.cloned.1.call-start
  20.8 0.0 copy-done.1
  20.8 4.1 %collective-permute-start = (s32[18,1,2]{0,2,1:T(2,128)S(1)}, s32[18,1,2]{0,2,1:T(2,128)S(1)}, u32[]{:S(2)}, u32[]{:S(2)}) collective-permute-start(s32[18,1,2]{0,2,1:T(2,128)S(1)} %copy-done.1), channel_id=1, source_target_pairs={{0,4},{4,0},{1,5},{5,1},{2,6},{6,2},{3,7},{7,3},{8,12},{12,8},{9,1... | collective-permute-start | bytes 440 | tf_op jit(solution)/shard_map/ppermute | solution.py:13
  25.6 0.0 copy-done
  25.6 1.9 %copy.22 = f32[1152,1,256]{0,2,1:T(8,128)S(1)} copy(f32[1152,1,256]{2,1,0:T(1,128)S(1)} %copy-done) | data formatting | bytes 2359296 | tf_op args[0]
  27.6 0.9 fusion.16
  28.5 0.0 collective-permute-done
  28.6 11.0 %shard_map.55 = f32[256,4608]{1,0:T(8,128)} custom-call(bf16[256,1152]{1,0:T(8,128)(2,1)} %bitcast.37, bf16[4608,1152]{1,0:T(8,128)(2,1)} %bitcast.31), custom_call_target="tpu_custom_call" | custom-call | flops 2717908992 | bytes 15925248 | tf_op jit(solution)/shard_map/pallas_call | solution.py:48
  39.6 0.0 reduce-scatter.2.cloned.1.call-update
  39.6 0.1 copy.26
  39.7 0.1 reshape.46
  39.8 2.0 %copy.24 = f32[1152,1,256]{2,1,0:T(1,128)S(1)} copy(f32[1152,1,256]{0,2,1:T(8,128)S(1)} %get-tuple-element.14) | data formatting | bytes 2359296 | tf_op jit(solution)/shard_map/optimization_barrier | solution.py:91
  41.8 38.0 %all-gather.4.cloned.1.call-done = f32[32,2,128,128]{3,2,1,0:T(8,128)} async-done(((f32[4,2,128,128]{3,2,1,0:T(8,128)}), f32[32,2,128,128]{3,2,1,0:T(8,128)}) %all-gather.4.cloned.1.call-update) | async-done | bytes 4194320 | tf_op jit(solution)/shard_map/all_gather | solution.py:73
  79.8 4.3 %gather_fusion.1 = f32[36,128,128]{2,1,0:T(8,128)} fusion(f32[64,128,128]{2,1,0:T(8,128)} %bitcast.33, s32[1024]{0:T(1024)S(1)} %pad_clamp_fusion), kind=kCustom, calls=%fused_computation.1 | custom fusion | bytes 4718736 | tf_op jit(solution)/shard_map/gather | solution.py:100
  84.2 0.7 collective-permute-start.1
  84.8 0.1 copy.23
  85.0 0.1 copy.25
  85.1 0.1 reshape.38
  85.2 2.9 %gather_fusion = f32[36,128,128]{2,1,0:T(8,128)S(1)} fusion(f32[64,128,128]{2,1,0:T(8,128)} %bitcast.34, s32[1024]{0:T(1024)S(1)} %pad_clamp_fusion.1), kind=kCustom, calls=%fused_computation | custom fusion | bytes 4718736 | tf_op jit(solution)/shard_map/gather | solution.py:101
  88.1 1.3 %collective-permute-done.1 = f32[18,1,2,128,128]{4,3,2,0,1:T(8,128)} collective-permute-done((f32[18,1,2,128,128]{4,3,2,0,1:T(8,128)}, f32[18,1,2,128,128]{4,3,2,0,1:T(8,128)}, u32[]{:S(2)}, u32[]{:S(2)}) %collective-permute-start.1) | collective-permute-done | bytes 2359328 | tf_op jit(solution)/shard_map/ppermute | solution.py:13
  89.4 3.0 %fusion.3 = f32[18,64,1,2,128]{4,1,3,0,2:T(8,128)S(1)} fusion(f32[18,1,2,128,128]{4,3,2,0,1:T(8,128)S(1)} %bitcast.32, f32[18,1,2,128,128]{4,3,2,0,1:T(8,128)} %collective-permute-done.1, f32[18,64,2,128]{3,2,1,0:T(2,128)S(1)} %bitcast.36, pred[18,2]{1,0:T(8,128)(4,1)S(1)} %copy.23), kind=kOutput, calls=%fused_computation.5 | convolution fusion | flops 227082240 | bytes 7077924 | tf_op jit(solution)/shard_map/rschk,rchkl->rschl/dot_general | solution.py:102
  92.3 0.9 copy.28
  93.2 1.9 %copy.29 = f32[1152,1,256]{0,2,1:T(8,128)S(1)} copy(f32[1152,1,256]{2,1,0:T(1,128)S(1)} %bitcast.35) | data formatting | bytes 2359296 | tf_op jit(solution)/shard_map/reshape | solution.py:104
  95.2 0.0 reduce-scatter.2.cloned.1.call-done
  95.2 1.4 %select_add_fusion = f32[1152,1,256]{0,2,1:T(8,128)S(1)} fusion(f32[1152,1,256]{0,2,1:T(8,128)S(1)} %copy.29, f32[1152,1,256]{0,2,1:T(8,128)} %reduce-scatter.2.cloned.1.call-done, pred[1152]{0:T(1024)(128)(4,1)S(1)} %add_compare_fusion), kind=kLoop, calls=%fused_computation.7 | loop fusion | flops 589824 | bytes 3540096 | tf_op jit(solution)/shard_map/add | solution.py:105
  96.6 2.1 %copy.30 = f32[1152,1,256]{2,1,0:T(1,128)} copy(f32[1152,1,256]{0,2,1:T(8,128)S(1)} %select_add_fusion) | data formatting | bytes 2359296 | tf_op jit(solution)/shard_map/add | solution.py:105
  (7 shorter events, 0.1 us)
Async XLA Ops:
  7.4 13.5 %copy-start.1 = (s32[18,1,2]{0,2,1:T(2,128)S(1)}, s32[18,1,2]{0,2,1:T(2,128)}, u32[]{:S(2)}) copy-start(s32[18,1,2]{0,2,1:T(2,128)} %param.9) | copy-start | bytes 436
  7.4 18.2 %copy-start = (f32[1152,1,256]{2,1,0:T(1,128)S(1)}, f32[1152,1,256]{2,1,0:T(1,128)}, u32[]{:S(2)}) copy-start(f32[1152,1,256]{2,1,0:T(1,128)} %param.5) | copy-start | bytes 3538948
  7.4 72.5 %all-gather.4.cloned.1.call-start = ((), (), s32[]{:S(2)}) async-start(), calls=%async_computation.2 | async-start | bytes 4718592 | tf_op jit(solution)/shard_map/all_gather | solution.py:73
  20.8 74.5 %reduce-scatter.2.cloned.1.call-start = ((), (), s32[]{:S(2)}) async-start(), calls=%async_computation.1 | async-start | bytes 5898240 | tf_op jit(solution)/shard_map/reduce_scatter | solution.py:94
  20.8 7.7 %collective-permute-start = (s32[18,1,2]{0,2,1:T(2,128)S(1)}, s32[18,1,2]{0,2,1:T(2,128)S(1)}, u32[]{:S(2)}, u32[]{:S(2)}) collective-permute-start(s32[18,1,2]{0,2,1:T(2,128)S(1)} %copy-done.1), channel_id=1, source_target_pairs={{0,4},{4,0},{1,5},{5,1},{2,6},{6,2},{3,7},{7,3},{8,12},{12,8},{9,1... | collective-permute-start | bytes 440 | tf_op jit(solution)/shard_map/ppermute | solution.py:13
  84.2 5.2 %collective-permute-start.1 = (f32[18,1,2,128,128]{4,3,2,0,1:T(8,128)}, f32[18,1,2,128,128]{4,3,2,0,1:T(8,128)}, u32[]{:S(2)}, u32[]{:S(2)}) collective-permute-start(f32[18,1,2,128,128]{4,3,2,0,1:T(8,128)} %bitcast.11), channel_id=1, source_target_pairs={{0,4},{4,0},{1,5},{5,1},{2,6},{6,2},{3,7},{7,3},{8,12},{12,8},{9,1... | collective-permute-start | bytes 7077896 | tf_op jit(solution)/shard_map/ppermute | solution.py:13
Sparse Core Ops, SparseCore 0:
  20.9 58.9 all-gather.3
Sparse Core Ops, SparseCore 1:
  39.7 53.7 reduce-scatter.1

commit v20 on v19

--- a/solution.py
+++ b/solution.py
@@ -97,7 +97,10 @@
         scatter_dimension=0,
         tiled=True,
     )
-    from_sibling = shift(own[sib_slot], "core", 1)
+    cut = sib_slot.shape[0] // 2
+    from_sibling = jnp.concatenate(
+        [shift(own[sib_slot[:cut]], "core", 1), shift(own[sib_slot[cut:]], "core", 1)], axis=0
+    )
     chosen = jnp.where((owner_core == my_core)[..., None, None], own[slot], from_sibling)
     cycle = jnp.einsum(
         "rschk,rchkl->rschl", blocks, chosen, precision=lax.Precision.HIGH

time: 107 us -> 110 us (1.028)
  local copies, waits for them, and re-layouts: 16.6 us -> 20.2 us
    gather x1 -> x2, local copies, waits for them, and re-layouts: 4.33 us -> 7.66 us  [the longest x1 3.84 us: local(): own[sib_slot[:cut]]]
    ppermute x2 -> x3, starting transfers between devices: 4.75 us -> 4.82 us  [shift(): return lax.ppermute(x, axis, [(k, (k + step) % n) for k in range(n)])]
  transfers between devices with their start and end apart: 4 -> 5, of which waited for: 2 -> 2; matrix products, arithmetic and copies ran while one was open for 17% -> 20% of each run, Pallas kernels for 10% -> 10%
where the time goes in v20:
time: 110 us; the launch traced here: 109 us
  waiting for transfers between devices  39.1 us (36%)
  local copies, waits for them, and re-layouts  20.2 us (18%)
  between operations  15.6 us (14%)
  blocking collectives  13.4 us (12%)
  Pallas kernels  11 us (10%)
  starting transfers between devices  4.87 us (4%)
  matrix products  2.86 us (3%)
  other arithmetic  2.51 us (2%)
    all_gather x1, waiting for transfers between devices, local(): own = lax.all_gather(by_y, 'cz', axis=0, tiled=False)  37.8 us
    all_gather x1, blocking collectives, local(): by_y = lax.all_gather(ph_interaction, 'cy', axis=0, tiled=False)  13.4 us
    pallas_call x1, Pallas kernels, ladder_matmul_t(): pl.pallas_call(ladder_kernel, grid=(rows // block,), in_specs=[pl.BlockSp...  11 us
    ppermute x3, starting transfers between devices, shift(): return lax.ppermute(x, axis, [(k, (k + step) % n) for k in range(n)])  4.82 us
    gather x1, local copies, waits for them, and re-layouts, local(): own[sib_slot[:cut]]  3.84 us
    gather x1, local copies, waits for them, and re-layouts, local(): own[sib_slot[cut:]]  3.82 us
    gather x1, local copies, waits for them, and re-layouts, local(): own[slot]  2.97 us
    dot_general x1, matrix products, local(): jnp.einsum('rschk,rchkl->rschl', blocks, chosen, precision=lax.Precision....  2.86 us
  transfers between devices with their start and end apart: 5, of which 2 were waited for; matrix products, arithmetic and copies ran while one was open for 20% of the time, Pallas kernels for 10%

profile of v20, /device:TPU:1, one launch (start us, length us, event | category | flops | bytes accessed | tf_op | source)
XLA Modules:
  0.0 109.5 jit_solution(10053985403378594382)
XLA Ops:
  7.4 13.4 %all-gather = f32[8,128,128]{2,1,0:T(8,128)} all-gather(f32[2,128,128]{2,1,0:T(8,128)} %param.7), channel_id=2, replica_groups=mesh['cy'=4,'cz'=8,'core'=2,'ctr'=4] {'cy'}, dimensions={0}, use_global_device_ids=true | all-gather | bytes 655360 | tf_op jit(solution)/shard_map/all_gather | solution.py:72
  20.7 0.0 all-gather.4.cloned.1.call-update
  20.8 0.0 reduce-scatter.2.cloned.1.call-start
  20.8 4.1 %collective-permute-start = (s32[18,1,2]{0,2,1:T(2,128)S(1)}, s32[18,1,2]{0,2,1:T(2,128)S(1)}, u32[]{:S(2)}, u32[]{:S(2)}) collective-permute-start(s32[18,1,2]{0,2,1:T(2,128)S(1)} %copy-done.1), channel_id=1, source_target_pairs={{0,4},{4,0},{1,5},{5,1},{2,6},{6,2},{3,7},{7,3},{8,12},{12,8},{9,1... | collective-permute-start | bytes 440 | tf_op jit(solution)/shard_map/ppermute | solution.py:13
  25.6 1.9 %copy.24 = f32[1152,1,256]{0,2,1:T(8,128)S(1)} copy(f32[1152,1,256]{2,1,0:T(1,128)S(1)} %copy-done) | data formatting | bytes 2359296 | tf_op args[0]
  27.6 0.9 fusion.15
  28.5 0.0 collective-permute-done
  28.6 11.0 %shard_map.55 = f32[256,4608]{1,0:T(8,128)} custom-call(bf16[256,1152]{1,0:T(8,128)(2,1)} %bitcast.38, bf16[4608,1152]{1,0:T(8,128)(2,1)} %bitcast.31), custom_call_target="tpu_custom_call" | custom-call | flops 2717908992 | bytes 15925248 | tf_op jit(solution)/shard_map/pallas_call | solution.py:48
  39.6 0.0 reduce-scatter.2.cloned.1.call-update
  39.6 0.1 compare_select_fusion.1
  39.7 0.1 copy.28
  39.8 0.1 reshape.56
  39.8 0.1 copy.29
  39.9 0.1 reshape.64
  40.0 1.9 %copy.26 = f32[1152,1,256]{2,1,0:T(1,128)S(1)} copy(f32[1152,1,256]{0,2,1:T(8,128)S(1)} %get-tuple-element.14) | data formatting | bytes 2359296 | tf_op jit(solution)/shard_map/optimization_barrier | solution.py:91
  42.0 37.8 %all-gather.4.cloned.1.call-done = f32[32,2,128,128]{3,2,1,0:T(8,128)} async-done(((f32[4,2,128,128]{3,2,1,0:T(8,128)}), f32[32,2,128,128]{3,2,1,0:T(8,128)}) %all-gather.4.cloned.1.call-update) | async-done | bytes 4194320 | tf_op jit(solution)/shard_map/all_gather | solution.py:73
  79.8 3.8 %gather_fusion.2 = f32[18,128,128]{2,1,0:T(8,128)} fusion(f32[64,128,128]{2,1,0:T(8,128)} %bitcast.33, s32[1024]{0:T(1024)S(1)} %pad_clamp_fusion), kind=kCustom, calls=%fused_computation.2 | custom fusion | bytes 2359368 | tf_op jit(solution)/shard_map/gather | solution.py:102
  83.7 3.8 %gather_fusion.1 = f32[18,128,128]{2,1,0:T(8,128)} fusion(f32[64,128,128]{2,1,0:T(8,128)} %bitcast.34, s32[1024]{0:T(1024)S(1)} %pad_clamp_fusion.1), kind=kCustom, calls=%fused_computation.1 | custom fusion | bytes 2359368 | tf_op jit(solution)/shard_map/gather | solution.py:102
  87.5 0.7 collective-permute-start.1
  88.2 0.0 collective-permute-start.2
  88.2 0.1 copy.25
  88.4 0.1 copy.27
  88.5 0.1 reshape.48
  88.6 3.0 %gather_fusion = f32[36,128,128]{2,1,0:T(8,128)S(1)} fusion(f32[64,128,128]{2,1,0:T(8,128)} %bitcast.35, s32[1024]{0:T(1024)S(1)} %pad_clamp_fusion.2), kind=kCustom, calls=%fused_computation | custom fusion | bytes 4718736 | tf_op jit(solution)/shard_map/gather | solution.py:104
  91.5 0.0 collective-permute-done.1
  91.6 1.2 %collective-permute-done.2 = f32[9,1,2,128,128]{4,3,2,0,1:T(8,128)} collective-permute-done((f32[9,1,2,128,128]{4,3,2,0,1:T(8,128)}, f32[9,1,2,128,128]{4,3,2,0,1:T(8,128)}, u32[]{:S(2)}, u32[]{:S(2)}) %collective-permute-start.2) | collective-permute-done | bytes 1179680 | tf_op jit(solution)/shard_map/ppermute | solution.py:13
  92.7 2.9 %fusion.3 = f32[18,64,1,2,128]{4,1,3,0,2:T(8,128)S(1)} fusion(f32[18,2,128,128]{3,2,1,0:T(8,128)S(1)} %bitcast.32, f32[9,2,128,128]{3,2,1,0:T(8,128)} %bitcast.14, f32[9,2,128,128]{3,2,1,0:T(8,128)} %bitcast.12, f32[18,64,2,128]{3,2,1,0:T(2,128)S(1)} %bitcast.37, pred[18,2]{1,0:T(8,128)(4,1)S(1)} %copy.25), kind=kOutput, calls=%fused_computation.7 | convolution fusion | flops 227672064 | bytes 7077924 | tf_op jit(solution)/shard_map/rschk,rchkl->rschl/dot_general | solution.py:105
  95.6 0.9 copy.31
  96.5 1.9 %copy.32 = f32[1152,1,256]{0,2,1:T(8,128)S(1)} copy(f32[1152,1,256]{2,1,0:T(1,128)S(1)} %bitcast.36) | data formatting | bytes 2359296 | tf_op jit(solution)/shard_map/reshape | solution.py:107
  98.5 0.0 reduce-scatter.2.cloned.1.call-done
  98.5 1.4 %select_add_fusion = f32[1152,1,256]{0,2,1:T(8,128)S(1)} fusion(f32[1152,1,256]{0,2,1:T(8,128)S(1)} %copy.32, f32[1152,1,256]{0,2,1:T(8,128)} %reduce-scatter.2.cloned.1.call-done, pred[1152]{0:T(1024)(128)(4,1)S(1)} %add_compare_fusion), kind=kLoop, calls=%fused_computation.9 | loop fusion | flops 589824 | bytes 3540096 | tf_op jit(solution)/shard_map/add | solution.py:108
  99.9 2.1 %copy.33 = f32[1152,1,256]{2,1,0:T(1,128)} copy(f32[1152,1,256]{0,2,1:T(8,128)S(1)} %select_add_fusion) | data formatting | bytes 2359296 | tf_op jit(solution)/shard_map/add | solution.py:108
  (13 shorter events, 0.1 us)
Async XLA Ops:
  7.4 13.4 %copy-start.1 = (s32[18,1,2]{0,2,1:T(2,128)S(1)}, s32[18,1,2]{0,2,1:T(2,128)}, u32[]{:S(2)}) copy-start(s32[18,1,2]{0,2,1:T(2,128)} %param.9) | copy-start | bytes 436
  7.4 18.2 %copy-start = (f32[1152,1,256]{2,1,0:T(1,128)S(1)}, f32[1152,1,256]{2,1,0:T(1,128)}, u32[]{:S(2)}) copy-start(f32[1152,1,256]{2,1,0:T(1,128)} %param.5) | copy-start | bytes 3538948
  7.4 72.5 %all-gather.4.cloned.1.call-start = ((), (), s32[]{:S(2)}) async-start(), calls=%async_computation.2 | async-start | bytes 4718592 | tf_op jit(solution)/shard_map/all_gather | solution.py:73
  20.8 77.8 %reduce-scatter.2.cloned.1.call-start = ((), (), s32[]{:S(2)}) async-start(), calls=%async_computation.1 | async-start | bytes 5898240 | tf_op jit(solution)/shard_map/reduce_scatter | solution.py:94
  20.8 7.7 %collective-permute-start = (s32[18,1,2]{0,2,1:T(2,128)S(1)}, s32[18,1,2]{0,2,1:T(2,128)S(1)}, u32[]{:S(2)}, u32[]{:S(2)}) collective-permute-start(s32[18,1,2]{0,2,1:T(2,128)S(1)} %copy-done.1), channel_id=1, source_target_pairs={{0,4},{4,0},{1,5},{5,1},{2,6},{6,2},{3,7},{7,3},{8,12},{12,8},{9,1... | collective-permute-start | bytes 440 | tf_op jit(solution)/shard_map/ppermute | solution.py:13
  87.5 4.0 %collective-permute-start.1 = (f32[9,1,2,128,128]{4,3,2,0,1:T(8,128)}, f32[9,1,2,128,128]{4,3,2,0,1:T(8,128)}, u32[]{:S(2)}, u32[]{:S(2)}) collective-permute-start(f32[9,1,2,128,128]{4,3,2,0,1:T(8,128)} %bitcast.11), channel_id=1, source_target_pairs={{0,4},{4,0},{1,5},{5,1},{2,6},{6,2},{3,7},{7,3},{8,12},{12,8},{9,1... | collective-permute-start | bytes 3538952 | tf_op jit(solution)/shard_map/ppermute | solution.py:13
  88.2 4.5 %collective-permute-start.2 = (f32[9,1,2,128,128]{4,3,2,0,1:T(8,128)}, f32[9,1,2,128,128]{4,3,2,0,1:T(8,128)}, u32[]{:S(2)}, u32[]{:S(2)}) collective-permute-start(f32[9,1,2,128,128]{4,3,2,0,1:T(8,128)} %bitcast.13), channel_id=1, source_target_pairs={{0,4},{4,0},{1,5},{5,1},{2,6},{6,2},{3,7},{7,3},{8,12},{12,8},{9,1... | collective-permute-start | bytes 3538952 | tf_op jit(solution)/shard_map/ppermute | solution.py:13
Sparse Core Ops, SparseCore 0:
  20.9 58.9 all-gather.3
Sparse Core Ops, SparseCore 1:
  39.7 53.7 reduce-scatter.1
